TPU v7x, 768 devices: a whole 4x8x12 slice. The times are simulated.
768 devices in a mesh: space: 24 (over x, z_hi, core), energy: 32 (over z_lo, y).
Axes of the slice: x: 4, y: 8, z: 12 (z_hi: 3, z_lo: 4; z = z_hi * 4 + z_lo), core: 2. Of those that a mesh axis runs over, the one named last changes fastest.
Arguments:
- green_lower: bfloat16 [24, 128, 2, 128, 128], P('space', 'energy'), may hold values from -0.5 to 0.5
- green_diag: bfloat16 [24, 128, 2, 128, 128], P('space', 'energy'), may hold values from -0.5 to 0.5
- green_upper: bfloat16 [24, 128, 2, 128, 128], P('space', 'energy'), may hold values from -0.5 to 0.5
- self_energy: bfloat16 [2, 24, 128, 2, 128, 128], P(None, 'space', 'energy'), may hold values from -1.75 to 1.75
- coulomb: bfloat16 [24, 128, 128], P('space'), may hold values from -0.5 to 0.5
Outputs:
- screened_polarization: bfloat16 [2, 24, 128, 2, 128, 128], P(None, 'space', 'energy')
All inputs are finite; a program needn't handle non-finite values.
Results may differ from a plain program's by a relative error of at most 0.017.
Values may be sent and summed in bfloat16 or wider, within the bound.
No kernel may reach another device: no remote copies, remote signals or barrier semaphores. Data moves between devices by JAX's collectives and lax.ppermute only.
A program may use at most 64 MiB of HBM per device.

v0:
```python
import math

import jax
import jax.numpy as jnp
from jax import lax
from jax.sharding import PartitionSpec as P


def padded_2(shard, sides, width):
    for axis, dim in sides:
        peers, length = (lax.axis_size(axis), shard.shape[dim])
        up = [(i, (i + 1) % peers) for i in range(peers - 1)]
        down = [(j, i) for i, j in up]
        last = lax.slice_in_dim(shard, length - width, length, axis=dim)
        initial = lax.slice_in_dim(shard, 0, width, axis=dim)
        before = lax.ppermute(last, axis, up)
        after = lax.ppermute(initial, axis, down)
        shard = jnp.concatenate([before, shard, after], axis=dim)
    return shard


def in_blocks(shard, dim, peers):
    before, after = (shard.shape[:dim], shard.shape[dim + 1 :])
    return jnp.moveaxis(shard.reshape(*before, peers, -1, *after), dim, 0)


def edges_of(length, count):
    unit = 8 if length >= 8 * count else 1
    return [length // unit * k // count * unit for k in range(1, count)]


def joined_along(tiles, dim):
    tiles = jnp.moveaxis(tiles, 0, dim)
    shape = tiles.shape
    return tiles.reshape(*shape[:dim], shape[dim] * shape[dim + 1], *shape[dim + 2 :])


def cut_exchange(shard, axis, pieces, split_dim, concat_dim):
    tiles = in_blocks(shard, split_dim, lax.axis_size(axis))
    split_at = max(range(1, max(2, tiles.ndim - 1)), key=lambda d: tiles.shape[d])
    gathered = []
    for slab in jnp.split(tiles, edges_of(tiles.shape[split_at], pieces), axis=split_at):
        if slab.size:
            gathered.append(lax.all_to_all(slab, axis, split_axis=0, concat_axis=0, tiled=True))
    return joined_along(jnp.concatenate(gathered, axis=split_at), concat_dim)


def congruence(green, sigma):
    green_real = green[:, :, 0]
    green_imag = green[:, :, 1]
    sigma_real = sigma[:, :, :, 0]
    sigma_imag = sigma[:, :, :, 1]
    green_wide = jnp.concatenate([green_real, green_imag], axis=-1)
    sigma_tall = jnp.concatenate(
        [
            jnp.concatenate([sigma_real, sigma_imag], axis=-1),
            jnp.concatenate([-sigma_imag, sigma_real], axis=-1),
        ],
        axis=-2,
    )
    mixed = jnp.einsum(
        "nepq,fneqr->fnepr", green_wide, sigma_tall, preferred_element_type=jnp.float32
    ).astype(jnp.bfloat16)
    adjoint_tall = jnp.concatenate(
        [green_wide, jnp.concatenate([-green_imag, green_real], axis=-1)], axis=-2
    )
    return jnp.einsum("fnepr,nesr->fneps", mixed, adjoint_tall, preferred_element_type=jnp.float32)


def split_table(table):
    high_part = table.astype(jnp.bfloat16)
    low_part = (table - high_part.astype(jnp.float32)).astype(jnp.bfloat16)
    return (high_part, low_part)


def spectrum(values, table_high, table_low, padded_len):

    def apply_table(part):
        return jnp.dot(table_high, part, preferred_element_type=jnp.float32) + jnp.dot(
            table_low, part, preferred_element_type=jnp.float32
        )

    real_terms = apply_table(values[:, 0])
    imag_terms = apply_table(values[:, 1])
    out_real = real_terms[:padded_len] + imag_terms[padded_len:]
    out_imag = imag_terms[:padded_len] - real_terms[padded_len:]
    return (out_real, out_imag)


def body(green_lower, green_diag, green_upper, self_energy, coulomb):
    block_count = green_diag.shape[0]
    energy_local = green_diag.shape[1]
    block_order = green_diag.shape[-1]
    energies = energy_local * lax.axis_size("energy")
    padded_len = 2 * energies
    padded = padded_2(self_energy, (("space", 1),), 1)
    lower_term = congruence(green_lower, padded[:, :block_count])
    diag_term = congruence(green_diag, padded[:, 1 : block_count + 1])
    upper_term = congruence(green_upper, padded[:, 2:])
    total = lower_term + diag_term + upper_term
    total = total.reshape(2, block_count, energy_local, block_order, 2, block_order)
    green_function = (
        jnp.transpose(total, (0, 2, 4, 1, 3, 5))
        .astype(jnp.bfloat16)
        .reshape(2, energy_local, 2, -1)
    )
    frequency = lax.iota(jnp.int32, padded_len)
    energy_index = lax.iota(jnp.int32, energies)
    step_angle = 2.0 * math.pi / padded_len
    forward_angle = (frequency[:, None] * energy_index[None, :] % padded_len).astype(
        jnp.float32
    ) * step_angle
    forward_table = jnp.concatenate([jnp.cos(forward_angle), jnp.sin(forward_angle)], axis=0)
    table_high, table_low = split_table(forward_table)
    entries = cut_exchange(green_function, "energy", 2, 3, 1)
    lesser_values = entries[0]
    greater_values = entries[1]
    lesser_real, lesser_imag = spectrum(lesser_values, table_high, table_low, padded_len)
    greater_real, greater_imag = spectrum(greater_values, table_high, table_low, padded_len)
    product_real = lesser_real * greater_real + lesser_imag * greater_imag
    product_imag = lesser_imag * greater_real - lesser_real * greater_imag
    row_index = jnp.concatenate([energy_index, (padded_len - energy_index) % padded_len])
    back_angle = (row_index[:, None] * frequency[None, :] % padded_len).astype(
        jnp.float32
    ) * step_angle
    back_cos = jnp.cos(back_angle)
    back_sin = jnp.sin(back_angle)
    back_table = jnp.concatenate(
        [
            jnp.concatenate([back_cos, -back_sin], axis=1),
            jnp.concatenate([back_sin, back_cos], axis=1),
        ],
        axis=0,
    )
    stacked_product = jnp.concatenate([product_real, product_imag], axis=0)
    factor = 1.0 / (padded_len * math.sqrt(energies))
    combined = (
        jnp.dot(
            back_table,
            stacked_product,
            precision=lax.Precision.HIGH,
            preferred_element_type=jnp.float32,
        )
        * factor
    )
    corr_real = combined[:padded_len]
    corr_imag = combined[padded_len:]
    lesser_lags = jnp.stack([corr_real[:energies], corr_imag[:energies]], axis=1)
    greater_lags = jnp.stack([corr_real[energies:], -corr_imag[energies:]], axis=1)
    polar = jnp.stack([lesser_lags, greater_lags], axis=0).astype(jnp.bfloat16)
    returned = lax.all_to_all(polar, "energy", split_axis=1, concat_axis=3, tiled=True)
    returned = returned.reshape(2, energy_local, 2, block_count, block_order, block_order)
    left_product = jnp.einsum(
        "npq,fetnqr->fetnpr", coulomb, returned, preferred_element_type=jnp.float32
    ).astype(jnp.bfloat16)
    screened = jnp.einsum(
        "fetnpr,nsr->fnetps", left_product, coulomb, preferred_element_type=jnp.float32
    )
    return screened.astype(jnp.bfloat16)


def solution(mesh):
    in_specs = (
        P("space", "energy", None, None, None),
        P("space", "energy", None, None, None),
        P("space", "energy", None, None, None),
        P(None, "space", "energy", None, None, None),
        P("space", None, None),
    )
    out_specs = P(None, "space", "energy", None, None, None)
    return jax.shard_map(body, mesh=mesh, in_specs=in_specs, out_specs=out_specs, check_vma=False)
```

profile of v0, /device:TPU:270, one launch (start us, length us, event | category | flops | bytes accessed | tf_op | source)
XLA Modules:
  0.0 113.0 jit_solution(439462115900175373)
XLA Ops:
  0.0 0.0 copy-start
  0.0 0.0 copy-start.1
  0.0 1.4 %copy.43 = bf16[2,1,4,2,128,128]{4,5,0,2,3,1:T(8,128)(2,1)S(1)} copy(bf16[2,1,4,2,128,128]{5,4,3,2,1,0:T(8,128)(2,1)} %param.8) | data formatting | bytes 1048576 | tf_op args[3]
  1.4 0.0 copy-start.3
  1.4 2.1 %collective-permute-start = (bf16[2,1,4,2,128,128]{4,5,0,2,3,1:T(8,128)(2,1)S(1)}, bf16[2,1,4,2,128,128]{4,5,0,2,3,1:T(8,128)(2,1)S(1)}, u32[]{:S(2)}, u32[]{:S(2)}) collective-permute-start(bf16[2,1,4,2,128,128]{4,5,0,2,3,1:T(8,128)(2,1)S(1)} %copy.43), channel_id=1, source_target_pairs={{0,32},{32,64},{64,96},{96,128},{128,160},{160,192},{192,224},{224... | collective-permute-start | bytes 1572872 | tf_op jit(solution)/shard_map/ppermute | solution.py:16
  3.5 7.5 %collective-permute-start.1 = (bf16[2,1,4,2,128,128]{4,5,0,2,3,1:T(8,128)(2,1)S(1)}, bf16[2,1,4,2,128,128]{4,5,0,2,3,1:T(8,128)(2,1)S(1)}, u32[]{:S(2)}, u32[]{:S(2)}) collective-permute-start(bf16[2,1,4,2,128,128]{4,5,0,2,3,1:T(8,128)(2,1)S(1)} %copy.43), channel_id=1, source_target_pairs={{32,0},{64,32},{96,64},{128,96},{160,128},{192,160},{224,192},{256... | collective-permute-start | bytes 1572872 | tf_op jit(solution)/shard_map/ppermute | solution.py:17
  11.0 0.0 copy-done.1
  11.0 0.7 slice_bitcast_fusion.13
  11.8 0.0 copy-done.2
  11.8 0.7 slice_bitcast_fusion.11
  12.5 0.0 copy-done.3
  12.6 3.6 %collective-permute-done = bf16[2,1,4,2,128,128]{4,5,0,2,3,1:T(8,128)(2,1)S(1)} collective-permute-done((bf16[2,1,4,2,128,128]{4,5,0,2,3,1:T(8,128)(2,1)S(1)}, bf16[2,1,4,2,128,128]{4,5,0,2,3,1:T(8,128)(2,1)S(1)}, u32[]{:S(2)}, u32[]{:S(2)}) %collective-permute-start) | collective-permute-done | bytes 524320 | tf_op jit(solution)/shard_map/ppermute | solution.py:16
  16.3 2.8 %fusion.4 = f32[4,256,2,128]{3,1,2,0:T(8,128)} fusion(bf16[2,1,4,128,128]{3,4,0,2,1:T(8,128)(2,1)S(1)} %get-tuple-element.19, bf16[2,1,4,128,128]{3,4,0,2,1:T(8,128)(2,1)S(1)} %fusion.136, bf16[2,1,4,128,128]{3,4,0,2,1:T(8,128)(2,1)S(1)} %get-tuple-element.18, bf16[1,4,128,128]{3,2,1,0:T(8,128)(2,1)} %get-tuple-element.29, ...), kind=kOutput, calls=%fused_computation.16 | convolution fusion | flops 275513344 | bytes 2228224 | tf_op jit(solution)/shard_map/fnepr,nesr->fneps/dot_general | solution.py:67
  19.1 3.1 %convolution_add_fusion.5 = f32[4,256,2,128]{3,1,2,0:T(8,128)} fusion(f32[4,256,2,128]{3,1,2,0:T(8,128)} %fusion.4, bf16[2,1,4,128,128]{3,4,0,2,1:T(8,128)(2,1)S(1)} %get-tuple-element.17, bf16[2,1,4,128,128]{3,4,0,2,1:T(8,128)(2,1)S(1)} %fusion.137, bf16[2,1,4,128,128]{3,4,0,2,1:T(8,128)(2,1)S(1)} %get-tuple-element.16, ...), kind=kOutput, calls=%fused_computation.6 | convolution fusion | flops 275775488 | bytes 3276800 | tf_op jit(solution)/shard_map/fnepr,nesr->fneps/dot_general | solution.py:67
  22.2 6.1 %collective-permute-done.1 = bf16[2,1,4,2,128,128]{4,5,0,2,3,1:T(8,128)(2,1)S(1)} collective-permute-done((bf16[2,1,4,2,128,128]{4,5,0,2,3,1:T(8,128)(2,1)S(1)}, bf16[2,1,4,2,128,128]{4,5,0,2,3,1:T(8,128)(2,1)S(1)}, u32[]{:S(2)}, u32[]{:S(2)}) %collective-permute-start.1) | collective-permute-done | bytes 524320 | tf_op jit(solution)/shard_map/ppermute | solution.py:17
  28.4 0.0 copy-done.4
  28.4 0.6 fusion
  29.1 0.3 copy.54
  29.4 0.3 reshape_reshape.3
  29.7 1.0 copy.55
  30.7 22.1 %all-to-all-start = ((bf16[32,2,2,2,512]{4,3,2,1,0:T(2,128)(2,1)}), bf16[32,2,2,2,512]{4,3,2,1,0:T(2,128)(2,1)S(1)}, u32[]{:S(2)}, u32[]{:S(2)}) async-start(bf16[32,2,2,2,512]{4,3,2,1,0:T(2,128)(2,1)} %copy.55), calls=%async_computation | async-start | bytes 524288 | tf_op jit(solution)/shard_map/all_to_all | solution.py:44
  52.8 1.0 copy.56
  53.8 11.1 %all-to-all-done = bf16[32,2,2,2,512]{4,3,2,1,0:T(2,128)(2,1)S(1)} async-done(((bf16[32,2,2,2,512]{4,3,2,1,0:T(2,128)(2,1)}), bf16[32,2,2,2,512]{4,3,2,1,0:T(2,128)(2,1)S(1)}, u32[]{:S(2)}, u32[]{:S(2)}) %all-to-all-start) | async-done | bytes 262176 | tf_op jit(solution)/shard_map/all_to_all | solution.py:44
  64.9 5.8 %all-to-all-start.1 = ((bf16[32,2,2,2,512]{4,3,2,1,0:T(2,128)(2,1)}), bf16[32,2,2,2,512]{4,3,2,1,0:T(2,128)(2,1)S(1)}, u32[]{:S(2)}, u32[]{:S(2)}) async-start(bf16[32,2,2,2,512]{4,3,2,1,0:T(2,128)(2,1)} %copy.56), calls=%async_computation.1 | async-start | bytes 524288 | tf_op jit(solution)/shard_map/all_to_all | solution.py:44
  70.8 0.5 fusion.113
  71.3 1.1 fusion.112
  72.5 10.4 %all-to-all-done.1 = bf16[32,2,2,2,512]{4,3,2,1,0:T(2,128)(2,1)S(1)} async-done(((bf16[32,2,2,2,512]{4,3,2,1,0:T(2,128)(2,1)}), bf16[32,2,2,2,512]{4,3,2,1,0:T(2,128)(2,1)S(1)}, u32[]{:S(2)}, u32[]{:S(2)}) %all-to-all-start.1) | async-done | bytes 262176 | tf_op jit(solution)/shard_map/all_to_all | solution.py:44
  82.9 0.7 maximum_bitcast_fusion.15
  83.5 0.4 fusion.143
  83.9 0.4 fusion.145
  84.3 0.3 fusion.99
  84.6 0.3 fusion.96
  84.9 0.3 convolution_add_fusion.1
  85.1 0.3 convolution_add_fusion
  85.4 0.4 fusion.146
  85.8 0.3 fusion.105
  86.1 0.3 convolution_add_fusion.3
  86.4 0.3 fusion.102
  86.7 0.3 convolution_add_fusion.2
  86.9 0.5 multiply_add_fusion
  87.5 1.0 fusion.147
  88.6 0.1 pad_maximum_fusion
  88.7 0.5 copy.57
  89.2 21.7 %all_to_all.25 = bf16[2,128,2,512]{3,2,0,1:T(2,128)(2,1)S(1)} all-to-all(bf16[2,128,2,512]{3,2,0,1:T(2,128)(2,1)S(1)} %copy.57), channel_id=1, replica_groups=mesh['space'=24,'energy'=32] {'energy'}, dimensions={1} | all-to-all | bytes 1048576 | tf_op jit(solution)/shard_map/all_to_all | solution.py:151
  111.0 0.3 copy.117
  111.3 0.3 reshape.157
  111.6 0.0 copy-done
  111.6 1.4 %fusion.2 = bf16[2,1,4,2,128,128]{5,4,3,2,1,0:T(8,128)(2,1)} fusion(bf16[2,4,2,128,128]{4,3,2,1,0:T(8,128)(2,1)S(1)} %reshape.157, bf16[1,128,128]{2,1,0:T(8,128)(2,1)S(1)} %copy-done), kind=kOutput, calls=%fused_computation.14 | convolution fusion | flops 134742016 | bytes 1081344 | tf_op jit(solution)/shard_map/fetnpr,nsr->fnetps/dot_general | solution.py:156
  (21 shorter events, 0.5 us)
Async XLA Ops:
  0.0 111.6 %copy-start = (bf16[1,128,128]{2,1,0:T(8,128)(2,1)S(1)}, bf16[1,128,128]{2,1,0:T(8,128)(2,1)}, u32[]{:S(2)}) copy-start(bf16[1,128,128]{2,1,0:T(8,128)(2,1)} %param.9) | copy-start | bytes 98308
  0.0 11.0 %copy-start.1 = (bf16[1,4,2,128,128]{4,3,2,1,0:T(8,128)(2,1)S(1)}, bf16[1,4,2,128,128]{4,3,2,1,0:T(8,128)(2,1)}, u32[]{:S(2)}) copy-start(bf16[1,4,2,128,128]{4,3,2,1,0:T(8,128)(2,1)} %param.5) | copy-start | bytes 786436
  0.0 11.8 %copy-start.2 = (bf16[1,4,2,128,128]{4,3,2,1,0:T(8,128)(2,1)S(1)}, bf16[1,4,2,128,128]{4,3,2,1,0:T(8,128)(2,1)}, u32[]{:S(2)}) copy-start(bf16[1,4,2,128,128]{4,3,2,1,0:T(8,128)(2,1)} %param.6) | copy-start | bytes 786436
  1.4 11.1 %copy-start.3 = (bf16[1,4,2,128,128]{4,3,2,1,0:T(8,128)(2,1)S(1)}, bf16[1,4,2,128,128]{4,3,2,1,0:T(8,128)(2,1)}, u32[]{:S(2)}) copy-start(bf16[1,4,2,128,128]{4,3,2,1,0:T(8,128)(2,1)} %param.7) | copy-start | bytes 786436
  1.4 14.8 %collective-permute-start = (bf16[2,1,4,2,128,128]{4,5,0,2,3,1:T(8,128)(2,1)S(1)}, bf16[2,1,4,2,128,128]{4,5,0,2,3,1:T(8,128)(2,1)S(1)}, u32[]{:S(2)}, u32[]{:S(2)}) collective-permute-start(bf16[2,1,4,2,128,128]{4,5,0,2,3,1:T(8,128)(2,1)S(1)} %copy.43), channel_id=1, source_target_pairs={{0,32},{32,64},{64,96},{96,128},{128,160},{160,192},{192,224},{224... | collective-permute-start | bytes 1572872 | tf_op jit(solution)/shard_map/ppermute | solution.py:16
  3.5 24.9 %collective-permute-start.1 = (bf16[2,1,4,2,128,128]{4,5,0,2,3,1:T(8,128)(2,1)S(1)}, bf16[2,1,4,2,128,128]{4,5,0,2,3,1:T(8,128)(2,1)S(1)}, u32[]{:S(2)}, u32[]{:S(2)}) collective-permute-start(bf16[2,1,4,2,128,128]{4,5,0,2,3,1:T(8,128)(2,1)S(1)} %copy.43), channel_id=1, source_target_pairs={{32,0},{64,32},{96,64},{128,96},{160,128},{192,160},{224,192},{256... | collective-permute-start | bytes 1572872 | tf_op jit(solution)/shard_map/ppermute | solution.py:17
  22.2 6.2 %copy-start.4 = (f32[4,256,2,128]{3,1,2,0:T(8,128)S(1)}, f32[4,256,2,128]{3,1,2,0:T(8,128)}, u32[]{:S(2)}) copy-start(f32[4,256,2,128]{3,1,2,0:T(8,128)} %convolution_add_fusion.5) | copy-start | bytes 3145732
  30.7 34.2 %all-to-all-start = ((bf16[32,2,2,2,512]{4,3,2,1,0:T(2,128)(2,1)}), bf16[32,2,2,2,512]{4,3,2,1,0:T(2,128)(2,1)S(1)}, u32[]{:S(2)}, u32[]{:S(2)}) async-start(bf16[32,2,2,2,512]{4,3,2,1,0:T(2,128)(2,1)} %copy.55), calls=%async_computation | async-start | bytes 524288 | tf_op jit(solution)/shard_map/all_to_all | solution.py:44
  64.9 17.9 %all-to-all-start.1 = ((bf16[32,2,2,2,512]{4,3,2,1,0:T(2,128)(2,1)}), bf16[32,2,2,2,512]{4,3,2,1,0:T(2,128)(2,1)S(1)}, u32[]{:S(2)}, u32[]{:S(2)}) async-start(bf16[32,2,2,2,512]{4,3,2,1,0:T(2,128)(2,1)} %copy.56), calls=%async_computation.1 | async-start | bytes 524288 | tf_op jit(solution)/shard_map/all_to_all | solution.py:44
where the time goes:
time: 113 us
  starting transfers between devices  37.5 us (33%)
  waiting for transfers between devices  31.3 us (28%)
  blocking collectives  21.7 us (19%)
  matrix products  11.2 us (10%)
  local copies, waits for them, and re-layouts  7.77 us (7%)
  other arithmetic  3.16 us (3%)
    all_to_all x2, starting transfers between devices, cut_exchange(): lax.all_to_all(slab, axis, split_axis=0, concat_axis=0, tiled=True)  27.9 us
    all_to_all x1, blocking collectives, body(): lax.all_to_all(polar, 'energy', split_axis=1, concat_axis=3, tiled=True)  21.7 us
    all_to_all x2, waiting for transfers between devices, cut_exchange(): lax.all_to_all(slab, axis, split_axis=0, concat_axis=0, tiled=True)  21.6 us
    ppermute x1, starting transfers between devices, padded_2(): after = lax.ppermute(initial, axis, down)  7.55 us
    dot_general x3, matrix products, congruence(): jnp.einsum('fnepr,nesr->fneps', mixed, adjoint_tall, preferred_element_ty...  6.52 us
    ppermute x1, waiting for transfers between devices, padded_2(): after = lax.ppermute(initial, axis, down)  6.12 us
    ppermute x1, waiting for transfers between devices, padded_2(): before = lax.ppermute(last, axis, up)  3.61 us
  transfers between devices with their start and end apart: 4, of which 4 were waited for; matrix products, arithmetic and copies ran while one was open for 9% of the time, Pallas kernels for 0%

commit v1 on v0

--- a/solution.py
+++ b/solution.py
@@ -112,7 +112,7 @@
     ) * step_angle
     forward_table = jnp.concatenate([jnp.cos(forward_angle), jnp.sin(forward_angle)], axis=0)
     table_high, table_low = split_table(forward_table)
-    entries = cut_exchange(green_function, "energy", 2, 3, 1)
+    entries = cut_exchange(green_function, "energy", 1, 3, 1)
     lesser_values = entries[0]
     greater_values = entries[1]
     lesser_real, lesser_imag = spectrum(lesser_values, table_high, table_low, padded_len)

time: 113 us -> 105 us (0.929)
  the two profiles are of different devices: /device:TPU:270 before, /device:TPU:14 now
where the time goes in v1:
time: 105 us
  starting transfers between devices  37.7 us (36%)
  waiting for transfers between devices  24 us (23%)
  blocking collectives  22.1 us (21%)
  matrix products  11.2 us (11%)
  local copies, waits for them, and re-layouts  7.14 us (7%)
  other arithmetic  2.48 us (2%)
    all_to_all x1, blocking collectives, body(): lax.all_to_all(polar, 'energy', split_axis=1, concat_axis=3, tiled=True)  22.1 us
    all_to_all x1, starting transfers between devices, cut_exchange(): lax.all_to_all(slab, axis, split_axis=0, concat_axis=0, tiled=True)  21.4 us
    ppermute x1, starting transfers between devices, padded_2(): after = lax.ppermute(initial, axis, down)  14.3 us
    all_to_all x1, waiting for transfers between devices, cut_exchange(): lax.all_to_all(slab, axis, split_axis=0, concat_axis=0, tiled=True)  13.7 us
    ppermute x1, waiting for transfers between devices, padded_2(): after = lax.ppermute(initial, axis, down)  6.68 us
    dot_general x3, matrix products, congruence(): jnp.einsum('fnepr,nesr->fneps', mixed, adjoint_tall, preferred_element_ty...  6.53 us
    ppermute x1, waiting for transfers between devices, padded_2(): before = lax.ppermute(last, axis, up)  3.6 us
  transfers between devices with their start and end apart: 3, of which 3 were waited for; matrix products, arithmetic and copies ran while one was open for 9% of the time, Pallas kernels for 0%

profile of v1, /device:TPU:14, one launch (start us, length us, event | category | flops | bytes accessed | tf_op | source)
XLA Modules:
  0.0 104.9 jit_solution(1389754086480269411)
XLA Ops:
  0.0 0.0 copy-start
  0.0 0.0 copy-start.1
  0.0 0.0 copy-start.2
  0.0 1.4 %copy.43 = bf16[2,1,4,2,128,128]{4,5,0,2,3,1:T(8,128)(2,1)S(1)} copy(bf16[2,1,4,2,128,128]{5,4,3,2,1,0:T(8,128)(2,1)} %param.8) | data formatting | bytes 1048576 | tf_op args[3]
  1.4 0.0 copy-start.3
  1.4 2.1 %collective-permute-start = (bf16[2,1,4,2,128,128]{4,5,0,2,3,1:T(8,128)(2,1)S(1)}, bf16[2,1,4,2,128,128]{4,5,0,2,3,1:T(8,128)(2,1)S(1)}, u32[]{:S(2)}, u32[]{:S(2)}) collective-permute-start(bf16[2,1,4,2,128,128]{4,5,0,2,3,1:T(8,128)(2,1)S(1)} %copy.43), channel_id=1, source_target_pairs={{0,32},{32,64},{64,96},{96,128},{128,160},{160,192},{192,224},{224... | collective-permute-start | bytes 1572872 | tf_op jit(solution)/shard_map/ppermute | solution.py:16
  3.5 14.3 %collective-permute-start.1 = (bf16[2,1,4,2,128,128]{4,5,0,2,3,1:T(8,128)(2,1)S(1)}, bf16[2,1,4,2,128,128]{4,5,0,2,3,1:T(8,128)(2,1)S(1)}, u32[]{:S(2)}, u32[]{:S(2)}) collective-permute-start(bf16[2,1,4,2,128,128]{4,5,0,2,3,1:T(8,128)(2,1)S(1)} %copy.43), channel_id=1, source_target_pairs={{32,0},{64,32},{96,64},{128,96},{160,128},{192,160},{224,192},{256... | collective-permute-start | bytes 1572872 | tf_op jit(solution)/shard_map/ppermute | solution.py:17
  17.7 0.0 copy-done.1
  17.7 0.7 slice_bitcast_fusion.13
  18.5 0.0 copy-done.2
  18.5 0.7 slice_bitcast_fusion.11
  19.2 0.0 copy-done.3
  19.3 3.6 %collective-permute-done = bf16[2,1,4,2,128,128]{4,5,0,2,3,1:T(8,128)(2,1)S(1)} collective-permute-done((bf16[2,1,4,2,128,128]{4,5,0,2,3,1:T(8,128)(2,1)S(1)}, bf16[2,1,4,2,128,128]{4,5,0,2,3,1:T(8,128)(2,1)S(1)}, u32[]{:S(2)}, u32[]{:S(2)}) %collective-permute-start) | collective-permute-done | bytes 524320 | tf_op jit(solution)/shard_map/ppermute | solution.py:16
  23.0 2.8 %fusion.4 = f32[4,256,2,128]{3,1,2,0:T(8,128)} fusion(bf16[2,1,4,128,128]{3,4,0,2,1:T(8,128)(2,1)S(1)} %get-tuple-element.17, bf16[2,1,4,128,128]{3,4,0,2,1:T(8,128)(2,1)S(1)} %fusion.136, bf16[2,1,4,128,128]{3,4,0,2,1:T(8,128)(2,1)S(1)} %get-tuple-element.16, bf16[1,4,128,128]{3,2,1,0:T(8,128)(2,1)} %get-tuple-element.27, ...), kind=kOutput, calls=%fused_computation.16 | convolution fusion | flops 275513344 | bytes 2228224 | tf_op jit(solution)/shard_map/fnepr,nesr->fneps/dot_general | solution.py:67
  25.8 3.1 %convolution_add_fusion.5 = f32[4,256,2,128]{3,1,2,0:T(8,128)} fusion(f32[4,256,2,128]{3,1,2,0:T(8,128)} %fusion.4, bf16[2,1,4,128,128]{3,4,0,2,1:T(8,128)(2,1)S(1)} %get-tuple-element.15, bf16[2,1,4,128,128]{3,4,0,2,1:T(8,128)(2,1)S(1)} %fusion.137, bf16[2,1,4,128,128]{3,4,0,2,1:T(8,128)(2,1)S(1)} %get-tuple-element.14, ...), kind=kOutput, calls=%fused_computation.6 | convolution fusion | flops 275775488 | bytes 3276800 | tf_op jit(solution)/shard_map/fnepr,nesr->fneps/dot_general | solution.py:67
  28.9 0.0 copy-start.4
  28.9 6.7 %collective-permute-done.1 = bf16[2,1,4,2,128,128]{4,5,0,2,3,1:T(8,128)(2,1)S(1)} collective-permute-done((bf16[2,1,4,2,128,128]{4,5,0,2,3,1:T(8,128)(2,1)S(1)}, bf16[2,1,4,2,128,128]{4,5,0,2,3,1:T(8,128)(2,1)S(1)}, u32[]{:S(2)}, u32[]{:S(2)}) %collective-permute-start.1) | collective-permute-done | bytes 524320 | tf_op jit(solution)/shard_map/ppermute | solution.py:17
  35.7 0.0 copy-done.4
  35.7 0.6 fusion
  36.4 0.3 copy.54
  36.6 0.3 reshape_reshape.3
  37.0 1.3 %copy.55 = bf16[32,2,4,2,512]{4,3,2,1,0:T(2,128)(2,1)} copy(bf16[32,2,4,2,512]{4,0,3,2,1:T(8,128)(2,1)S(1)} %bitcast.210) | data formatting | bytes 1048576 | tf_op jit(solution)/shard_map/transpose | solution.py:24
  38.3 21.4 %all-to-all-start = ((bf16[32,2,4,2,512]{4,3,2,1,0:T(2,128)(2,1)}), bf16[32,2,4,2,512]{4,3,2,1,0:T(2,128)(2,1)S(1)}, u32[]{:S(2)}, u32[]{:S(2)}) async-start(bf16[32,2,4,2,512]{4,3,2,1,0:T(2,128)(2,1)} %copy.55), calls=%async_computation | async-start | bytes 1048576 | tf_op jit(solution)/shard_map/all_to_all | solution.py:44
  59.7 0.5 fusion.113
  60.3 1.1 %fusion.112 = (f32[256,256]{1,0:T(8,128)S(1)}, f32[256,256]{1,0:T(8,128)S(1)}, f32[256,256]{1,0:T(8,128)S(1)}) fusion(s32[256]{0:T(256)S(1)} %pad_add_fusion), kind=kLoop, calls=%fused_computation.143 | loop fusion | flops 983040 | bytes 787456 | tf_op jit(solution)/shard_map/neg | solution.py:130
  61.4 13.7 %all-to-all-done = bf16[32,2,4,2,512]{4,3,2,1,0:T(2,128)(2,1)S(1)} async-done(((bf16[32,2,4,2,512]{4,3,2,1,0:T(2,128)(2,1)}), bf16[32,2,4,2,512]{4,3,2,1,0:T(2,128)(2,1)S(1)}, u32[]{:S(2)}, u32[]{:S(2)}) %all-to-all-start) | async-done | bytes 524320 | tf_op jit(solution)/shard_map/all_to_all | solution.py:44
  75.1 0.4 fusion.143
  75.5 0.4 fusion.144
  75.9 0.3 fusion.99
  76.2 0.3 fusion.96
  76.5 0.3 convolution_add_fusion.1
  76.7 0.3 convolution_add_fusion
  77.0 0.4 fusion.145
  77.4 0.3 fusion.105
  77.7 0.3 convolution_add_fusion.3
  78.0 0.3 fusion.102
  78.3 0.3 convolution_add_fusion.2
  78.5 0.5 multiply_add_fusion
  79.0 1.0 fusion.146
  80.2 0.1 pad_maximum_fusion
  80.3 0.5 copy.56
  80.8 22.1 %all_to_all.20 = bf16[2,128,2,512]{3,2,0,1:T(2,128)(2,1)S(1)} all-to-all(bf16[2,128,2,512]{3,2,0,1:T(2,128)(2,1)S(1)} %copy.56), channel_id=1, replica_groups=mesh['space'=24,'energy'=32] {'energy'}, dimensions={1} | all-to-all | bytes 1048576 | tf_op jit(solution)/shard_map/all_to_all | solution.py:151
  102.9 0.3 copy.116
  103.2 0.3 reshape.157
  103.5 0.0 copy-done
  103.5 1.4 %fusion.2 = bf16[2,1,4,2,128,128]{5,4,3,2,1,0:T(8,128)(2,1)} fusion(bf16[2,4,2,128,128]{4,3,2,1,0:T(8,128)(2,1)S(1)} %reshape.157, bf16[1,128,128]{2,1,0:T(8,128)(2,1)S(1)} %copy-done), kind=kOutput, calls=%fused_computation.14 | convolution fusion | flops 134742016 | bytes 1081344 | tf_op jit(solution)/shard_map/fetnpr,nsr->fnetps/dot_general | solution.py:156
  (18 shorter events, 0.5 us)
Async XLA Ops:
  0.0 103.5 %copy-start = (bf16[1,128,128]{2,1,0:T(8,128)(2,1)S(1)}, bf16[1,128,128]{2,1,0:T(8,128)(2,1)}, u32[]{:S(2)}) copy-start(bf16[1,128,128]{2,1,0:T(8,128)(2,1)} %param.9) | copy-start | bytes 98308
  0.0 17.7 %copy-start.1 = (bf16[1,4,2,128,128]{4,3,2,1,0:T(8,128)(2,1)S(1)}, bf16[1,4,2,128,128]{4,3,2,1,0:T(8,128)(2,1)}, u32[]{:S(2)}) copy-start(bf16[1,4,2,128,128]{4,3,2,1,0:T(8,128)(2,1)} %param.5) | copy-start | bytes 786436
  0.0 18.5 %copy-start.2 = (bf16[1,4,2,128,128]{4,3,2,1,0:T(8,128)(2,1)S(1)}, bf16[1,4,2,128,128]{4,3,2,1,0:T(8,128)(2,1)}, u32[]{:S(2)}) copy-start(bf16[1,4,2,128,128]{4,3,2,1,0:T(8,128)(2,1)} %param.6) | copy-start | bytes 786436
  1.4 17.8 %copy-start.3 = (bf16[1,4,2,128,128]{4,3,2,1,0:T(8,128)(2,1)S(1)}, bf16[1,4,2,128,128]{4,3,2,1,0:T(8,128)(2,1)}, u32[]{:S(2)}) copy-start(bf16[1,4,2,128,128]{4,3,2,1,0:T(8,128)(2,1)} %param.7) | copy-start | bytes 786436
  1.4 21.5 %collective-permute-start = (bf16[2,1,4,2,128,128]{4,5,0,2,3,1:T(8,128)(2,1)S(1)}, bf16[2,1,4,2,128,128]{4,5,0,2,3,1:T(8,128)(2,1)S(1)}, u32[]{:S(2)}, u32[]{:S(2)}) collective-permute-start(bf16[2,1,4,2,128,128]{4,5,0,2,3,1:T(8,128)(2,1)S(1)} %copy.43), channel_id=1, source_target_pairs={{0,32},{32,64},{64,96},{96,128},{128,160},{160,192},{192,224},{224... | collective-permute-start | bytes 1572872 | tf_op jit(solution)/shard_map/ppermute | solution.py:16
  3.5 32.1 %collective-permute-start.1 = (bf16[2,1,4,2,128,128]{4,5,0,2,3,1:T(8,128)(2,1)S(1)}, bf16[2,1,4,2,128,128]{4,5,0,2,3,1:T(8,128)(2,1)S(1)}, u32[]{:S(2)}, u32[]{:S(2)}) collective-permute-start(bf16[2,1,4,2,128,128]{4,5,0,2,3,1:T(8,128)(2,1)S(1)} %copy.43), channel_id=1, source_target_pairs={{32,0},{64,32},{96,64},{128,96},{160,128},{192,160},{224,192},{256... | collective-permute-start | bytes 1572872 | tf_op jit(solution)/shard_map/ppermute | solution.py:17
  28.9 6.8 %copy-start.4 = (f32[4,256,2,128]{3,1,2,0:T(8,128)S(1)}, f32[4,256,2,128]{3,1,2,0:T(8,128)}, u32[]{:S(2)}) copy-start(f32[4,256,2,128]{3,1,2,0:T(8,128)} %convolution_add_fusion.5) | copy-start | bytes 3145732
  38.3 36.8 %all-to-all-start = ((bf16[32,2,4,2,512]{4,3,2,1,0:T(2,128)(2,1)}), bf16[32,2,4,2,512]{4,3,2,1,0:T(2,128)(2,1)S(1)}, u32[]{:S(2)}, u32[]{:S(2)}) async-start(bf16[32,2,4,2,512]{4,3,2,1,0:T(2,128)(2,1)} %copy.55), calls=%async_computation | async-start | bytes 1048576 | tf_op jit(solution)/shard_map/all_to_all | solution.py:44

commit v2 on v1

--- a/solution.py
+++ b/solution.py
@@ -93,11 +93,19 @@
     block_order = green_diag.shape[-1]
     energies = energy_local * lax.axis_size("energy")
     padded_len = 2 * energies
-    padded = padded_2(self_energy, (("space", 1),), 1)
-    lower_term = congruence(green_lower, padded[:, :block_count])
-    diag_term = congruence(green_diag, padded[:, 1 : block_count + 1])
-    upper_term = congruence(green_upper, padded[:, 2:])
-    total = lower_term + diag_term + upper_term
+    peers = lax.axis_size("space")
+    on_chip = [(i, i ^ 1) for i in range(peers - peers % 2)]
+    across = [(i, i + 1) for i in range(1, peers - 1, 2)]
+    across = across + [(j, i) for i, j in across]
+    partner = lax.ppermute(self_energy, "space", on_chip)
+    neighbour = lax.ppermute(self_energy, "space", across)
+    even = lax.axis_index("space") % 2 == 0
+    green_on = jnp.where(even, green_upper, green_lower)
+    green_across = jnp.where(even, green_lower, green_upper)
+    diag_term = congruence(green_diag, self_energy)
+    on_term = congruence(green_on, partner)
+    across_term = congruence(green_across, neighbour)
+    total = diag_term + on_term + across_term
     total = total.reshape(2, block_count, energy_local, block_order, 2, block_order)
     green_function = (
         jnp.transpose(total, (0, 2, 4, 1, 3, 5))

time: 105 us -> 101 us (0.962)
  the two profiles are of different devices: /device:TPU:14 before, /device:TPU:10 now
where the time goes in v2:
time: 101 us
  waiting for transfers between devices  30.4 us (30%)
  starting transfers between devices  27.2 us (27%)
  blocking collectives  22.1 us (22%)
  matrix products  11 us (11%)
  local copies, waits for them, and re-layouts  6.45 us (6%)
  other arithmetic  3.16 us (3%)
    all_to_all x1, blocking collectives, body(): lax.all_to_all(polar, 'energy', split_axis=1, concat_axis=3, tiled=True)  22.1 us
    ppermute x1, waiting for transfers between devices, body(): neighbour = lax.ppermute(self_energy, 'space', across)  16.2 us
    ppermute x1, starting transfers between devices, body(): neighbour = lax.ppermute(self_energy, 'space', across)  14.6 us
    all_to_all x1, waiting for transfers between devices, cut_exchange(): lax.all_to_all(slab, axis, split_axis=0, concat_axis=0, tiled=True)  14.2 us
    all_to_all x1, starting transfers between devices, cut_exchange(): lax.all_to_all(slab, axis, split_axis=0, concat_axis=0, tiled=True)  10.6 us
    dot_general x3, matrix products, congruence(): jnp.einsum('fnepr,nesr->fneps', mixed, adjoint_tall, preferred_element_ty...  6.34 us
    ppermute x1, starting transfers between devices, body(): partner = lax.ppermute(self_energy, 'space', on_chip)  2.05 us
  transfers between devices with their start and end apart: 3, of which 2 were waited for; matrix products, arithmetic and copies ran while one was open for 9% of the time, Pallas kernels for 0%

profile of v2, /device:TPU:10, one launch (start us, length us, event | category | flops | bytes accessed | tf_op | source)
XLA Modules:
  0.0 100.7 jit_solution(1399553083024055906)
XLA Ops:
  0.0 0.0 copy-start
  0.0 1.3 %copy.43 = bf16[2,1,4,2,128,128]{4,5,0,2,3,1:T(8,128)(2,1)S(1)} copy(bf16[2,1,4,2,128,128]{5,4,3,2,1,0:T(8,128)(2,1)} %param.8) | data formatting | bytes 1048576 | tf_op args[3]
  1.3 0.0 copy-start.1
  1.3 2.1 %collective-permute-start = (bf16[2,1,4,2,128,128]{4,5,0,2,3,1:T(8,128)(2,1)S(1)}, bf16[2,1,4,2,128,128]{4,5,0,2,3,1:T(8,128)(2,1)S(1)}, u32[]{:S(2)}, u32[]{:S(2)}) collective-permute-start(bf16[2,1,4,2,128,128]{4,5,0,2,3,1:T(8,128)(2,1)S(1)} %copy.43), channel_id=1, source_target_pairs={{0,32},{32,0},{64,96},{96,64},{128,160},{160,128},{192,224},{224,1... | collective-permute-start | bytes 1572872 | tf_op jit(solution)/shard_map/ppermute | solution.py:100
  3.4 14.6 %collective-permute-start.1 = (bf16[2,1,4,2,128,128]{4,5,0,2,3,1:T(8,128)(2,1)S(1)}, bf16[2,1,4,2,128,128]{4,5,0,2,3,1:T(8,128)(2,1)S(1)}, u32[]{:S(2)}, u32[]{:S(2)}) collective-permute-start(bf16[2,1,4,2,128,128]{4,5,0,2,3,1:T(8,128)(2,1)S(1)} %copy.43), channel_id=1, source_target_pairs={{32,64},{96,128},{160,192},{224,256},{288,320},{352,384},{416,448}... | collective-permute-start | bytes 1572872 | tf_op jit(solution)/shard_map/ppermute | solution.py:101
  18.0 0.0 copy-start.2
  18.1 0.0 copy-start.3
  18.2 0.0 copy-done.1
  18.2 0.7 slice_bitcast_fusion.13
  18.9 0.7 fusion.133
  19.6 0.0 copy-done.2
  19.6 0.0 copy-done.3
  19.7 2.8 %fusion.4 = f32[4,256,2,128]{3,1,2,0:T(8,128)} fusion(bf16[2,1,4,128,128]{3,4,0,2,1:T(8,128)(2,1)S(1)} %get-tuple-element.19, bf16[2,1,4,128,128]{3,4,0,2,1:T(8,128)(2,1)S(1)} %fusion.136, bf16[2,1,4,128,128]{3,4,0,2,1:T(8,128)(2,1)S(1)} %get-tuple-element.18, bf16[1,4,128,128]{3,2,1,0:T(8,128)(2,1)} %get-tuple-element.29, ...), kind=kOutput, calls=%fused_computation.16 | convolution fusion | flops 275513344 | bytes 2228224 | tf_op jit(solution)/shard_map/fnepr,nesr->fneps/dot_general | solution.py:67
  22.6 0.0 collective-permute-done
  22.7 2.9 %convolution_add_fusion.5 = f32[4,256,2,128]{3,1,2,0:T(8,128)} fusion(f32[4,256,2,128]{3,1,2,0:T(8,128)} %fusion.4, bf16[2,1,4,128,128]{3,4,0,2,1:T(8,128)(2,1)S(1)} %get-tuple-element.17, bf16[2,1,4,128,128]{3,4,0,2,1:T(8,128)(2,1)S(1)} %fusion.137, bf16[2,1,4,128,128]{3,4,0,2,1:T(8,128)(2,1)S(1)} %get-tuple-element.16, ...), kind=kOutput, calls=%fused_computation.6 | convolution fusion | flops 275775488 | bytes 3276800 | tf_op jit(solution)/shard_map/fnepr,nesr->fneps/dot_general | solution.py:67
  25.5 0.0 copy-start.4
  25.5 16.2 %collective-permute-done.1 = bf16[2,1,4,2,128,128]{4,5,0,2,3,1:T(8,128)(2,1)S(1)} collective-permute-done((bf16[2,1,4,2,128,128]{4,5,0,2,3,1:T(8,128)(2,1)S(1)}, bf16[2,1,4,2,128,128]{4,5,0,2,3,1:T(8,128)(2,1)S(1)}, u32[]{:S(2)}, u32[]{:S(2)}) %collective-permute-start.1) | collective-permute-done | bytes 524320 | tf_op jit(solution)/shard_map/ppermute | solution.py:101
  41.8 0.0 copy-done.4
  41.8 0.6 fusion
  42.5 0.3 copy.54
  42.8 0.3 reshape_reshape.3
  43.1 1.3 %copy.55 = bf16[32,2,4,2,512]{4,3,2,1,0:T(2,128)(2,1)} copy(bf16[32,2,4,2,512]{4,0,3,2,1:T(8,128)(2,1)S(1)} %bitcast.202) | data formatting | bytes 1048576 | tf_op jit(solution)/shard_map/transpose | solution.py:24
  44.4 10.6 %all-to-all-start = ((bf16[32,2,4,2,512]{4,3,2,1,0:T(2,128)(2,1)}), bf16[32,2,4,2,512]{4,3,2,1,0:T(2,128)(2,1)S(1)}, u32[]{:S(2)}, u32[]{:S(2)}) async-start(bf16[32,2,4,2,512]{4,3,2,1,0:T(2,128)(2,1)} %copy.55), calls=%async_computation | async-start | bytes 1048576 | tf_op jit(solution)/shard_map/all_to_all | solution.py:44
  55.0 0.5 fusion.113
  55.6 1.1 %fusion.112 = (f32[256,256]{1,0:T(8,128)S(1)}, f32[256,256]{1,0:T(8,128)S(1)}, f32[256,256]{1,0:T(8,128)S(1)}) fusion(s32[256]{0:T(256)S(1)} %pad_add_fusion), kind=kLoop, calls=%fused_computation.145 | loop fusion | flops 983040 | bytes 787456 | tf_op jit(solution)/shard_map/neg | solution.py:138
  56.7 14.2 %all-to-all-done = bf16[32,2,4,2,512]{4,3,2,1,0:T(2,128)(2,1)S(1)} async-done(((bf16[32,2,4,2,512]{4,3,2,1,0:T(2,128)(2,1)}), bf16[32,2,4,2,512]{4,3,2,1,0:T(2,128)(2,1)S(1)}, u32[]{:S(2)}, u32[]{:S(2)}) %all-to-all-start) | async-done | bytes 524320 | tf_op jit(solution)/shard_map/all_to_all | solution.py:44
  70.9 0.4 fusion.143
  71.3 0.4 fusion.144
  71.6 0.3 fusion.99
  71.9 0.3 fusion.96
  72.2 0.3 convolution_add_fusion.1
  72.5 0.3 convolution_add_fusion
  72.8 0.4 fusion.145
  73.2 0.3 fusion.105
  73.5 0.3 convolution_add_fusion.3
  73.7 0.3 fusion.102
  74.0 0.3 convolution_add_fusion.2
  74.3 0.5 multiply_add_fusion
  74.8 1.0 %fusion.146 = (bf16[512,512]{1,0:T(8,128)(2,1)S(1)}, f32[512,512]{1,0:T(8,128)S(1)}) fusion(f32[256,512]{1,0:T(8,128)S(1)} %get-tuple-element.6, f32[256,512]{1,0:T(8,128)S(1)} %get-tuple-element.5, f32[256,256]{1,0:T(8,128)S(1)} %get-tuple-element.32, f32[256,256]{1,0:T(8,128)S(1)} %get-tuple-element.31, f32[256,256]{1,0:T(8,128)S(1)} %get-tuple-element.30), kind=kOutput, calls=%fused_computation.175 | convolution fusion | flops 806879232 | bytes 3407872 | tf_op jit(solution)/shard_map/dot_general | solution.py:146
  76.0 0.1 pad_maximum_fusion
  76.1 0.5 copy.56
  76.6 22.1 %all_to_all.20 = bf16[2,128,2,512]{3,2,0,1:T(2,128)(2,1)S(1)} all-to-all(bf16[2,128,2,512]{3,2,0,1:T(2,128)(2,1)S(1)} %copy.56), channel_id=1, replica_groups=mesh['space'=24,'energy'=32] {'energy'}, dimensions={1} | all-to-all | bytes 1048576 | tf_op jit(solution)/shard_map/all_to_all | solution.py:159
  98.7 0.3 copy.116
  99.0 0.3 reshape.157
  99.3 0.0 copy-done
  99.3 1.4 %fusion.2 = bf16[2,1,4,2,128,128]{5,4,3,2,1,0:T(8,128)(2,1)} fusion(bf16[2,4,2,128,128]{4,3,2,1,0:T(8,128)(2,1)S(1)} %reshape.157, bf16[1,128,128]{2,1,0:T(8,128)(2,1)S(1)} %copy-done), kind=kOutput, calls=%fused_computation.14 | convolution fusion | flops 134742016 | bytes 1081344 | tf_op jit(solution)/shard_map/fetnpr,nsr->fnetps/dot_general | solution.py:164
  (18 shorter events, 0.5 us)
Async XLA Ops:
  0.0 99.3 %copy-start = (bf16[1,128,128]{2,1,0:T(8,128)(2,1)S(1)}, bf16[1,128,128]{2,1,0:T(8,128)(2,1)}, u32[]{:S(2)}) copy-start(bf16[1,128,128]{2,1,0:T(8,128)(2,1)} %param.9) | copy-start | bytes 98308
  1.3 16.8 %copy-start.1 = (bf16[1,4,2,128,128]{4,3,2,1,0:T(8,128)(2,1)S(1)}, bf16[1,4,2,128,128]{4,3,2,1,0:T(8,128)(2,1)}, u32[]{:S(2)}) copy-start(bf16[1,4,2,128,128]{4,3,2,1,0:T(8,128)(2,1)} %param.6) | copy-start | bytes 786436
  1.3 21.2 %collective-permute-start = (bf16[2,1,4,2,128,128]{4,5,0,2,3,1:T(8,128)(2,1)S(1)}, bf16[2,1,4,2,128,128]{4,5,0,2,3,1:T(8,128)(2,1)S(1)}, u32[]{:S(2)}, u32[]{:S(2)}) collective-permute-start(bf16[2,1,4,2,128,128]{4,5,0,2,3,1:T(8,128)(2,1)S(1)} %copy.43), channel_id=1, source_target_pairs={{0,32},{32,0},{64,96},{96,64},{128,160},{160,128},{192,224},{224,1... | collective-permute-start | bytes 1572872 | tf_op jit(solution)/shard_map/ppermute | solution.py:100
  3.4 38.3 %collective-permute-start.1 = (bf16[2,1,4,2,128,128]{4,5,0,2,3,1:T(8,128)(2,1)S(1)}, bf16[2,1,4,2,128,128]{4,5,0,2,3,1:T(8,128)(2,1)S(1)}, u32[]{:S(2)}, u32[]{:S(2)}) collective-permute-start(bf16[2,1,4,2,128,128]{4,5,0,2,3,1:T(8,128)(2,1)S(1)} %copy.43), channel_id=1, source_target_pairs={{32,64},{96,128},{160,192},{224,256},{288,320},{352,384},{416,448}... | collective-permute-start | bytes 1572872 | tf_op jit(solution)/shard_map/ppermute | solution.py:101
  18.0 1.5 %copy-start.2 = (bf16[1,4,2,128,128]{4,3,2,1,0:T(8,128)(2,1)S(1)}, bf16[1,4,2,128,128]{4,3,2,1,0:T(8,128)(2,1)}, u32[]{:S(2)}) copy-start(bf16[1,4,2,128,128]{4,3,2,1,0:T(8,128)(2,1)} %param.5) | copy-start | bytes 786436
  18.1 1.5 %copy-start.3 = (bf16[1,4,2,128,128]{4,3,2,1,0:T(8,128)(2,1)S(1)}, bf16[1,4,2,128,128]{4,3,2,1,0:T(8,128)(2,1)}, u32[]{:S(2)}) copy-start(bf16[1,4,2,128,128]{4,3,2,1,0:T(8,128)(2,1)} %param.7) | copy-start | bytes 786436
  25.5 16.3 %copy-start.4 = (f32[4,256,2,128]{3,1,2,0:T(8,128)S(1)}, f32[4,256,2,128]{3,1,2,0:T(8,128)}, u32[]{:S(2)}) copy-start(f32[4,256,2,128]{3,1,2,0:T(8,128)} %convolution_add_fusion.5) | copy-start | bytes 3145732
  44.4 26.5 %all-to-all-start = ((bf16[32,2,4,2,512]{4,3,2,1,0:T(2,128)(2,1)}), bf16[32,2,4,2,512]{4,3,2,1,0:T(2,128)(2,1)S(1)}, u32[]{:S(2)}, u32[]{:S(2)}) async-start(bf16[32,2,4,2,512]{4,3,2,1,0:T(2,128)(2,1)} %copy.55), calls=%async_computation | async-start | bytes 1048576 | tf_op jit(solution)/shard_map/all_to_all | solution.py:44

commit v3 on v2

--- a/solution.py
+++ b/solution.py
@@ -119,43 +119,41 @@
         jnp.float32
     ) * step_angle
     forward_table = jnp.concatenate([jnp.cos(forward_angle), jnp.sin(forward_angle)], axis=0)
-    table_high, table_low = split_table(forward_table)
     entries = cut_exchange(green_function, "energy", 1, 3, 1)
-    lesser_values = entries[0]
-    greater_values = entries[1]
-    lesser_real, lesser_imag = spectrum(lesser_values, table_high, table_low, padded_len)
-    greater_real, greater_imag = spectrum(greater_values, table_high, table_low, padded_len)
-    product_real = lesser_real * greater_real + lesser_imag * greater_imag
-    product_imag = lesser_imag * greater_real - lesser_real * greater_imag
-    row_index = jnp.concatenate([energy_index, (padded_len - energy_index) % padded_len])
-    back_angle = (row_index[:, None] * frequency[None, :] % padded_len).astype(
-        jnp.float32
-    ) * step_angle
-    back_cos = jnp.cos(back_angle)
-    back_sin = jnp.sin(back_angle)
-    back_table = jnp.concatenate(
-        [
-            jnp.concatenate([back_cos, -back_sin], axis=1),
-            jnp.concatenate([back_sin, back_cos], axis=1),
-        ],
-        axis=0,
+    spectra = jnp.einsum(
+        "qe,fern->qfrn",
+        forward_table.astype(jnp.bfloat16),
+        entries,
+        preferred_element_type=jnp.float32,
     )
+    cos_part = spectra[:padded_len]
+    sin_part = spectra[padded_len:]
+    spec_real = cos_part[:, :, 0] + sin_part[:, :, 1]
+    spec_imag = cos_part[:, :, 1] - sin_part[:, :, 0]
+    product_real = spec_real[:, 0] * spec_real[:, 1] + spec_imag[:, 0] * spec_imag[:, 1]
+    product_imag = spec_imag[:, 0] * spec_real[:, 1] - spec_real[:, 0] * spec_imag[:, 1]
     stacked_product = jnp.concatenate([product_real, product_imag], axis=0)
+    mirrored = (padded_len - energy_index) % padded_len
+
+    def back_rows(lags):
+        angle = (lags[:, None] * frequency[None, :] % padded_len).astype(jnp.float32) * step_angle
+        cos_rows, sin_rows = jnp.cos(angle), jnp.sin(angle)
+        real_rows = jnp.concatenate([cos_rows, -sin_rows], axis=1)
+        imag_rows = jnp.concatenate([sin_rows, cos_rows], axis=1)
+        return real_rows, imag_rows
+
+    lesser_real, lesser_imag = back_rows(energy_index)
+    greater_real, greater_imag = back_rows(mirrored)
+    back_table = jnp.stack([lesser_real, lesser_imag, greater_real, -greater_imag], axis=1)
+    back_table = back_table.reshape(4 * energies, 2 * padded_len)
     factor = 1.0 / (padded_len * math.sqrt(energies))
-    combined = (
-        jnp.dot(
-            back_table,
-            stacked_product,
-            precision=lax.Precision.HIGH,
-            preferred_element_type=jnp.float32,
-        )
-        * factor
+    combined = jnp.dot(
+        back_table.astype(jnp.bfloat16),
+        stacked_product.astype(jnp.bfloat16),
+        preferred_element_type=jnp.float32,
     )
-    corr_real = combined[:padded_len]
-    corr_imag = combined[padded_len:]
-    lesser_lags = jnp.stack([corr_real[:energies], corr_imag[:energies]], axis=1)
-    greater_lags = jnp.stack([corr_real[energies:], -corr_imag[energies:]], axis=1)
-    polar = jnp.stack([lesser_lags, greater_lags], axis=0).astype(jnp.bfloat16)
+    polar = (combined * factor).reshape(energies, 2, 2, -1)
+    polar = jnp.transpose(polar, (1, 0, 2, 3)).astype(jnp.bfloat16)
     returned = lax.all_to_all(polar, "energy", split_axis=1, concat_axis=3, tiled=True)
     returned = returned.reshape(2, energy_local, 2, block_count, block_order, block_order)
     left_product = jnp.einsum(

time: 101 us -> 99 us (0.980)
  the two profiles are of different devices: /device:TPU:10 before, /device:TPU:12 now
where the time goes in v3:
time: 99 us; the launch traced here: 98.6 us
  starting transfers between devices  26.9 us (27%)
  waiting for transfers between devices  26 us (26%)
  blocking collectives  22.1 us (22%)
  matrix products  10.1 us (10%)
  local copies, waits for them, and re-layouts  7.81 us (8%)
  other arithmetic  5.26 us (5%)
    all_to_all x1, blocking collectives, body(): lax.all_to_all(polar, 'energy', split_axis=1, concat_axis=3, tiled=True)  22.1 us
    ppermute x1, waiting for transfers between devices, body(): neighbour = lax.ppermute(self_energy, 'space', across)  14.8 us
    ppermute x1, starting transfers between devices, body(): neighbour = lax.ppermute(self_energy, 'space', across)  14.6 us
    all_to_all x1, waiting for transfers between devices, cut_exchange(): lax.all_to_all(slab, axis, split_axis=0, concat_axis=0, tiled=True)  11.3 us
    all_to_all x1, starting transfers between devices, cut_exchange(): lax.all_to_all(slab, axis, split_axis=0, concat_axis=0, tiled=True)  10.4 us
    dot_general x3, matrix products, congruence(): jnp.einsum('fnepr,nesr->fneps', mixed, adjoint_tall, preferred_element_ty...  7.57 us
    another operation x5, other arithmetic  2.46 us
    unnamed x13, local copies, waits for them, and re-layouts  2.2 us
  transfers between devices with their start and end apart: 3, of which 2 were waited for; matrix products, arithmetic and copies ran while one was open for 13% of the time, Pallas kernels for 0%

profile of v3, /device:TPU:12, one launch (start us, length us, event | category | flops | bytes accessed | tf_op | source)
XLA Modules:
  0.0 98.6 jit_solution(6373981774576564448)
XLA Ops:
  0.0 0.0 copy-start
  0.0 0.0 copy-start.3
  0.0 1.4 %copy.79 = bf16[2,1,4,2,128,128]{4,5,0,2,3,1:T(8,128)(2,1)S(1)} copy(bf16[2,1,4,2,128,128]{5,4,3,2,1,0:T(8,128)(2,1)} %param.8) | data formatting | bytes 1048576 | tf_op args[3]
  1.4 1.9 %collective-permute-start = (bf16[2,1,4,2,128,128]{4,5,0,2,3,1:T(8,128)(2,1)S(1)}, bf16[2,1,4,2,128,128]{4,5,0,2,3,1:T(8,128)(2,1)S(1)}, u32[]{:S(2)}, u32[]{:S(2)}) collective-permute-start(bf16[2,1,4,2,128,128]{4,5,0,2,3,1:T(8,128)(2,1)S(1)} %copy.79), channel_id=1, source_target_pairs={{0,32},{32,0},{64,96},{96,64},{128,160},{160,128},{192,224},{224,1... | collective-permute-start | bytes 1572872 | tf_op jit(solution)/shard_map/ppermute | solution.py:100
  3.3 14.6 %collective-permute-start.1 = (bf16[2,1,4,2,128,128]{4,5,0,2,3,1:T(8,128)(2,1)S(1)}, bf16[2,1,4,2,128,128]{4,5,0,2,3,1:T(8,128)(2,1)S(1)}, u32[]{:S(2)}, u32[]{:S(2)}) collective-permute-start(bf16[2,1,4,2,128,128]{4,5,0,2,3,1:T(8,128)(2,1)S(1)} %copy.79), channel_id=1, source_target_pairs={{32,64},{96,128},{160,192},{224,256},{288,320},{352,384},{416,448}... | collective-permute-start | bytes 1572872 | tf_op jit(solution)/shard_map/ppermute | solution.py:101
  18.1 0.0 copy-done.1
  18.1 0.7 slice_bitcast_fusion.12
  18.8 0.7 fusion.121
  19.5 0.0 copy-done.2
  19.5 0.0 copy-done.3
  19.5 0.7 slice_bitcast_fusion.10
  20.3 2.8 %fusion.5 = f32[4,256,2,128]{3,1,2,0:T(8,128)} fusion(bf16[2,1,4,128,128]{3,4,0,2,1:T(8,128)(2,1)S(1)} %get-tuple-element.14, bf16[2,1,4,128,128]{3,4,0,2,1:T(8,128)(2,1)S(1)} %fusion.124, bf16[2,1,4,128,128]{3,4,0,2,1:T(8,128)(2,1)S(1)} %get-tuple-element.13, bf16[1,4,128,128]{3,2,1,0:T(8,128)(2,1)} %get-tuple-element.20, ...), kind=kOutput, calls=%fused_computation.13 | convolution fusion | flops 275513344 | bytes 2228224 | tf_op jit(solution)/shard_map/fnepr,nesr->fneps/dot_general | solution.py:67
  23.2 0.0 collective-permute-done
  23.3 0.7 copy-done.4
  24.0 0.1 copy-done.5
  24.1 2.9 %convolution_add_fusion.1 = f32[4,256,2,128]{3,1,2,0:T(8,128)} fusion(f32[4,256,2,128]{3,1,2,0:T(8,128)} %fusion.5, bf16[2,1,4,128,128]{3,4,0,2,1:T(8,128)(2,1)S(1)} %get-tuple-element.12, bf16[2,1,4,128,128]{3,4,0,2,1:T(8,128)(2,1)S(1)} %fusion.125, bf16[2,1,4,128,128]{3,4,0,2,1:T(8,128)(2,1)S(1)} %get-tuple-element.11, ...), kind=kOutput, calls=%fused_computation.2 | convolution fusion | flops 275775488 | bytes 3276800 | tf_op jit(solution)/shard_map/fnepr,nesr->fneps/dot_general | solution.py:67
  26.9 14.8 %collective-permute-done.1 = bf16[2,1,4,2,128,128]{4,5,0,2,3,1:T(8,128)(2,1)S(1)} collective-permute-done((bf16[2,1,4,2,128,128]{4,5,0,2,3,1:T(8,128)(2,1)S(1)}, bf16[2,1,4,2,128,128]{4,5,0,2,3,1:T(8,128)(2,1)S(1)}, u32[]{:S(2)}, u32[]{:S(2)}) %collective-permute-start.1) | collective-permute-done | bytes 524320 | tf_op jit(solution)/shard_map/ppermute | solution.py:101
  41.8 1.9 %fusion = bf16[4,256,2,128]{3,1,2,0:T(8,128)(2,1)S(1)} fusion(f32[4,256,2,128]{3,1,2,0:T(8,128)} %convolution_add_fusion.1, bf16[2,1,4,128,128]{3,4,0,2,1:T(8,128)(2,1)S(1)} %get-tuple-element.10, bf16[2,1,4,128,128]{3,4,0,2,1:T(8,128)(2,1)S(1)} %fusion.126, bf16[2,1,4,128,128]{3,4,0,2,1:T(8,128)(2,1)S(1)} %get-tuple-element.9, ...), kind=kOutput, calls=%fused_computation.8 | convolution fusion | flops 276037632 | bytes 2752512 | tf_op jit(solution)/shard_map/fnepr,nesr->fneps/dot_general | solution.py:67
  43.6 0.3 copy.90
  43.9 0.3 reshape_reshape.3
  44.3 1.3 %copy.91 = bf16[32,2,4,2,512]{4,3,2,1,0:T(2,128)(2,1)} copy(bf16[32,2,4,2,512]{4,0,3,2,1:T(8,128)(2,1)S(1)} %bitcast.197) | data formatting | bytes 1048576 | tf_op jit(solution)/shard_map/transpose | solution.py:24
  45.6 10.4 %all-to-all-start = ((bf16[32,2,4,2,512]{4,3,2,1,0:T(2,128)(2,1)}), bf16[32,2,4,2,512]{4,3,2,1,0:T(2,128)(2,1)S(1)}, u32[]{:S(2)}, u32[]{:S(2)}) async-start(bf16[32,2,4,2,512]{4,3,2,1,0:T(2,128)(2,1)} %copy.91), calls=%async_computation | async-start | bytes 1048576 | tf_op jit(solution)/shard_map/all_to_all | solution.py:44
  56.0 0.6 fusion.109
  56.6 0.2 copy.76
  56.9 0.1 concatenate.92
  57.0 0.1 copy.73
  57.1 0.5 fusion.105
  57.6 0.5 negate_convert_fusion.1
  58.2 0.2 copy.74
  58.4 0.2 copy.75
  58.6 0.3 fusion.70
  58.9 1.2 %pad_maximum_fusion = bf16[128,4,512]{2,1,0:T(4,128)(2,1)S(1)} fusion(bf16[128,1,512]{2,1,0:T(2,128)(2,1)S(1)} %fusion.70, bf16[128,1,512]{2,1,0:T(2,128)(2,1)S(1)} %copy.76, bf16[128,1,512]{2,1,0:T(2,128)(2,1)S(1)} %copy.75, bf16[128,1,512]{2,1,0:T(2,128)(2,1)S(1)} %copy.74), kind=kLoop, calls=%fused_computation.43 | loop fusion | flops 2097152 | bytes 1048576 | tf_op jit(solution)/shard_map/stack | solution.py:147
  60.1 0.1 convert_element_type.115
  60.2 0.5 sine_convert_fusion
  60.8 11.3 %all-to-all-done = bf16[32,2,4,2,512]{4,3,2,1,0:T(2,128)(2,1)S(1)} async-done(((bf16[32,2,4,2,512]{4,3,2,1,0:T(2,128)(2,1)}), bf16[32,2,4,2,512]{4,3,2,1,0:T(2,128)(2,1)S(1)}, u32[]{:S(2)}, u32[]{:S(2)}) %all-to-all-start) | async-done | bytes 524320 | tf_op jit(solution)/shard_map/all_to_all | solution.py:44
  72.1 0.2 copy.92
  72.3 0.1 reshape.236
  72.4 0.7 fusion.92
  73.1 0.2 fusion.10
  73.3 0.2 fusion.8
  73.5 0.3 fusion.68
  73.8 0.4 fusion.1
  74.2 0.2 convert_element_type.132
  74.4 22.1 %all_to_all.20 = bf16[2,128,2,512]{3,2,0,1:T(2,128)(2,1)S(1)} all-to-all(bf16[2,128,2,512]{3,2,0,1:T(2,128)(2,1)S(1)} %bitcast.198), channel_id=1, replica_groups=mesh['space'=24,'energy'=32] {'energy'}, dimensions={1} | all-to-all | bytes 1048576 | tf_op jit(solution)/shard_map/all_to_all | solution.py:157
  96.5 0.3 copy.96
  96.8 0.3 reshape.237
  97.1 0.0 copy-done
  97.1 1.4 %fusion.3 = bf16[2,1,4,2,128,128]{5,4,3,2,1,0:T(8,128)(2,1)} fusion(bf16[2,4,2,128,128]{4,3,2,1,0:T(8,128)(2,1)S(1)} %reshape.237, bf16[1,128,128]{2,1,0:T(8,128)(2,1)S(1)} %copy-done), kind=kOutput, calls=%fused_computation.11 | convolution fusion | flops 134742016 | bytes 1081344 | tf_op jit(solution)/shard_map/fetnpr,nsr->fnetps/dot_general | solution.py:162
  (16 shorter events, 0.4 us)
Async XLA Ops:
  0.0 97.1 %copy-start = (bf16[1,128,128]{2,1,0:T(8,128)(2,1)S(1)}, bf16[1,128,128]{2,1,0:T(8,128)(2,1)}, u32[]{:S(2)}) copy-start(bf16[1,128,128]{2,1,0:T(8,128)(2,1)} %param.9) | copy-start | bytes 98308
  0.0 18.1 %copy-start.1 = (bf16[1,4,2,128,128]{4,3,2,1,0:T(8,128)(2,1)S(1)}, bf16[1,4,2,128,128]{4,3,2,1,0:T(8,128)(2,1)}, u32[]{:S(2)}) copy-start(bf16[1,4,2,128,128]{4,3,2,1,0:T(8,128)(2,1)} %param.6) | copy-start | bytes 786436
  0.0 19.5 %copy-start.2 = (bf16[1,4,2,128,128]{4,3,2,1,0:T(8,128)(2,1)S(1)}, bf16[1,4,2,128,128]{4,3,2,1,0:T(8,128)(2,1)}, u32[]{:S(2)}) copy-start(bf16[1,4,2,128,128]{4,3,2,1,0:T(8,128)(2,1)} %param.5) | copy-start | bytes 786436
  0.0 19.5 %copy-start.3 = (bf16[1,4,2,128,128]{4,3,2,1,0:T(8,128)(2,1)S(1)}, bf16[1,4,2,128,128]{4,3,2,1,0:T(8,128)(2,1)}, u32[]{:S(2)}) copy-start(bf16[1,4,2,128,128]{4,3,2,1,0:T(8,128)(2,1)} %param.7) | copy-start | bytes 786436
  1.4 21.8 %collective-permute-start = (bf16[2,1,4,2,128,128]{4,5,0,2,3,1:T(8,128)(2,1)S(1)}, bf16[2,1,4,2,128,128]{4,5,0,2,3,1:T(8,128)(2,1)S(1)}, u32[]{:S(2)}, u32[]{:S(2)}) collective-permute-start(bf16[2,1,4,2,128,128]{4,5,0,2,3,1:T(8,128)(2,1)S(1)} %copy.79), channel_id=1, source_target_pairs={{0,32},{32,0},{64,96},{96,64},{128,160},{160,128},{192,224},{224,1... | collective-permute-start | bytes 1572872 | tf_op jit(solution)/shard_map/ppermute | solution.py:100
  3.3 38.3 %collective-permute-start.1 = (bf16[2,1,4,2,128,128]{4,5,0,2,3,1:T(8,128)(2,1)S(1)}, bf16[2,1,4,2,128,128]{4,5,0,2,3,1:T(8,128)(2,1)S(1)}, u32[]{:S(2)}, u32[]{:S(2)}) collective-permute-start(bf16[2,1,4,2,128,128]{4,5,0,2,3,1:T(8,128)(2,1)S(1)} %copy.79), channel_id=1, source_target_pairs={{32,64},{96,128},{160,192},{224,256},{288,320},{352,384},{416,448}... | collective-permute-start | bytes 1572872 | tf_op jit(solution)/shard_map/ppermute | solution.py:101
  23.1 0.9 copy-start.4
  23.1 1.0 copy-start.5
  45.6 26.5 %all-to-all-start = ((bf16[32,2,4,2,512]{4,3,2,1,0:T(2,128)(2,1)}), bf16[32,2,4,2,512]{4,3,2,1,0:T(2,128)(2,1)S(1)}, u32[]{:S(2)}, u32[]{:S(2)}) async-start(bf16[32,2,4,2,512]{4,3,2,1,0:T(2,128)(2,1)} %copy.91), calls=%async_computation | async-start | bytes 1048576 | tf_op jit(solution)/shard_map/all_to_all | solution.py:44

commit v4 on v3

--- a/solution.py
+++ b/solution.py
@@ -106,12 +106,10 @@
     on_term = congruence(green_on, partner)
     across_term = congruence(green_across, neighbour)
     total = diag_term + on_term + across_term
-    total = total.reshape(2, block_count, energy_local, block_order, 2, block_order)
-    green_function = (
-        jnp.transpose(total, (0, 2, 4, 1, 3, 5))
-        .astype(jnp.bfloat16)
-        .reshape(2, energy_local, 2, -1)
-    )
+    groups = lax.axis_size("energy")
+    total = total.reshape(2, block_count, energy_local, groups, block_order // groups, 2, block_order)
+    outgoing = jnp.transpose(total, (3, 0, 2, 5, 1, 4, 6)).astype(jnp.bfloat16)
+    outgoing = outgoing.reshape(groups, 2, energy_local, 2, -1)
     frequency = lax.iota(jnp.int32, padded_len)
     energy_index = lax.iota(jnp.int32, energies)
     step_angle = 2.0 * math.pi / padded_len
@@ -119,10 +117,10 @@
         jnp.float32
     ) * step_angle
     forward_table = jnp.concatenate([jnp.cos(forward_angle), jnp.sin(forward_angle)], axis=0)
-    entries = cut_exchange(green_function, "energy", 1, 3, 1)
+    entries = lax.all_to_all(outgoing, "energy", 0, 0, tiled=True)
     spectra = jnp.einsum(
-        "qe,fern->qfrn",
-        forward_table.astype(jnp.bfloat16),
+        "qxe,xfern->qfrn",
+        forward_table.astype(jnp.bfloat16).reshape(2 * padded_len, groups, energy_local),
         entries,
         preferred_element_type=jnp.float32,
     )
@@ -152,9 +150,10 @@
         stacked_product.astype(jnp.bfloat16),
         preferred_element_type=jnp.float32,
     )
-    polar = (combined * factor).reshape(energies, 2, 2, -1)
-    polar = jnp.transpose(polar, (1, 0, 2, 3)).astype(jnp.bfloat16)
-    returned = lax.all_to_all(polar, "energy", split_axis=1, concat_axis=3, tiled=True)
+    polar = (combined * factor).astype(jnp.bfloat16).reshape(groups, energy_local, 2, 2, -1)
+    returned = lax.all_to_all(polar, "energy", 0, 0, tiled=True)
+    returned = returned.reshape(groups, energy_local, 2, 2, block_count, -1, block_order)
+    returned = jnp.transpose(returned, (2, 1, 3, 4, 0, 5, 6))
     returned = returned.reshape(2, energy_local, 2, block_count, block_order, block_order)
     left_product = jnp.einsum(
         "npq,fetnqr->fetnpr", coulomb, returned, preferred_element_type=jnp.float32

time: 99 us -> 98.3 us (level)
  the two profiles are of different devices: /device:TPU:12 before, /device:TPU:10 now
where the time goes in v4:
time: 98.3 us; the launch traced here: 97.9 us
  starting transfers between devices  27.1 us (28%)
  waiting for transfers between devices  25.9 us (26%)
  blocking collectives  22.1 us (22%)
  matrix products  10.2 us (10%)
  local copies, waits for them, and re-layouts  7.09 us (7%)
  other arithmetic  5.33 us (5%)
    all_to_all x1, blocking collectives, body(): returned = lax.all_to_all(polar, 'energy', 0, 0, tiled=True)  22.1 us
    ppermute x1, waiting for transfers between devices, body(): neighbour = lax.ppermute(self_energy, 'space', across)  14.8 us
    ppermute x1, starting transfers between devices, body(): neighbour = lax.ppermute(self_energy, 'space', across)  14.6 us
    all_to_all x1, waiting for transfers between devices, body(): entries = lax.all_to_all(outgoing, 'energy', 0, 0, tiled=True)  11.1 us
    all_to_all x1, starting transfers between devices, body(): entries = lax.all_to_all(outgoing, 'energy', 0, 0, tiled=True)  10.5 us
    dot_general x3, matrix products, congruence(): jnp.einsum('fnepr,nesr->fneps', mixed, adjoint_tall, preferred_element_ty...  7.58 us
    another operation x5, other arithmetic  2.52 us
    unnamed x13, local copies, waits for them, and re-layouts  2.2 us
  transfers between devices with their start and end apart: 3, of which 2 were waited for; matrix products, arithmetic and copies ran while one was open for 13% of the time, Pallas kernels for 0%

profile of v4, /device:TPU:10, one launch (start us, length us, event | category | flops | bytes accessed | tf_op | source)
XLA Modules:
  0.0 97.9 jit_solution(1141720227773887898)
XLA Ops:
  0.0 0.0 copy-start
  0.0 0.0 copy-start.1
  0.0 0.0 copy-start.3
  0.0 1.4 %copy.81 = bf16[2,1,4,2,128,128]{4,5,0,2,3,1:T(8,128)(2,1)S(1)} copy(bf16[2,1,4,2,128,128]{5,4,3,2,1,0:T(8,128)(2,1)} %param.8) | data formatting | bytes 1048576 | tf_op args[3]
  1.4 1.9 %collective-permute-start = (bf16[2,1,4,2,128,128]{4,5,0,2,3,1:T(8,128)(2,1)S(1)}, bf16[2,1,4,2,128,128]{4,5,0,2,3,1:T(8,128)(2,1)S(1)}, u32[]{:S(2)}, u32[]{:S(2)}) collective-permute-start(bf16[2,1,4,2,128,128]{4,5,0,2,3,1:T(8,128)(2,1)S(1)} %copy.81), channel_id=1, source_target_pairs={{0,32},{32,0},{64,96},{96,64},{128,160},{160,128},{192,224},{224,1... | collective-permute-start | bytes 1572872 | tf_op jit(solution)/shard_map/ppermute | solution.py:100
  3.3 14.6 %collective-permute-start.1 = (bf16[2,1,4,2,128,128]{4,5,0,2,3,1:T(8,128)(2,1)S(1)}, bf16[2,1,4,2,128,128]{4,5,0,2,3,1:T(8,128)(2,1)S(1)}, u32[]{:S(2)}, u32[]{:S(2)}) collective-permute-start(bf16[2,1,4,2,128,128]{4,5,0,2,3,1:T(8,128)(2,1)S(1)} %copy.81), channel_id=1, source_target_pairs={{32,64},{96,128},{160,192},{224,256},{288,320},{352,384},{416,448}... | collective-permute-start | bytes 1572872 | tf_op jit(solution)/shard_map/ppermute | solution.py:101
  18.1 0.0 copy-done.1
  18.1 0.7 slice_bitcast_fusion.12
  18.8 0.7 fusion.122
  19.5 0.0 copy-done.2
  19.5 0.0 copy-done.3
  19.5 0.7 slice_bitcast_fusion.10
  20.3 2.8 %fusion.6 = f32[4,256,2,128]{3,1,2,0:T(8,128)} fusion(bf16[2,1,4,128,128]{3,4,0,2,1:T(8,128)(2,1)S(1)} %get-tuple-element.14, bf16[2,1,4,128,128]{3,4,0,2,1:T(8,128)(2,1)S(1)} %fusion.125, bf16[2,1,4,128,128]{3,4,0,2,1:T(8,128)(2,1)S(1)} %get-tuple-element.13, bf16[1,4,128,128]{3,2,1,0:T(8,128)(2,1)} %get-tuple-element.20, ...), kind=kOutput, calls=%fused_computation.15 | convolution fusion | flops 275513344 | bytes 2228224 | tf_op jit(solution)/shard_map/fnepr,nesr->fneps/dot_general | solution.py:67
  23.2 0.0 collective-permute-done
  23.3 0.7 copy-done.4
  24.0 0.1 copy-done.5
  24.1 2.9 %convolution_add_fusion.1 = f32[4,256,2,128]{3,1,2,0:T(8,128)} fusion(f32[4,256,2,128]{3,1,2,0:T(8,128)} %fusion.6, bf16[2,1,4,128,128]{3,4,0,2,1:T(8,128)(2,1)S(1)} %get-tuple-element.12, bf16[2,1,4,128,128]{3,4,0,2,1:T(8,128)(2,1)S(1)} %fusion.126, bf16[2,1,4,128,128]{3,4,0,2,1:T(8,128)(2,1)S(1)} %get-tuple-element.11, ...), kind=kOutput, calls=%fused_computation.3 | convolution fusion | flops 275775488 | bytes 3276800 | tf_op jit(solution)/shard_map/fnepr,nesr->fneps/dot_general | solution.py:67
  26.9 14.8 %collective-permute-done.1 = bf16[2,1,4,2,128,128]{4,5,0,2,3,1:T(8,128)(2,1)S(1)} collective-permute-done((bf16[2,1,4,2,128,128]{4,5,0,2,3,1:T(8,128)(2,1)S(1)}, bf16[2,1,4,2,128,128]{4,5,0,2,3,1:T(8,128)(2,1)S(1)}, u32[]{:S(2)}, u32[]{:S(2)}) %collective-permute-start.1) | collective-permute-done | bytes 524320 | tf_op jit(solution)/shard_map/ppermute | solution.py:101
  41.8 1.9 %fusion.2 = bf16[2,1,4,128,256]{3,4,0,2,1:T(8,128)(2,1)S(1)} fusion(f32[4,256,2,128]{3,1,2,0:T(8,128)} %convolution_add_fusion.1, bf16[2,1,4,128,128]{3,4,0,2,1:T(8,128)(2,1)S(1)} %get-tuple-element.10, bf16[2,1,4,128,128]{3,4,0,2,1:T(8,128)(2,1)S(1)} %fusion.127, bf16[2,1,4,128,128]{3,4,0,2,1:T(8,128)(2,1)S(1)} %get-tuple-element.9, ...), kind=kOutput, calls=%fused_computation.11 | convolution fusion | flops 276037632 | bytes 2752512 | tf_op jit(solution)/shard_map/fnepr,nesr->fneps/dot_general | solution.py:67
  43.6 0.2 copy.92
  43.9 0.1 convert_element_type.126
  44.0 0.2 copy.116
  44.3 1.0 %reshape.271 = bf16[32,2,4,2,512]{4,2,3,1,0:T(4,128)(2,1)} reshape(bf16[32,2,4,2,1,4,128]{6,5,2,3,1,0,4:T(4,128)(2,1)S(1)} %copy.116) | data formatting | bytes 1048576 | tf_op jit(solution)/shard_map/reshape | solution.py:112
  45.3 10.5 %all-to-all-start = ((bf16[32,2,4,2,512]{4,2,3,1,0:T(4,128)(2,1)}), bf16[32,2,4,2,512]{4,2,3,1,0:T(4,128)(2,1)S(1)}, u32[]{:S(2)}, u32[]{:S(2)}) async-start(bf16[32,2,4,2,512]{4,2,3,1,0:T(4,128)(2,1)} %reshape.271), calls=%async_computation | async-start | bytes 1048576 | tf_op jit(solution)/shard_map/all_to_all | solution.py:120
  55.8 0.6 fusion.110
  56.4 0.2 copy.78
  56.6 0.1 concatenate.93
  56.7 0.1 copy.75
  56.9 0.5 fusion.106
  57.4 0.5 negate_convert_fusion.1
  57.9 0.2 copy.76
  58.1 0.2 copy.77
  58.4 0.3 fusion.72
  58.6 1.2 %pad_maximum_fusion = bf16[128,4,512]{2,1,0:T(4,128)(2,1)S(1)} fusion(bf16[128,1,512]{2,1,0:T(2,128)(2,1)S(1)} %fusion.72, bf16[128,1,512]{2,1,0:T(2,128)(2,1)S(1)} %copy.78, bf16[128,1,512]{2,1,0:T(2,128)(2,1)S(1)} %copy.77, bf16[128,1,512]{2,1,0:T(2,128)(2,1)S(1)} %copy.76), kind=kLoop, calls=%fused_computation.45 | loop fusion | flops 2097152 | bytes 1048576 | tf_op jit(solution)/shard_map/stack | solution.py:145
  59.9 0.1 convert_element_type.112
  60.0 0.6 cosine_convert_fusion
  60.6 11.1 %all-to-all-done = bf16[32,2,4,2,512]{4,2,3,1,0:T(4,128)(2,1)S(1)} async-done(((bf16[32,2,4,2,512]{4,2,3,1,0:T(4,128)(2,1)}), bf16[32,2,4,2,512]{4,2,3,1,0:T(4,128)(2,1)S(1)}, u32[]{:S(2)}, u32[]{:S(2)}) %all-to-all-start) | async-done | bytes 524320 | tf_op jit(solution)/shard_map/all_to_all | solution.py:120
  71.7 0.8 convolution_bitcast_fusion
  72.5 0.2 fusion.11
  72.7 0.2 fusion.9
  72.9 0.3 fusion.70
  73.2 0.4 fusion.1
  73.7 0.2 reshape.257
  73.9 22.1 %all_to_all.10 = bf16[32,4,2,2,512]{4,3,2,1,0:T(2,128)(2,1)S(1)} all-to-all(bf16[32,4,2,2,512]{4,3,2,1,0:T(2,128)(2,1)S(1)} %reshape.257), channel_id=1, replica_groups=mesh['space'=24,'energy'=32] {'energy'}, dimensions={0} | all-to-all | bytes 1048576 | tf_op jit(solution)/shard_map/all_to_all | solution.py:154
  95.9 0.3 reshape.272
  96.3 0.2 copy.117
  96.5 0.0 copy-done
  96.5 1.4 %fusion.4 = bf16[2,1,4,2,128,128]{5,4,3,2,1,0:T(8,128)(2,1)} fusion(bf16[2,4,2,128,128]{4,3,2,1,0:T(8,128)(2,1)S(1)} %bitcast.192, bf16[1,128,128]{2,1,0:T(8,128)(2,1)S(1)} %copy-done), kind=kOutput, calls=%fused_computation.13 | convolution fusion | flops 134742016 | bytes 1081344 | tf_op jit(solution)/shard_map/fetnpr,nsr->fnetps/dot_general | solution.py:161
  (16 shorter events, 0.4 us)
Async XLA Ops:
  0.0 96.5 %copy-start = (bf16[1,128,128]{2,1,0:T(8,128)(2,1)S(1)}, bf16[1,128,128]{2,1,0:T(8,128)(2,1)}, u32[]{:S(2)}) copy-start(bf16[1,128,128]{2,1,0:T(8,128)(2,1)} %param.9) | copy-start | bytes 98308
  0.0 18.1 %copy-start.1 = (bf16[1,4,2,128,128]{4,3,2,1,0:T(8,128)(2,1)S(1)}, bf16[1,4,2,128,128]{4,3,2,1,0:T(8,128)(2,1)}, u32[]{:S(2)}) copy-start(bf16[1,4,2,128,128]{4,3,2,1,0:T(8,128)(2,1)} %param.6) | copy-start | bytes 786436
  0.0 19.5 %copy-start.2 = (bf16[1,4,2,128,128]{4,3,2,1,0:T(8,128)(2,1)S(1)}, bf16[1,4,2,128,128]{4,3,2,1,0:T(8,128)(2,1)}, u32[]{:S(2)}) copy-start(bf16[1,4,2,128,128]{4,3,2,1,0:T(8,128)(2,1)} %param.5) | copy-start | bytes 786436
  0.0 19.5 %copy-start.3 = (bf16[1,4,2,128,128]{4,3,2,1,0:T(8,128)(2,1)S(1)}, bf16[1,4,2,128,128]{4,3,2,1,0:T(8,128)(2,1)}, u32[]{:S(2)}) copy-start(bf16[1,4,2,128,128]{4,3,2,1,0:T(8,128)(2,1)} %param.7) | copy-start | bytes 786436
  1.4 21.8 %collective-permute-start = (bf16[2,1,4,2,128,128]{4,5,0,2,3,1:T(8,128)(2,1)S(1)}, bf16[2,1,4,2,128,128]{4,5,0,2,3,1:T(8,128)(2,1)S(1)}, u32[]{:S(2)}, u32[]{:S(2)}) collective-permute-start(bf16[2,1,4,2,128,128]{4,5,0,2,3,1:T(8,128)(2,1)S(1)} %copy.81), channel_id=1, source_target_pairs={{0,32},{32,0},{64,96},{96,64},{128,160},{160,128},{192,224},{224,1... | collective-permute-start | bytes 1572872 | tf_op jit(solution)/shard_map/ppermute | solution.py:100
  3.3 38.3 %collective-permute-start.1 = (bf16[2,1,4,2,128,128]{4,5,0,2,3,1:T(8,128)(2,1)S(1)}, bf16[2,1,4,2,128,128]{4,5,0,2,3,1:T(8,128)(2,1)S(1)}, u32[]{:S(2)}, u32[]{:S(2)}) collective-permute-start(bf16[2,1,4,2,128,128]{4,5,0,2,3,1:T(8,128)(2,1)S(1)} %copy.81), channel_id=1, source_target_pairs={{32,64},{96,128},{160,192},{224,256},{288,320},{352,384},{416,448}... | collective-permute-start | bytes 1572872 | tf_op jit(solution)/shard_map/ppermute | solution.py:101
  23.1 0.9 copy-start.4
  23.1 1.0 copy-start.5
  45.3 26.5 %all-to-all-start = ((bf16[32,2,4,2,512]{4,2,3,1,0:T(4,128)(2,1)}), bf16[32,2,4,2,512]{4,2,3,1,0:T(4,128)(2,1)S(1)}, u32[]{:S(2)}, u32[]{:S(2)}) async-start(bf16[32,2,4,2,512]{4,2,3,1,0:T(4,128)(2,1)} %reshape.271), calls=%async_computation | async-start | bytes 1048576 | tf_op jit(solution)/shard_map/all_to_all | solution.py:120

commit v5 on v4

--- a/solution.py
+++ b/solution.py
@@ -97,15 +97,17 @@
     on_chip = [(i, i ^ 1) for i in range(peers - peers % 2)]
     across = [(i, i + 1) for i in range(1, peers - 1, 2)]
     across = across + [(j, i) for i, j in across]
-    partner = lax.ppermute(self_energy, "space", on_chip)
     neighbour = lax.ppermute(self_energy, "space", across)
+    diag_term = congruence(green_diag, self_energy)
+    own_energy, diag_term = lax.optimization_barrier((self_energy, diag_term))
+    partner = lax.ppermute(own_energy, "space", on_chip)
     even = lax.axis_index("space") % 2 == 0
     green_on = jnp.where(even, green_upper, green_lower)
     green_across = jnp.where(even, green_lower, green_upper)
-    diag_term = congruence(green_diag, self_energy)
-    on_term = congruence(green_on, partner)
+    near_sum = diag_term + congruence(green_on, partner)
+    near_sum, neighbour = lax.optimization_barrier((near_sum, neighbour))
     across_term = congruence(green_across, neighbour)
-    total = diag_term + on_term + across_term
+    total = near_sum + across_term
     groups = lax.axis_size("energy")
     total = total.reshape(2, block_count, energy_local, groups, block_order // groups, 2, block_order)
     outgoing = jnp.transpose(total, (3, 0, 2, 5, 1, 4, 6)).astype(jnp.bfloat16)

time: 98.3 us -> 97.1 us (0.988)
  the two profiles are of different devices: /device:TPU:10 before, /device:TPU:14 now
where the time goes in v5:
time: 97.1 us; the launch traced here: 96.7 us
  waiting for transfers between devices  26.7 us (27%)
  starting transfers between devices  26.6 us (27%)
  blocking collectives  22.1 us (23%)
  matrix products  9.08 us (9%)
  local copies, waits for them, and re-layouts  6.51 us (7%)
  other arithmetic  5.44 us (6%)
    all_to_all x1, blocking collectives, body(): returned = lax.all_to_all(polar, 'energy', 0, 0, tiled=True)  22.1 us
    ppermute x1, starting transfers between devices, body(): neighbour = lax.ppermute(self_energy, 'space', across)  14.3 us
    ppermute x1, waiting for transfers between devices, body(): neighbour = lax.ppermute(self_energy, 'space', across)  14.1 us
    all_to_all x1, waiting for transfers between devices, body(): entries = lax.all_to_all(outgoing, 'energy', 0, 0, tiled=True)  12.2 us
    all_to_all x1, starting transfers between devices, body(): entries = lax.all_to_all(outgoing, 'energy', 0, 0, tiled=True)  10.4 us
    dot_general x3, matrix products, congruence(): jnp.einsum('fnepr,nesr->fneps', mixed, adjoint_tall, preferred_element_ty...  6.45 us
    another operation x5, other arithmetic  2.52 us
  transfers between devices with their start and end apart: 3, of which 3 were waited for; matrix products, arithmetic and copies ran while one was open for 12% of the time, Pallas kernels for 0%

profile of v5, /device:TPU:14, one launch (start us, length us, event | category | flops | bytes accessed | tf_op | source)
XLA Modules:
  0.0 96.7 jit_solution(17581558367516084770)
XLA Ops:
  0.0 0.0 copy-start
  0.0 1.4 %copy.81 = bf16[2,1,4,2,128,128]{4,5,0,2,3,1:T(8,128)(2,1)S(1)} copy(bf16[2,1,4,2,128,128]{5,4,3,2,1,0:T(8,128)(2,1)} %param.8) | data formatting | bytes 1048576 | tf_op args[3]
  1.4 14.3 %collective-permute-start.1 = (bf16[2,1,4,2,128,128]{4,5,0,2,3,1:T(8,128)(2,1)S(1)}, bf16[2,1,4,2,128,128]{4,5,0,2,3,1:T(8,128)(2,1)S(1)}, u32[]{:S(2)}, u32[]{:S(2)}) collective-permute-start(bf16[2,1,4,2,128,128]{4,5,0,2,3,1:T(8,128)(2,1)S(1)} %copy.81), channel_id=1, source_target_pairs={{32,64},{96,128},{160,192},{224,256},{288,320},{352,384},{416,448}... | collective-permute-start | bytes 1572872 | tf_op jit(solution)/shard_map/ppermute | solution.py:100
  15.7 0.0 copy-done.2
  15.7 0.7 slice_bitcast_fusion.12
  16.4 0.0 copy-start.1
  16.4 0.0 copy-start.3
  16.5 0.0 copy-start.4
  16.5 2.7 %convolution_bitcast_fusion.3 = f32[2,1,4,128,256]{3,4,0,2,1:T(8,128)} fusion(bf16[2,1,4,128,128]{3,4,0,2,1:T(8,128)(2,1)S(1)} %get-tuple-element.22, bf16[2,1,4,128,128]{3,4,0,2,1:T(8,128)(2,1)S(1)} %fusion.124, bf16[2,1,4,128,128]{3,4,0,2,1:T(8,128)(2,1)S(1)} %get-tuple-element.21, bf16[1,4,128,128]{3,2,1,0:T(8,128)(2,1)} %get-tuple-element.28, ...), kind=kOutput, calls=%fused_computation.4 | convolution fusion | flops 275513344 | bytes 2228224 | tf_op jit(solution)/shard_map/fnepr,nesr->fneps/dot_general | solution.py:67
  19.2 0.3 copy.86
  19.5 1.9 %collective-permute-start = (bf16[2,1,4,2,128,128]{4,5,0,2,3,1:T(8,128)(2,1)S(1)}, bf16[2,1,4,2,128,128]{4,5,0,2,3,1:T(8,128)(2,1)S(1)}, u32[]{:S(2)}, u32[]{:S(2)}) collective-permute-start(bf16[2,1,4,2,128,128]{4,5,0,2,3,1:T(8,128)(2,1)S(1)} %copy.86), channel_id=1, source_target_pairs={{0,32},{32,0},{64,96},{96,64},{128,160},{160,128},{192,224},{224,1... | collective-permute-start | bytes 1572872 | tf_op jit(solution)/shard_map/ppermute | solution.py:103
  21.5 0.0 copy-done.3
  21.5 0.0 copy-done.4
  21.5 0.7 fusion.122
  22.2 0.7 slice_bitcast_fusion.8
  23.0 0.4 collective-permute-done
  23.4 1.9 %fusion = f32[2,1,4,128,256]{3,4,0,2,1:T(8,128)S(1)} fusion(f32[2,1,4,128,256]{3,4,0,2,1:T(8,128)} %convolution_bitcast_fusion.3, bf16[2,1,4,128,128]{3,4,0,2,1:T(8,128)(2,1)S(1)} %get-tuple-element.20, bf16[2,1,4,128,128]{3,4,0,2,1:T(8,128)(2,1)S(1)} %fusion.125, bf16[2,1,4,128,128]{3,4,0,2,1:T(8,128)(2,1)S(1)} %get-tuple-element.19, ...), kind=kOutput, calls=%fused_computation.5 | convolution fusion | flops 275775488 | bytes 3276800 | tf_op jit(solution)/shard_map/fnepr,nesr->fneps/dot_general | solution.py:67
  25.3 14.1 %collective-permute-done.1 = bf16[2,1,4,2,128,128]{4,5,0,2,3,1:T(8,128)(2,1)S(1)} collective-permute-done((bf16[2,1,4,2,128,128]{4,5,0,2,3,1:T(8,128)(2,1)S(1)}, bf16[2,1,4,2,128,128]{4,5,0,2,3,1:T(8,128)(2,1)S(1)}, u32[]{:S(2)}, u32[]{:S(2)}) %collective-permute-start.1) | collective-permute-done | bytes 524320 | tf_op jit(solution)/shard_map/ppermute | solution.py:100
  39.4 1.8 %convolution_bitcast_fusion.1 = f32[2,1,4,128,256]{3,4,0,2,1:T(8,128)S(1)} fusion(bf16[2,1,4,128,128]{3,4,0,2,1:T(8,128)(2,1)S(1)} %get-tuple-element.18, bf16[2,1,4,128,128]{3,4,0,2,1:T(8,128)(2,1)S(1)} %fusion.123, bf16[2,1,4,128,128]{3,4,0,2,1:T(8,128)(2,1)S(1)} %get-tuple-element.17, bf16[1,4,128,128]{3,2,1,0:T(8,128)(2,1)} %get-tuple-element.24, ...), kind=kOutput, calls=%fused_computation.2 | convolution fusion | flops 275513344 | bytes 2228224 | tf_op jit(solution)/shard_map/fnepr,nesr->fneps/dot_general | solution.py:67
  41.3 0.1 add_convert_fusion
  41.4 0.2 copy.92
  41.6 0.1 convert_element_type.118
  41.8 0.2 copy.116
  42.0 1.0 %reshape.268 = bf16[32,2,4,2,512]{4,2,3,1,0:T(4,128)(2,1)} reshape(bf16[32,2,4,2,1,4,128]{6,5,2,3,1,0,4:T(4,128)(2,1)S(1)} %copy.116) | data formatting | bytes 1048576 | tf_op jit(solution)/shard_map/reshape | solution.py:114
  43.0 10.4 %all-to-all-start = ((bf16[32,2,4,2,512]{4,2,3,1,0:T(4,128)(2,1)}), bf16[32,2,4,2,512]{4,2,3,1,0:T(4,128)(2,1)S(1)}, u32[]{:S(2)}, u32[]{:S(2)}) async-start(bf16[32,2,4,2,512]{4,2,3,1,0:T(4,128)(2,1)} %reshape.268), calls=%async_computation | async-start | bytes 1048576 | tf_op jit(solution)/shard_map/all_to_all | solution.py:122
  53.4 0.6 fusion.108
  54.1 0.2 copy.78
  54.3 0.1 concatenate.93
  54.4 0.1 copy.75
  54.5 0.5 fusion.104
  55.0 0.5 negate_convert_fusion.1
  55.6 0.2 copy.76
  55.8 0.2 copy.77
  56.0 0.3 fusion.70
  56.3 1.2 %pad_maximum_fusion = bf16[128,4,512]{2,1,0:T(4,128)(2,1)S(1)} fusion(bf16[128,1,512]{2,1,0:T(2,128)(2,1)S(1)} %fusion.70, bf16[128,1,512]{2,1,0:T(2,128)(2,1)S(1)} %copy.78, bf16[128,1,512]{2,1,0:T(2,128)(2,1)S(1)} %copy.77, bf16[128,1,512]{2,1,0:T(2,128)(2,1)S(1)} %copy.76), kind=kLoop, calls=%fused_computation.45 | loop fusion | flops 2097152 | bytes 1048576 | tf_op jit(solution)/shard_map/stack | solution.py:147
  57.5 0.1 convert_element_type.106
  57.7 0.6 cosine_convert_fusion
  58.3 12.2 %all-to-all-done = bf16[32,2,4,2,512]{4,2,3,1,0:T(4,128)(2,1)S(1)} async-done(((bf16[32,2,4,2,512]{4,2,3,1,0:T(4,128)(2,1)}), bf16[32,2,4,2,512]{4,2,3,1,0:T(4,128)(2,1)S(1)}, u32[]{:S(2)}, u32[]{:S(2)}) %all-to-all-start) | async-done | bytes 524320 | tf_op jit(solution)/shard_map/all_to_all | solution.py:122
  70.5 0.8 convolution_bitcast_fusion
  71.3 0.2 fusion.7
  71.5 0.2 fusion.9
  71.7 0.3 fusion.68
  72.0 0.4 fusion.1
  72.4 0.2 reshape.254
  72.6 22.1 %all_to_all.10 = bf16[32,4,2,2,512]{4,3,2,1,0:T(2,128)(2,1)S(1)} all-to-all(bf16[32,4,2,2,512]{4,3,2,1,0:T(2,128)(2,1)S(1)} %reshape.254), channel_id=1, replica_groups=mesh['space'=24,'energy'=32] {'energy'}, dimensions={0} | all-to-all | bytes 1048576 | tf_op jit(solution)/shard_map/all_to_all | solution.py:156
  94.7 0.3 reshape.269
  95.0 0.2 copy.117
  95.3 1.4 %fusion.3 = bf16[2,1,4,2,128,128]{5,4,3,2,1,0:T(8,128)(2,1)} fusion(bf16[2,4,2,128,128]{4,3,2,1,0:T(8,128)(2,1)S(1)} %bitcast.202, bf16[1,128,128]{2,1,0:T(8,128)(2,1)S(1)} %copy-done), kind=kOutput, calls=%fused_computation.13 | convolution fusion | flops 134742016 | bytes 1081344 | tf_op jit(solution)/shard_map/fetnpr,nsr->fnetps/dot_general | solution.py:163
  (17 shorter events, 0.4 us)
Async XLA Ops:
  0.0 95.3 %copy-start = (bf16[1,128,128]{2,1,0:T(8,128)(2,1)S(1)}, bf16[1,128,128]{2,1,0:T(8,128)(2,1)}, u32[]{:S(2)}) copy-start(bf16[1,128,128]{2,1,0:T(8,128)(2,1)} %param.9) | copy-start | bytes 98308
  0.0 15.7 %copy-start.2 = (bf16[1,4,2,128,128]{4,3,2,1,0:T(8,128)(2,1)S(1)}, bf16[1,4,2,128,128]{4,3,2,1,0:T(8,128)(2,1)}, u32[]{:S(2)}) copy-start(bf16[1,4,2,128,128]{4,3,2,1,0:T(8,128)(2,1)} %param.6) | copy-start | bytes 786436
  1.4 38.0 %collective-permute-start.1 = (bf16[2,1,4,2,128,128]{4,5,0,2,3,1:T(8,128)(2,1)S(1)}, bf16[2,1,4,2,128,128]{4,5,0,2,3,1:T(8,128)(2,1)S(1)}, u32[]{:S(2)}, u32[]{:S(2)}) collective-permute-start(bf16[2,1,4,2,128,128]{4,5,0,2,3,1:T(8,128)(2,1)S(1)} %copy.81), channel_id=1, source_target_pairs={{32,64},{96,128},{160,192},{224,256},{288,320},{352,384},{416,448}... | collective-permute-start | bytes 1572872 | tf_op jit(solution)/shard_map/ppermute | solution.py:100
  16.4 2.8 %copy-start.1 = (bf16[2,1,4,2,128,128]{5,4,3,2,1,0:T(8,128)(2,1)S(1)}, bf16[2,1,4,2,128,128]{5,4,3,2,1,0:T(8,128)(2,1)}, u32[]{:S(2)}) copy-start(bf16[2,1,4,2,128,128]{5,4,3,2,1,0:T(8,128)(2,1)} %param.8) | copy-start | bytes 1572868
  16.4 5.0 %copy-start.3 = (bf16[1,4,2,128,128]{4,3,2,1,0:T(8,128)(2,1)S(1)}, bf16[1,4,2,128,128]{4,3,2,1,0:T(8,128)(2,1)}, u32[]{:S(2)}) copy-start(bf16[1,4,2,128,128]{4,3,2,1,0:T(8,128)(2,1)} %param.5) | copy-start | bytes 786436
  16.5 5.0 %copy-start.4 = (bf16[1,4,2,128,128]{4,3,2,1,0:T(8,128)(2,1)S(1)}, bf16[1,4,2,128,128]{4,3,2,1,0:T(8,128)(2,1)}, u32[]{:S(2)}) copy-start(bf16[1,4,2,128,128]{4,3,2,1,0:T(8,128)(2,1)} %param.7) | copy-start | bytes 786436
  19.5 3.8 %collective-permute-start = (bf16[2,1,4,2,128,128]{4,5,0,2,3,1:T(8,128)(2,1)S(1)}, bf16[2,1,4,2,128,128]{4,5,0,2,3,1:T(8,128)(2,1)S(1)}, u32[]{:S(2)}, u32[]{:S(2)}) collective-permute-start(bf16[2,1,4,2,128,128]{4,5,0,2,3,1:T(8,128)(2,1)S(1)} %copy.86), channel_id=1, source_target_pairs={{0,32},{32,0},{64,96},{96,64},{128,160},{160,128},{192,224},{224,1... | collective-permute-start | bytes 1572872 | tf_op jit(solution)/shard_map/ppermute | solution.py:103
  43.0 27.5 %all-to-all-start = ((bf16[32,2,4,2,512]{4,2,3,1,0:T(4,128)(2,1)}), bf16[32,2,4,2,512]{4,2,3,1,0:T(4,128)(2,1)S(1)}, u32[]{:S(2)}, u32[]{:S(2)}) async-start(bf16[32,2,4,2,512]{4,2,3,1,0:T(4,128)(2,1)} %reshape.268), calls=%async_computation | async-start | bytes 1048576 | tf_op jit(solution)/shard_map/all_to_all | solution.py:122

commit v6 on v5

--- a/solution.py
+++ b/solution.py
@@ -118,18 +118,23 @@
     forward_angle = (frequency[:, None] * energy_index[None, :] % padded_len).astype(
         jnp.float32
     ) * step_angle
-    forward_table = jnp.concatenate([jnp.cos(forward_angle), jnp.sin(forward_angle)], axis=0)
+    cos_table, sin_table = jnp.cos(forward_angle), jnp.sin(forward_angle)
+    forward_table = jnp.concatenate(
+        [
+            jnp.stack([cos_table, sin_table], axis=-1),
+            jnp.stack([-sin_table, cos_table], axis=-1),
+        ],
+        axis=0,
+    ).astype(jnp.bfloat16)
     entries = lax.all_to_all(outgoing, "energy", 0, 0, tiled=True)
     spectra = jnp.einsum(
-        "qxe,xfern->qfrn",
-        forward_table.astype(jnp.bfloat16).reshape(2 * padded_len, groups, energy_local),
+        "qxer,xfern->qfn",
+        forward_table.reshape(2 * padded_len, groups, energy_local, 2),
         entries,
         preferred_element_type=jnp.float32,
     )
-    cos_part = spectra[:padded_len]
-    sin_part = spectra[padded_len:]
-    spec_real = cos_part[:, :, 0] + sin_part[:, :, 1]
-    spec_imag = cos_part[:, :, 1] - sin_part[:, :, 0]
+    spec_real = spectra[:padded_len]
+    spec_imag = spectra[padded_len:]
     product_real = spec_real[:, 0] * spec_real[:, 1] + spec_imag[:, 0] * spec_imag[:, 1]
     product_imag = spec_imag[:, 0] * spec_real[:, 1] - spec_real[:, 0] * spec_imag[:, 1]
     stacked_product = jnp.concatenate([product_real, product_imag], axis=0)

time: 97.1 us -> 96.5 us (level)
  no operation moved by 1% of the time
where the time goes in v6:
time: 96.5 us; the launch traced here: 96.1 us
  waiting for transfers between devices  26.7 us (28%)
  starting transfers between devices  26.6 us (28%)
  blocking collectives  22.1 us (23%)
  matrix products  8.9 us (9%)
  local copies, waits for them, and re-layouts  6.53 us (7%)
  other arithmetic  5.02 us (5%)
    all_to_all x1, blocking collectives, body(): returned = lax.all_to_all(polar, 'energy', 0, 0, tiled=True)  22.1 us
    ppermute x1, starting transfers between devices, body(): neighbour = lax.ppermute(self_energy, 'space', across)  14.3 us
    ppermute x1, waiting for transfers between devices, body(): neighbour = lax.ppermute(self_energy, 'space', across)  14.1 us
    all_to_all x1, waiting for transfers between devices, body(): entries = lax.all_to_all(outgoing, 'energy', 0, 0, tiled=True)  12.2 us
    all_to_all x1, starting transfers between devices, body(): entries = lax.all_to_all(outgoing, 'energy', 0, 0, tiled=True)  10.4 us
    dot_general x3, matrix products, congruence(): jnp.einsum('fnepr,nesr->fneps', mixed, adjoint_tall, preferred_element_ty...  6.45 us
    another operation x5, other arithmetic  2.53 us
  transfers between devices with their start and end apart: 3, of which 3 were waited for; matrix products, arithmetic and copies ran while one was open for 12% of the time, Pallas kernels for 0%

profile of v6, /device:TPU:14, one launch (start us, length us, event | category | flops | bytes accessed | tf_op | source)
XLA Modules:
  0.0 96.1 jit_solution(4393623171719519848)
XLA Ops:
  0.0 0.0 copy-start
  0.0 1.4 %copy.75 = bf16[2,1,4,2,128,128]{4,5,0,2,3,1:T(8,128)(2,1)S(1)} copy(bf16[2,1,4,2,128,128]{5,4,3,2,1,0:T(8,128)(2,1)} %param.8) | data formatting | bytes 1048576 | tf_op args[3]
  1.4 14.3 %collective-permute-start.1 = (bf16[2,1,4,2,128,128]{4,5,0,2,3,1:T(8,128)(2,1)S(1)}, bf16[2,1,4,2,128,128]{4,5,0,2,3,1:T(8,128)(2,1)S(1)}, u32[]{:S(2)}, u32[]{:S(2)}) collective-permute-start(bf16[2,1,4,2,128,128]{4,5,0,2,3,1:T(8,128)(2,1)S(1)} %copy.75), channel_id=1, source_target_pairs={{32,64},{96,128},{160,192},{224,256},{288,320},{352,384},{416,448}... | collective-permute-start | bytes 1572872 | tf_op jit(solution)/shard_map/ppermute | solution.py:100
  15.7 0.0 copy-done.2
  15.7 0.7 slice_bitcast_fusion.10
  16.4 0.0 copy-start.1
  16.4 0.0 copy-start.3
  16.5 0.0 copy-start.4
  16.5 2.7 %convolution_bitcast_fusion.3 = f32[2,1,4,128,256]{3,4,0,2,1:T(8,128)} fusion(bf16[2,1,4,128,128]{3,4,0,2,1:T(8,128)(2,1)S(1)} %get-tuple-element.22, bf16[2,1,4,128,128]{3,4,0,2,1:T(8,128)(2,1)S(1)} %fusion.127, bf16[2,1,4,128,128]{3,4,0,2,1:T(8,128)(2,1)S(1)} %get-tuple-element.21, bf16[1,4,128,128]{3,2,1,0:T(8,128)(2,1)} %get-tuple-element.28, ...), kind=kOutput, calls=%fused_computation.4 | convolution fusion | flops 275513344 | bytes 2228224 | tf_op jit(solution)/shard_map/fnepr,nesr->fneps/dot_general | solution.py:67
  19.2 0.0 copy-done.1
  19.2 0.3 copy.80
  19.5 1.9 %collective-permute-start = (bf16[2,1,4,2,128,128]{4,5,0,2,3,1:T(8,128)(2,1)S(1)}, bf16[2,1,4,2,128,128]{4,5,0,2,3,1:T(8,128)(2,1)S(1)}, u32[]{:S(2)}, u32[]{:S(2)}) collective-permute-start(bf16[2,1,4,2,128,128]{4,5,0,2,3,1:T(8,128)(2,1)S(1)} %copy.80), channel_id=1, source_target_pairs={{0,32},{32,0},{64,96},{96,64},{128,160},{160,128},{192,224},{224,1... | collective-permute-start | bytes 1572872 | tf_op jit(solution)/shard_map/ppermute | solution.py:103
  21.5 0.0 copy-done.3
  21.5 0.0 copy-done.4
  21.5 0.7 fusion.125
  22.2 0.7 slice_bitcast_fusion.6
  23.0 0.4 collective-permute-done
  23.4 1.9 %fusion = f32[2,1,4,128,256]{3,4,0,2,1:T(8,128)S(1)} fusion(f32[2,1,4,128,256]{3,4,0,2,1:T(8,128)} %convolution_bitcast_fusion.3, bf16[2,1,4,128,128]{3,4,0,2,1:T(8,128)(2,1)S(1)} %get-tuple-element.20, bf16[2,1,4,128,128]{3,4,0,2,1:T(8,128)(2,1)S(1)} %fusion.128, bf16[2,1,4,128,128]{3,4,0,2,1:T(8,128)(2,1)S(1)} %get-tuple-element.19, ...), kind=kOutput, calls=%fused_computation.5 | convolution fusion | flops 275775488 | bytes 3276800 | tf_op jit(solution)/shard_map/fnepr,nesr->fneps/dot_general | solution.py:67
  25.3 14.1 %collective-permute-done.1 = bf16[2,1,4,2,128,128]{4,5,0,2,3,1:T(8,128)(2,1)S(1)} collective-permute-done((bf16[2,1,4,2,128,128]{4,5,0,2,3,1:T(8,128)(2,1)S(1)}, bf16[2,1,4,2,128,128]{4,5,0,2,3,1:T(8,128)(2,1)S(1)}, u32[]{:S(2)}, u32[]{:S(2)}) %collective-permute-start.1) | collective-permute-done | bytes 524320 | tf_op jit(solution)/shard_map/ppermute | solution.py:100
  39.4 1.8 %convolution_bitcast_fusion.1 = f32[2,1,4,128,256]{3,4,0,2,1:T(8,128)S(1)} fusion(bf16[2,1,4,128,128]{3,4,0,2,1:T(8,128)(2,1)S(1)} %get-tuple-element.18, bf16[2,1,4,128,128]{3,4,0,2,1:T(8,128)(2,1)S(1)} %fusion.126, bf16[2,1,4,128,128]{3,4,0,2,1:T(8,128)(2,1)S(1)} %get-tuple-element.17, bf16[1,4,128,128]{3,2,1,0:T(8,128)(2,1)} %get-tuple-element.24, ...), kind=kOutput, calls=%fused_computation.2 | convolution fusion | flops 275513344 | bytes 2228224 | tf_op jit(solution)/shard_map/fnepr,nesr->fneps/dot_general | solution.py:67
  41.3 0.1 add_convert_fusion
  41.4 0.2 copy.86
  41.6 0.1 convert_element_type.138
  41.8 0.3 copy.108
  42.0 1.0 %reshape.338 = bf16[32,2,4,2,512]{4,3,2,1,0:T(2,128)(2,1)} reshape(bf16[32,2,4,2,1,4,128]{6,5,3,2,1,0,4:T(4,128)(2,1)S(1)} %copy.108) | data formatting | bytes 1048576 | tf_op jit(solution)/shard_map/reshape | solution.py:114
  43.0 10.4 %all-to-all-start = ((bf16[32,2,4,2,512]{4,3,2,1,0:T(2,128)(2,1)}), bf16[32,2,4,2,512]{4,3,2,1,0:T(2,128)(2,1)S(1)}, u32[]{:S(2)}, u32[]{:S(2)}) async-start(bf16[32,2,4,2,512]{4,3,2,1,0:T(2,128)(2,1)} %reshape.338), calls=%async_computation | async-start | bytes 1048576 | tf_op jit(solution)/shard_map/all_to_all | solution.py:129
  53.5 0.6 fusion.111
  54.1 0.2 copy.72
  54.3 0.1 concatenate.97
  54.4 0.1 copy.69
  54.5 0.5 fusion.107
  55.0 0.5 negate_convert_fusion.2
  55.6 0.2 copy.70
  55.8 0.2 copy.71
  56.0 0.3 fusion.67
  56.3 1.2 %pad_maximum_fusion = bf16[128,4,512]{2,1,0:T(4,128)(2,1)S(1)} fusion(bf16[128,1,512]{2,1,0:T(2,128)(2,1)S(1)} %fusion.67, bf16[128,1,512]{2,1,0:T(2,128)(2,1)S(1)} %copy.72, bf16[128,1,512]{2,1,0:T(2,128)(2,1)S(1)} %copy.71, bf16[128,1,512]{2,1,0:T(2,128)(2,1)S(1)} %copy.70), kind=kLoop, calls=%fused_computation.39 | loop fusion | flops 2097152 | bytes 1048576 | tf_op jit(solution)/shard_map/stack | solution.py:152
  57.5 0.1 convert_element_type.126
  57.7 0.6 fusion.105
  58.3 12.2 %all-to-all-done = bf16[32,2,4,2,512]{4,3,2,1,0:T(2,128)(2,1)S(1)} async-done(((bf16[32,2,4,2,512]{4,3,2,1,0:T(2,128)(2,1)}), bf16[32,2,4,2,512]{4,3,2,1,0:T(2,128)(2,1)S(1)}, u32[]{:S(2)}, u32[]{:S(2)}) %all-to-all-start) | async-done | bytes 524320 | tf_op jit(solution)/shard_map/all_to_all | solution.py:129
  70.5 0.6 convolution_bitcast_fusion
  71.1 0.3 fusion.65
  71.4 0.4 fusion.1
  71.8 0.2 reshape.324
  72.1 22.1 %all_to_all.10 = bf16[32,4,2,2,512]{4,3,2,1,0:T(2,128)(2,1)S(1)} all-to-all(bf16[32,4,2,2,512]{4,3,2,1,0:T(2,128)(2,1)S(1)} %reshape.324), channel_id=1, replica_groups=mesh['space'=24,'energy'=32] {'energy'}, dimensions={0} | all-to-all | bytes 1048576 | tf_op jit(solution)/shard_map/all_to_all | solution.py:161
  94.1 0.3 reshape.339
  94.5 0.2 copy.109
  94.7 0.0 copy-done
  94.7 1.4 %fusion.3 = bf16[2,1,4,2,128,128]{5,4,3,2,1,0:T(8,128)(2,1)} fusion(bf16[2,4,2,128,128]{4,3,2,1,0:T(8,128)(2,1)S(1)} %bitcast.189, bf16[1,128,128]{2,1,0:T(8,128)(2,1)S(1)} %copy-done), kind=kOutput, calls=%fused_computation.13 | convolution fusion | flops 134742016 | bytes 1081344 | tf_op jit(solution)/shard_map/fetnpr,nsr->fnetps/dot_general | solution.py:168
  (15 shorter events, 0.4 us)
Async XLA Ops:
  0.0 94.7 %copy-start = (bf16[1,128,128]{2,1,0:T(8,128)(2,1)S(1)}, bf16[1,128,128]{2,1,0:T(8,128)(2,1)}, u32[]{:S(2)}) copy-start(bf16[1,128,128]{2,1,0:T(8,128)(2,1)} %param.9) | copy-start | bytes 98308
  0.0 15.7 %copy-start.2 = (bf16[1,4,2,128,128]{4,3,2,1,0:T(8,128)(2,1)S(1)}, bf16[1,4,2,128,128]{4,3,2,1,0:T(8,128)(2,1)}, u32[]{:S(2)}) copy-start(bf16[1,4,2,128,128]{4,3,2,1,0:T(8,128)(2,1)} %param.6) | copy-start | bytes 786436
  1.4 38.0 %collective-permute-start.1 = (bf16[2,1,4,2,128,128]{4,5,0,2,3,1:T(8,128)(2,1)S(1)}, bf16[2,1,4,2,128,128]{4,5,0,2,3,1:T(8,128)(2,1)S(1)}, u32[]{:S(2)}, u32[]{:S(2)}) collective-permute-start(bf16[2,1,4,2,128,128]{4,5,0,2,3,1:T(8,128)(2,1)S(1)} %copy.75), channel_id=1, source_target_pairs={{32,64},{96,128},{160,192},{224,256},{288,320},{352,384},{416,448}... | collective-permute-start | bytes 1572872 | tf_op jit(solution)/shard_map/ppermute | solution.py:100
  16.4 2.8 %copy-start.1 = (bf16[2,1,4,2,128,128]{5,4,3,2,1,0:T(8,128)(2,1)S(1)}, bf16[2,1,4,2,128,128]{5,4,3,2,1,0:T(8,128)(2,1)}, u32[]{:S(2)}) copy-start(bf16[2,1,4,2,128,128]{5,4,3,2,1,0:T(8,128)(2,1)} %param.8) | copy-start | bytes 1572868
  16.4 5.0 %copy-start.3 = (bf16[1,4,2,128,128]{4,3,2,1,0:T(8,128)(2,1)S(1)}, bf16[1,4,2,128,128]{4,3,2,1,0:T(8,128)(2,1)}, u32[]{:S(2)}) copy-start(bf16[1,4,2,128,128]{4,3,2,1,0:T(8,128)(2,1)} %param.5) | copy-start | bytes 786436
  16.5 5.0 %copy-start.4 = (bf16[1,4,2,128,128]{4,3,2,1,0:T(8,128)(2,1)S(1)}, bf16[1,4,2,128,128]{4,3,2,1,0:T(8,128)(2,1)}, u32[]{:S(2)}) copy-start(bf16[1,4,2,128,128]{4,3,2,1,0:T(8,128)(2,1)} %param.7) | copy-start | bytes 786436
  19.5 3.8 %collective-permute-start = (bf16[2,1,4,2,128,128]{4,5,0,2,3,1:T(8,128)(2,1)S(1)}, bf16[2,1,4,2,128,128]{4,5,0,2,3,1:T(8,128)(2,1)S(1)}, u32[]{:S(2)}, u32[]{:S(2)}) collective-permute-start(bf16[2,1,4,2,128,128]{4,5,0,2,3,1:T(8,128)(2,1)S(1)} %copy.80), channel_id=1, source_target_pairs={{0,32},{32,0},{64,96},{96,64},{128,160},{160,128},{192,224},{224,1... | collective-permute-start | bytes 1572872 | tf_op jit(solution)/shard_map/ppermute | solution.py:103
  43.0 27.5 %all-to-all-start = ((bf16[32,2,4,2,512]{4,3,2,1,0:T(2,128)(2,1)}), bf16[32,2,4,2,512]{4,3,2,1,0:T(2,128)(2,1)S(1)}, u32[]{:S(2)}, u32[]{:S(2)}) async-start(bf16[32,2,4,2,512]{4,3,2,1,0:T(2,128)(2,1)} %reshape.338), calls=%async_computation | async-start | bytes 1048576 | tf_op jit(solution)/shard_map/all_to_all | solution.py:129

commit v7 on v6

--- a/solution.py
+++ b/solution.py
@@ -46,25 +46,17 @@
 
 
 def congruence(green, sigma):
-    green_real = green[:, :, 0]
-    green_imag = green[:, :, 1]
-    sigma_real = sigma[:, :, :, 0]
-    sigma_imag = sigma[:, :, :, 1]
-    green_wide = jnp.concatenate([green_real, green_imag], axis=-1)
-    sigma_tall = jnp.concatenate(
-        [
-            jnp.concatenate([sigma_real, sigma_imag], axis=-1),
-            jnp.concatenate([-sigma_imag, sigma_real], axis=-1),
-        ],
-        axis=-2,
+    green = jnp.broadcast_to(green[None], (sigma.shape[0],) + green.shape)
+    product = jnp.einsum(
+        "fneiqr,fnegsr->fneiqgs", sigma, green, preferred_element_type=jnp.float32
     )
-    mixed = jnp.einsum(
-        "nepq,fneqr->fnepr", green_wide, sigma_tall, preferred_element_type=jnp.float32
-    ).astype(jnp.bfloat16)
-    adjoint_tall = jnp.concatenate(
-        [green_wide, jnp.concatenate([-green_imag, green_real], axis=-1)], axis=-2
-    )
-    return jnp.einsum("fnepr,nesr->fneps", mixed, adjoint_tall, preferred_element_type=jnp.float32)
+    right_real = product[:, :, :, 0, :, 0] + product[:, :, :, 1, :, 1]
+    right_imag = product[:, :, :, 1, :, 0] - product[:, :, :, 0, :, 1]
+    right = jnp.stack([right_real, right_imag], axis=3).astype(jnp.bfloat16)
+    total = jnp.einsum("fnegpq,fnecqs->fnegcps", green, right, preferred_element_type=jnp.float32)
+    out_real = total[:, :, :, 0, 0] - total[:, :, :, 1, 1]
+    out_imag = total[:, :, :, 0, 1] + total[:, :, :, 1, 0]
+    return jnp.stack([out_real, out_imag], axis=3)
 
 
 def split_table(table):
@@ -98,9 +90,8 @@
     across = [(i, i + 1) for i in range(1, peers - 1, 2)]
     across = across + [(j, i) for i, j in across]
     neighbour = lax.ppermute(self_energy, "space", across)
+    partner = lax.ppermute(self_energy, "space", on_chip)
     diag_term = congruence(green_diag, self_energy)
-    own_energy, diag_term = lax.optimization_barrier((self_energy, diag_term))
-    partner = lax.ppermute(own_energy, "space", on_chip)
     even = lax.axis_index("space") % 2 == 0
     green_on = jnp.where(even, green_upper, green_lower)
     green_across = jnp.where(even, green_lower, green_upper)
@@ -109,8 +100,8 @@
     across_term = congruence(green_across, neighbour)
     total = near_sum + across_term
     groups = lax.axis_size("energy")
-    total = total.reshape(2, block_count, energy_local, groups, block_order // groups, 2, block_order)
-    outgoing = jnp.transpose(total, (3, 0, 2, 5, 1, 4, 6)).astype(jnp.bfloat16)
+    total = total.reshape(2, block_count, energy_local, 2, groups, block_order // groups, block_order)
+    outgoing = jnp.transpose(total, (4, 0, 2, 3, 1, 5, 6)).astype(jnp.bfloat16)
     outgoing = outgoing.reshape(groups, 2, energy_local, 2, -1)
     frequency = lax.iota(jnp.int32, padded_len)
     energy_index = lax.iota(jnp.int32, energies)

time: 96.5 us -> 95 us (0.984)
  local copies, waits for them, and re-layouts: 6.53 us -> 3.56 us
  waiting for transfers between devices: 26.7 us -> 28.7 us
  matrix products: 8.9 us -> 7.27 us
  other arithmetic: 5.02 us -> 6.1 us
    ppermute x1, waiting for transfers between devices: 14.1 us -> 16.5 us  [body(): neighbour = lax.ppermute(self_energy, 'space', across)]
    dot_general x3 -> x6, matrix products: 6.45 us -> 4.83 us  [the longest x3 3.38 us: congruence(): jnp.einsum('fneiqr,fnegsr->fneiqgs', sigma, green, preferred_element_type...]
    squeeze x6 -> x0, local copies, waits for them, and re-layouts: 1.53 us -> none  [the longest x3 1.41 us: congruence(): green_imag = green[:, :, 1]]
    unnamed x11 -> x4, local copies, waits for them, and re-layouts: 1.38 us -> 0.01 us
    broadcast_in_dim x0 -> x1, other arithmetic: none -> 1.07 us  [congruence(): green = jnp.broadcast_to(green[None], (sigma.shape[0],) + green.shape)]
    another operation x5 -> x8, other arithmetic: 2.53 us -> 2.76 us
  transfers between devices with their start and end apart: 3 -> 3, of which waited for: 3 -> 2; matrix products, arithmetic and copies ran while one was open for 12% -> 11% of each run, Pallas kernels for 0% -> 0%
where the time goes in v7:
time: 95 us; the launch traced here: 94.6 us
  waiting for transfers between devices  28.7 us (30%)
  starting transfers between devices  26.5 us (28%)
  blocking collectives  22.1 us (23%)
  matrix products  7.27 us (8%)
  other arithmetic  6.1 us (6%)
  local copies, waits for them, and re-layouts  3.56 us (4%)
    all_to_all x1, blocking collectives, body(): returned = lax.all_to_all(polar, 'energy', 0, 0, tiled=True)  22.1 us
    ppermute x1, waiting for transfers between devices, body(): neighbour = lax.ppermute(self_energy, 'space', across)  16.5 us
    ppermute x1, starting transfers between devices, body(): neighbour = lax.ppermute(self_energy, 'space', across)  14.4 us
    all_to_all x1, waiting for transfers between devices, body(): entries = lax.all_to_all(outgoing, 'energy', 0, 0, tiled=True)  12.2 us
    all_to_all x1, starting transfers between devices, body(): entries = lax.all_to_all(outgoing, 'energy', 0, 0, tiled=True)  10.2 us
    dot_general x3, matrix products, congruence(): jnp.einsum('fneiqr,fnegsr->fneiqgs', sigma, green, preferred_element_type...  3.38 us
    another operation x5, other arithmetic  2.53 us
    ppermute x1, starting transfers between devices, body(): partner = lax.ppermute(self_energy, 'space', on_chip)  1.92 us
  transfers between devices with their start and end apart: 3, of which 2 were waited for; matrix products, arithmetic and copies ran while one was open for 11% of the time, Pallas kernels for 0%

profile of v7, /device:TPU:14, one launch (start us, length us, event | category | flops | bytes accessed | tf_op | source)
XLA Modules:
  0.0 94.6 jit_solution(8934316944061846520)
XLA Ops:
  0.0 14.4 %collective-permute-start.1 = (bf16[2,1,4,2,128,128]{5,4,3,2,1,0:T(8,128)(2,1)}, bf16[2,1,4,2,128,128]{5,4,3,2,1,0:T(8,128)(2,1)S(1)}, u32[]{:S(2)}, u32[]{:S(2)}) collective-permute-start(bf16[2,1,4,2,128,128]{5,4,3,2,1,0:T(8,128)(2,1)} %param.8), channel_id=1, source_target_pairs={{32,64},{96,128},{160,192},{224,256},{288,320},{352,384},{416,448}... | collective-permute-start | bytes 1572872 | tf_op jit(solution)/shard_map/ppermute | solution.py:92
  14.4 1.9 %collective-permute-start = (bf16[2,1,4,2,128,128]{5,4,3,2,0,1:T(8,128)(2,1)}, bf16[2,1,4,2,128,128]{5,4,3,2,0,1:T(8,128)(2,1)}, u32[]{:S(2)}, u32[]{:S(2)}) collective-permute-start(bf16[2,1,4,2,128,128]{5,4,3,2,0,1:T(8,128)(2,1)} %bitcast.202), channel_id=1, source_target_pairs={{0,32},{32,0},{64,96},{96,64},{128,160},{160,128},{192,224},{224,1... | collective-permute-start | bytes 1572872 | tf_op jit(solution)/shard_map/ppermute | solution.py:93
  16.3 1.5 %convolution_bitcast_fusion.6 = f32[2,1,4,2,128,2,128]{6,4,5,3,2,0,1:T(8,128)S(1)} fusion(bf16[2,1,4,2,128,128]{5,4,3,2,1,0:T(8,128)(2,1)} %param.8, bf16[4,2,128,128]{3,2,1,0:T(8,128)(2,1)S(1)} %bitcast.198), kind=kOutput, calls=%fused_computation.6 | convolution fusion | flops 134217728 | bytes 2883584 | tf_op jit(solution)/shard_map/fneiqr,fnegsr->fneiqgs/dot_general | solution.py:50
  17.8 0.1 fusion.38
  17.9 0.1 fusion.39
  17.9 0.5 convolution_bitcast_fusion.5
  18.4 0.1 fusion.16
  18.5 0.1 fusion.18
  18.6 1.1 %select_bitcast_fusion = (bf16[4,2,128,128]{3,2,1,0:T(8,128)(2,1)S(1)}, bf16[4,2,128,128]{3,2,1,0:T(8,128)(2,1)S(1)}) fusion(bf16[1,4,2,128,128]{4,3,2,1,0:T(8,128)(2,1)} %param.5, bf16[1,4,2,128,128]{4,3,2,1,0:T(8,128)(2,1)} %param.7, pred[]{:T(512)S(6)} %eq.12), kind=kLoop, calls=%fused_computation.93 | loop fusion | flops 262144 | bytes 1048577 | tf_op jit(solution)/shard_map/broadcast_in_dim | solution.py:49
  19.7 1.5 %convolution_bitcast_fusion.4 = f32[2,1,4,2,128,2,128]{4,6,3,5,2,0,1:T(8,128)S(1)} fusion(bf16[2,1,4,2,128,128]{5,4,3,2,0,1:T(8,128)(2,1)} %collective-permute-done, bf16[4,2,128,128]{3,2,1,0:T(8,128)(2,1)S(1)} %get-tuple-element.16), kind=kOutput, calls=%fused_computation.4 | convolution fusion | flops 134217728 | bytes 2883584 | tf_op jit(solution)/shard_map/fneiqr,fnegsr->fneiqgs/dot_general | solution.py:50
  21.1 0.1 fusion.40
  21.2 0.1 fusion.41
  21.3 0.5 convolution_bitcast_fusion.3
  21.7 0.1 fusion.12
  21.8 0.1 maximum_add_fusion
  22.0 16.5 %collective-permute-done.1 = bf16[2,1,4,2,128,128]{5,4,3,2,1,0:T(8,128)(2,1)S(1)} collective-permute-done((bf16[2,1,4,2,128,128]{5,4,3,2,1,0:T(8,128)(2,1)}, bf16[2,1,4,2,128,128]{5,4,3,2,1,0:T(8,128)(2,1)S(1)}, u32[]{:S(2)}, u32[]{:S(2)}) %collective-permute-start.1) | collective-permute-done | bytes 524320 | tf_op jit(solution)/shard_map/ppermute | solution.py:92
  38.5 0.4 convolution_bitcast_fusion.2
  38.9 0.1 fusion.42
  39.0 0.1 fusion.43
  39.0 0.5 convolution_bitcast_fusion.1
  39.5 0.1 fusion.7
  39.7 0.2 fusion.3
  39.8 0.3 copy.65
  40.1 0.2 reshape.647
  40.3 1.3 %copy.66 = bf16[32,2,4,2,512]{4,3,2,1,0:T(2,128)(2,1)} copy(bf16[32,2,4,2,512]{4,0,3,2,1:T(8,128)(2,1)S(1)} %reshape.647) | data formatting | bytes 1048576 | tf_op jit(solution)/shard_map/reshape | solution.py:105
  41.7 10.2 %all-to-all-start = ((bf16[32,2,4,2,512]{4,3,2,1,0:T(2,128)(2,1)}), bf16[32,2,4,2,512]{4,3,2,1,0:T(2,128)(2,1)S(1)}, u32[]{:S(2)}, u32[]{:S(2)}) async-start(bf16[32,2,4,2,512]{4,3,2,1,0:T(2,128)(2,1)} %copy.66), calls=%async_computation | async-start | bytes 1048576 | tf_op jit(solution)/shard_map/all_to_all | solution.py:120
  51.9 0.6 fusion.82
  52.5 0.2 copy.50
  52.8 0.1 concatenate.71
  52.9 0.1 copy.47
  53.0 0.5 fusion.78
  53.5 0.5 negate_convert_fusion.2
  54.1 0.2 copy.48
  54.3 0.2 copy.49
  54.5 0.3 fusion.44
  54.8 1.2 %pad_maximum_fusion = bf16[128,4,512]{2,1,0:T(4,128)(2,1)S(1)} fusion(bf16[128,1,512]{2,1,0:T(2,128)(2,1)S(1)} %fusion.44, bf16[128,1,512]{2,1,0:T(2,128)(2,1)S(1)} %copy.50, bf16[128,1,512]{2,1,0:T(2,128)(2,1)S(1)} %copy.49, bf16[128,1,512]{2,1,0:T(2,128)(2,1)S(1)} %copy.48), kind=kLoop, calls=%fused_computation.50 | loop fusion | flops 2097152 | bytes 1048576 | tf_op jit(solution)/shard_map/stack | solution.py:143
  56.0 0.1 convert_element_type.111
  56.2 0.6 fusion.76
  56.8 12.2 %all-to-all-done = bf16[32,2,4,2,512]{4,3,2,1,0:T(2,128)(2,1)S(1)} async-done(((bf16[32,2,4,2,512]{4,3,2,1,0:T(2,128)(2,1)}), bf16[32,2,4,2,512]{4,3,2,1,0:T(2,128)(2,1)S(1)}, u32[]{:S(2)}, u32[]{:S(2)}) %all-to-all-start) | async-done | bytes 524320 | tf_op jit(solution)/shard_map/all_to_all | solution.py:120
  69.0 0.6 convolution_bitcast_fusion
  69.6 0.3 fusion.36
  69.9 0.4 fusion
  70.3 0.0 copy-start.1
  70.3 0.2 reshape.648
  70.5 22.1 %all_to_all.10 = bf16[32,4,2,2,512]{4,3,2,1,0:T(2,128)(2,1)S(1)} all-to-all(bf16[32,4,2,2,512]{4,3,2,1,0:T(2,128)(2,1)S(1)} %reshape.648), channel_id=1, replica_groups=mesh['space'=24,'energy'=32] {'energy'}, dimensions={0} | all-to-all | bytes 1048576 | tf_op jit(solution)/shard_map/all_to_all | solution.py:152
  92.6 0.3 reshape.665
  92.9 0.2 copy.94
  93.2 1.4 %fusion.2 = bf16[2,1,4,2,128,128]{5,4,3,2,1,0:T(8,128)(2,1)} fusion(bf16[2,4,2,128,128]{4,3,2,1,0:T(8,128)(2,1)S(1)} %bitcast.201, bf16[1,128,128]{2,1,0:T(8,128)(2,1)S(1)} %copy-done.1), kind=kOutput, calls=%fused_computation.12 | convolution fusion | flops 134742016 | bytes 1081344 | tf_op jit(solution)/shard_map/fetnpr,nsr->fnetps/dot_general | solution.py:159
  (8 shorter events, 0.1 us)
Async XLA Ops:
  0.0 16.3 %copy-start = (bf16[1,4,2,128,128]{4,3,2,1,0:T(8,128)(2,1)S(1)}, bf16[1,4,2,128,128]{4,3,2,1,0:T(8,128)(2,1)}, u32[]{:S(2)}) copy-start(bf16[1,4,2,128,128]{4,3,2,1,0:T(8,128)(2,1)} %param.6) | copy-start | bytes 786436
  0.0 38.5 %collective-permute-start.1 = (bf16[2,1,4,2,128,128]{5,4,3,2,1,0:T(8,128)(2,1)}, bf16[2,1,4,2,128,128]{5,4,3,2,1,0:T(8,128)(2,1)S(1)}, u32[]{:S(2)}, u32[]{:S(2)}) collective-permute-start(bf16[2,1,4,2,128,128]{5,4,3,2,1,0:T(8,128)(2,1)} %param.8), channel_id=1, source_target_pairs={{32,64},{96,128},{160,192},{224,256},{288,320},{352,384},{416,448}... | collective-permute-start | bytes 1572872 | tf_op jit(solution)/shard_map/ppermute | solution.py:92
  14.4 5.3 %collective-permute-start = (bf16[2,1,4,2,128,128]{5,4,3,2,0,1:T(8,128)(2,1)}, bf16[2,1,4,2,128,128]{5,4,3,2,0,1:T(8,128)(2,1)}, u32[]{:S(2)}, u32[]{:S(2)}) collective-permute-start(bf16[2,1,4,2,128,128]{5,4,3,2,0,1:T(8,128)(2,1)} %bitcast.202), channel_id=1, source_target_pairs={{0,32},{32,0},{64,96},{96,64},{128,160},{160,128},{192,224},{224,1... | collective-permute-start | bytes 1572872 | tf_op jit(solution)/shard_map/ppermute | solution.py:93
  41.7 27.3 %all-to-all-start = ((bf16[32,2,4,2,512]{4,3,2,1,0:T(2,128)(2,1)}), bf16[32,2,4,2,512]{4,3,2,1,0:T(2,128)(2,1)S(1)}, u32[]{:S(2)}, u32[]{:S(2)}) async-start(bf16[32,2,4,2,512]{4,3,2,1,0:T(2,128)(2,1)} %copy.66), calls=%async_computation | async-start | bytes 1048576 | tf_op jit(solution)/shard_map/all_to_all | solution.py:120
  70.3 22.9 %copy-start.1 = (bf16[1,128,128]{2,1,0:T(8,128)(2,1)S(1)}, bf16[1,128,128]{2,1,0:T(8,128)(2,1)}, u32[]{:S(2)}) copy-start(bf16[1,128,128]{2,1,0:T(8,128)(2,1)} %param.9) | copy-start | bytes 98308

commit v8 on v7

--- a/solution.py
+++ b/solution.py
@@ -4,45 +4,6 @@
 import jax.numpy as jnp
 from jax import lax
 from jax.sharding import PartitionSpec as P
-
-
-def padded_2(shard, sides, width):
-    for axis, dim in sides:
-        peers, length = (lax.axis_size(axis), shard.shape[dim])
-        up = [(i, (i + 1) % peers) for i in range(peers - 1)]
-        down = [(j, i) for i, j in up]
-        last = lax.slice_in_dim(shard, length - width, length, axis=dim)
-        initial = lax.slice_in_dim(shard, 0, width, axis=dim)
-        before = lax.ppermute(last, axis, up)
-        after = lax.ppermute(initial, axis, down)
-        shard = jnp.concatenate([before, shard, after], axis=dim)
-    return shard
-
-
-def in_blocks(shard, dim, peers):
-    before, after = (shard.shape[:dim], shard.shape[dim + 1 :])
-    return jnp.moveaxis(shard.reshape(*before, peers, -1, *after), dim, 0)
-
-
-def edges_of(length, count):
-    unit = 8 if length >= 8 * count else 1
-    return [length // unit * k // count * unit for k in range(1, count)]
-
-
-def joined_along(tiles, dim):
-    tiles = jnp.moveaxis(tiles, 0, dim)
-    shape = tiles.shape
-    return tiles.reshape(*shape[:dim], shape[dim] * shape[dim + 1], *shape[dim + 2 :])
-
-
-def cut_exchange(shard, axis, pieces, split_dim, concat_dim):
-    tiles = in_blocks(shard, split_dim, lax.axis_size(axis))
-    split_at = max(range(1, max(2, tiles.ndim - 1)), key=lambda d: tiles.shape[d])
-    gathered = []
-    for slab in jnp.split(tiles, edges_of(tiles.shape[split_at], pieces), axis=split_at):
-        if slab.size:
-            gathered.append(lax.all_to_all(slab, axis, split_axis=0, concat_axis=0, tiled=True))
-    return joined_along(jnp.concatenate(gathered, axis=split_at), concat_dim)
 
 
 def congruence(green, sigma):
@@ -57,26 +18,6 @@
     out_real = total[:, :, :, 0, 0] - total[:, :, :, 1, 1]
     out_imag = total[:, :, :, 0, 1] + total[:, :, :, 1, 0]
     return jnp.stack([out_real, out_imag], axis=3)
-
-
-def split_table(table):
-    high_part = table.astype(jnp.bfloat16)
-    low_part = (table - high_part.astype(jnp.float32)).astype(jnp.bfloat16)
-    return (high_part, low_part)
-
-
-def spectrum(values, table_high, table_low, padded_len):
-
-    def apply_table(part):
-        return jnp.dot(table_high, part, preferred_element_type=jnp.float32) + jnp.dot(
-            table_low, part, preferred_element_type=jnp.float32
-        )
-
-    real_terms = apply_table(values[:, 0])
-    imag_terms = apply_table(values[:, 1])
-    out_real = real_terms[:padded_len] + imag_terms[padded_len:]
-    out_imag = imag_terms[:padded_len] - real_terms[padded_len:]
-    return (out_real, out_imag)
 
 
 def body(green_lower, green_diag, green_upper, self_energy, coulomb):

time: 95 us -> 95 us (level)
  no operation moved by 1% of the time
where the time goes in v8:
time: 95 us; the launch traced here: 94.6 us
  waiting for transfers between devices  28.7 us (30%)
  starting transfers between devices  26.5 us (28%)
  blocking collectives  22.1 us (23%)
  matrix products  7.27 us (8%)
  other arithmetic  6.1 us (6%)
  local copies, waits for them, and re-layouts  3.56 us (4%)
    all_to_all x1, blocking collectives, body(): returned = lax.all_to_all(polar, 'energy', 0, 0, tiled=True)  22.1 us
    ppermute x1, waiting for transfers between devices, body(): neighbour = lax.ppermute(self_energy, 'space', across)  16.5 us
    ppermute x1, starting transfers between devices, body(): neighbour = lax.ppermute(self_energy, 'space', across)  14.4 us
    all_to_all x1, waiting for transfers between devices, body(): entries = lax.all_to_all(outgoing, 'energy', 0, 0, tiled=True)  12.2 us
    all_to_all x1, starting transfers between devices, body(): entries = lax.all_to_all(outgoing, 'energy', 0, 0, tiled=True)  10.2 us
    dot_general x3, matrix products, congruence(): jnp.einsum('fneiqr,fnegsr->fneiqgs', sigma, green, preferred_element_type...  3.38 us
    another operation x5, other arithmetic  2.53 us
    ppermute x1, starting transfers between devices, body(): partner = lax.ppermute(self_energy, 'space', on_chip)  1.92 us
  transfers between devices with their start and end apart: 3, of which 2 were waited for; matrix products, arithmetic and copies ran while one was open for 11% of the time, Pallas kernels for 0%

profile of v8, /device:TPU:14, one launch (start us, length us, event | category | flops | bytes accessed | tf_op | source)
XLA Modules:
  0.0 94.6 jit_solution(8934316944061846520)
XLA Ops:
  0.0 14.4 %collective-permute-start.1 = (bf16[2,1,4,2,128,128]{5,4,3,2,1,0:T(8,128)(2,1)}, bf16[2,1,4,2,128,128]{5,4,3,2,1,0:T(8,128)(2,1)S(1)}, u32[]{:S(2)}, u32[]{:S(2)}) collective-permute-start(bf16[2,1,4,2,128,128]{5,4,3,2,1,0:T(8,128)(2,1)} %param.8), channel_id=1, source_target_pairs={{32,64},{96,128},{160,192},{224,256},{288,320},{352,384},{416,448}... | collective-permute-start | bytes 1572872 | tf_op jit(solution)/shard_map/ppermute | solution.py:33
  14.4 1.9 %collective-permute-start = (bf16[2,1,4,2,128,128]{5,4,3,2,0,1:T(8,128)(2,1)}, bf16[2,1,4,2,128,128]{5,4,3,2,0,1:T(8,128)(2,1)}, u32[]{:S(2)}, u32[]{:S(2)}) collective-permute-start(bf16[2,1,4,2,128,128]{5,4,3,2,0,1:T(8,128)(2,1)} %bitcast.202), channel_id=1, source_target_pairs={{0,32},{32,0},{64,96},{96,64},{128,160},{160,128},{192,224},{224,1... | collective-permute-start | bytes 1572872 | tf_op jit(solution)/shard_map/ppermute | solution.py:34
  16.3 1.5 %convolution_bitcast_fusion.6 = f32[2,1,4,2,128,2,128]{6,4,5,3,2,0,1:T(8,128)S(1)} fusion(bf16[2,1,4,2,128,128]{5,4,3,2,1,0:T(8,128)(2,1)} %param.8, bf16[4,2,128,128]{3,2,1,0:T(8,128)(2,1)S(1)} %bitcast.198), kind=kOutput, calls=%fused_computation.6 | convolution fusion | flops 134217728 | bytes 2883584 | tf_op jit(solution)/shard_map/fneiqr,fnegsr->fneiqgs/dot_general | solution.py:11
  17.8 0.1 fusion.38
  17.9 0.1 fusion.39
  17.9 0.5 convolution_bitcast_fusion.5
  18.4 0.1 fusion.16
  18.5 0.1 fusion.18
  18.6 1.1 %select_bitcast_fusion = (bf16[4,2,128,128]{3,2,1,0:T(8,128)(2,1)S(1)}, bf16[4,2,128,128]{3,2,1,0:T(8,128)(2,1)S(1)}) fusion(bf16[1,4,2,128,128]{4,3,2,1,0:T(8,128)(2,1)} %param.5, bf16[1,4,2,128,128]{4,3,2,1,0:T(8,128)(2,1)} %param.7, pred[]{:T(512)S(6)} %eq.12), kind=kLoop, calls=%fused_computation.93 | loop fusion | flops 262144 | bytes 1048577 | tf_op jit(solution)/shard_map/broadcast_in_dim | solution.py:10
  19.7 1.5 %convolution_bitcast_fusion.4 = f32[2,1,4,2,128,2,128]{4,6,3,5,2,0,1:T(8,128)S(1)} fusion(bf16[2,1,4,2,128,128]{5,4,3,2,0,1:T(8,128)(2,1)} %collective-permute-done, bf16[4,2,128,128]{3,2,1,0:T(8,128)(2,1)S(1)} %get-tuple-element.16), kind=kOutput, calls=%fused_computation.4 | convolution fusion | flops 134217728 | bytes 2883584 | tf_op jit(solution)/shard_map/fneiqr,fnegsr->fneiqgs/dot_general | solution.py:11
  21.1 0.1 fusion.40
  21.2 0.1 fusion.41
  21.3 0.5 convolution_bitcast_fusion.3
  21.7 0.1 fusion.12
  21.8 0.1 maximum_add_fusion
  22.0 16.5 %collective-permute-done.1 = bf16[2,1,4,2,128,128]{5,4,3,2,1,0:T(8,128)(2,1)S(1)} collective-permute-done((bf16[2,1,4,2,128,128]{5,4,3,2,1,0:T(8,128)(2,1)}, bf16[2,1,4,2,128,128]{5,4,3,2,1,0:T(8,128)(2,1)S(1)}, u32[]{:S(2)}, u32[]{:S(2)}) %collective-permute-start.1) | collective-permute-done | bytes 524320 | tf_op jit(solution)/shard_map/ppermute | solution.py:33
  38.5 0.4 convolution_bitcast_fusion.2
  38.9 0.1 fusion.42
  39.0 0.1 fusion.43
  39.0 0.5 convolution_bitcast_fusion.1
  39.5 0.1 fusion.7
  39.7 0.2 fusion.3
  39.8 0.3 copy.65
  40.1 0.2 reshape.647
  40.3 1.3 %copy.66 = bf16[32,2,4,2,512]{4,3,2,1,0:T(2,128)(2,1)} copy(bf16[32,2,4,2,512]{4,0,3,2,1:T(8,128)(2,1)S(1)} %reshape.647) | data formatting | bytes 1048576 | tf_op jit(solution)/shard_map/reshape | solution.py:46
  41.7 10.2 %all-to-all-start = ((bf16[32,2,4,2,512]{4,3,2,1,0:T(2,128)(2,1)}), bf16[32,2,4,2,512]{4,3,2,1,0:T(2,128)(2,1)S(1)}, u32[]{:S(2)}, u32[]{:S(2)}) async-start(bf16[32,2,4,2,512]{4,3,2,1,0:T(2,128)(2,1)} %copy.66), calls=%async_computation | async-start | bytes 1048576 | tf_op jit(solution)/shard_map/all_to_all | solution.py:61
  51.9 0.6 fusion.82
  52.5 0.2 copy.50
  52.8 0.1 concatenate.71
  52.9 0.1 copy.47
  53.0 0.5 fusion.78
  53.5 0.5 negate_convert_fusion.2
  54.1 0.2 copy.48
  54.3 0.2 copy.49
  54.5 0.3 fusion.44
  54.8 1.2 %pad_maximum_fusion = bf16[128,4,512]{2,1,0:T(4,128)(2,1)S(1)} fusion(bf16[128,1,512]{2,1,0:T(2,128)(2,1)S(1)} %fusion.44, bf16[128,1,512]{2,1,0:T(2,128)(2,1)S(1)} %copy.50, bf16[128,1,512]{2,1,0:T(2,128)(2,1)S(1)} %copy.49, bf16[128,1,512]{2,1,0:T(2,128)(2,1)S(1)} %copy.48), kind=kLoop, calls=%fused_computation.50 | loop fusion | flops 2097152 | bytes 1048576 | tf_op jit(solution)/shard_map/stack | solution.py:84
  56.0 0.1 convert_element_type.111
  56.2 0.6 fusion.76
  56.8 12.2 %all-to-all-done = bf16[32,2,4,2,512]{4,3,2,1,0:T(2,128)(2,1)S(1)} async-done(((bf16[32,2,4,2,512]{4,3,2,1,0:T(2,128)(2,1)}), bf16[32,2,4,2,512]{4,3,2,1,0:T(2,128)(2,1)S(1)}, u32[]{:S(2)}, u32[]{:S(2)}) %all-to-all-start) | async-done | bytes 524320 | tf_op jit(solution)/shard_map/all_to_all | solution.py:61
  69.0 0.6 convolution_bitcast_fusion
  69.6 0.3 fusion.36
  69.9 0.4 fusion
  70.3 0.0 copy-start.1
  70.3 0.2 reshape.648
  70.5 22.1 %all_to_all.10 = bf16[32,4,2,2,512]{4,3,2,1,0:T(2,128)(2,1)S(1)} all-to-all(bf16[32,4,2,2,512]{4,3,2,1,0:T(2,128)(2,1)S(1)} %reshape.648), channel_id=1, replica_groups=mesh['space'=24,'energy'=32] {'energy'}, dimensions={0} | all-to-all | bytes 1048576 | tf_op jit(solution)/shard_map/all_to_all | solution.py:93
  92.6 0.3 reshape.665
  92.9 0.2 copy.94
  93.2 1.4 %fusion.2 = bf16[2,1,4,2,128,128]{5,4,3,2,1,0:T(8,128)(2,1)} fusion(bf16[2,4,2,128,128]{4,3,2,1,0:T(8,128)(2,1)S(1)} %bitcast.201, bf16[1,128,128]{2,1,0:T(8,128)(2,1)S(1)} %copy-done.1), kind=kOutput, calls=%fused_computation.12 | convolution fusion | flops 134742016 | bytes 1081344 | tf_op jit(solution)/shard_map/fetnpr,nsr->fnetps/dot_general | solution.py:100
  (8 shorter events, 0.1 us)
Async XLA Ops:
  0.0 16.3 %copy-start = (bf16[1,4,2,128,128]{4,3,2,1,0:T(8,128)(2,1)S(1)}, bf16[1,4,2,128,128]{4,3,2,1,0:T(8,128)(2,1)}, u32[]{:S(2)}) copy-start(bf16[1,4,2,128,128]{4,3,2,1,0:T(8,128)(2,1)} %param.6) | copy-start | bytes 786436
  0.0 38.5 %collective-permute-start.1 = (bf16[2,1,4,2,128,128]{5,4,3,2,1,0:T(8,128)(2,1)}, bf16[2,1,4,2,128,128]{5,4,3,2,1,0:T(8,128)(2,1)S(1)}, u32[]{:S(2)}, u32[]{:S(2)}) collective-permute-start(bf16[2,1,4,2,128,128]{5,4,3,2,1,0:T(8,128)(2,1)} %param.8), channel_id=1, source_target_pairs={{32,64},{96,128},{160,192},{224,256},{288,320},{352,384},{416,448}... | collective-permute-start | bytes 1572872 | tf_op jit(solution)/shard_map/ppermute | solution.py:33
  14.4 5.3 %collective-permute-start = (bf16[2,1,4,2,128,128]{5,4,3,2,0,1:T(8,128)(2,1)}, bf16[2,1,4,2,128,128]{5,4,3,2,0,1:T(8,128)(2,1)}, u32[]{:S(2)}, u32[]{:S(2)}) collective-permute-start(bf16[2,1,4,2,128,128]{5,4,3,2,0,1:T(8,128)(2,1)} %bitcast.202), channel_id=1, source_target_pairs={{0,32},{32,0},{64,96},{96,64},{128,160},{160,128},{192,224},{224,1... | collective-permute-start | bytes 1572872 | tf_op jit(solution)/shard_map/ppermute | solution.py:34
  41.7 27.3 %all-to-all-start = ((bf16[32,2,4,2,512]{4,3,2,1,0:T(2,128)(2,1)}), bf16[32,2,4,2,512]{4,3,2,1,0:T(2,128)(2,1)S(1)}, u32[]{:S(2)}, u32[]{:S(2)}) async-start(bf16[32,2,4,2,512]{4,3,2,1,0:T(2,128)(2,1)} %copy.66), calls=%async_computation | async-start | bytes 1048576 | tf_op jit(solution)/shard_map/all_to_all | solution.py:61
  70.3 22.9 %copy-start.1 = (bf16[1,128,128]{2,1,0:T(8,128)(2,1)S(1)}, bf16[1,128,128]{2,1,0:T(8,128)(2,1)}, u32[]{:S(2)}) copy-start(bf16[1,128,128]{2,1,0:T(8,128)(2,1)} %param.9) | copy-start | bytes 98308

commit v9 on v7

--- a/solution.py
+++ b/solution.py
@@ -151,10 +151,9 @@
     polar = (combined * factor).astype(jnp.bfloat16).reshape(groups, energy_local, 2, 2, -1)
     returned = lax.all_to_all(polar, "energy", 0, 0, tiled=True)
     returned = returned.reshape(groups, energy_local, 2, 2, block_count, -1, block_order)
-    returned = jnp.transpose(returned, (2, 1, 3, 4, 0, 5, 6))
-    returned = returned.reshape(2, energy_local, 2, block_count, block_order, block_order)
+    coulomb_split = coulomb.reshape(block_count, block_order, groups, -1)
     left_product = jnp.einsum(
-        "npq,fetnqr->fetnpr", coulomb, returned, preferred_element_type=jnp.float32
+        "npxi,xeftnir->fetnpr", coulomb_split, returned, preferred_element_type=jnp.float32
     ).astype(jnp.bfloat16)
     screened = jnp.einsum(
         "fetnpr,nsr->fnetps", left_product, coulomb, preferred_element_type=jnp.float32

time: 95 us -> 96 us (1.011)
  blocking collectives: 22.1 us -> 0 us
  waiting for transfers between devices: 28.7 us -> 46 us
  starting transfers between devices: 26.5 us -> 31.4 us
    all_to_all x1 -> x0, blocking collectives: 22.1 us -> none  [body(): returned = lax.all_to_all(polar, 'energy', 0, 0, tiled=True)]
    all_to_all x0 -> x1, waiting for transfers between devices: none -> 17.3 us  [body(): returned = lax.all_to_all(polar, 'energy', 0, 0, tiled=True)]
    all_to_all x0 -> x1, starting transfers between devices: none -> 4.86 us  [body(): returned = lax.all_to_all(polar, 'energy', 0, 0, tiled=True)]
  transfers between devices with their start and end apart: 3 -> 4, of which waited for: 2 -> 3; matrix products, arithmetic and copies ran while one was open for 11% -> 11% of each run, Pallas kernels for 0% -> 0%
where the time goes in v9:
time: 96 us; the launch traced here: 95.6 us
  waiting for transfers between devices  46 us (48%)
  starting transfers between devices  31.4 us (33%)
  matrix products  7.52 us (8%)
  other arithmetic  6.1 us (6%)
  local copies, waits for them, and re-layouts  4.23 us (4%)
    all_to_all x1, waiting for transfers between devices, body(): returned = lax.all_to_all(polar, 'energy', 0, 0, tiled=True)  17.3 us
    ppermute x1, waiting for transfers between devices, body(): neighbour = lax.ppermute(self_energy, 'space', across)  16.5 us
    ppermute x1, starting transfers between devices, body(): neighbour = lax.ppermute(self_energy, 'space', across)  14.4 us
    all_to_all x1, waiting for transfers between devices, body(): entries = lax.all_to_all(outgoing, 'energy', 0, 0, tiled=True)  12.2 us
    all_to_all x1, starting transfers between devices, body(): entries = lax.all_to_all(outgoing, 'energy', 0, 0, tiled=True)  10.2 us
    all_to_all x1, starting transfers between devices, body(): returned = lax.all_to_all(polar, 'energy', 0, 0, tiled=True)  4.86 us
    dot_general x3, matrix products, congruence(): jnp.einsum('fneiqr,fnegsr->fneiqgs', sigma, green, preferred_element_type...  3.38 us
    another operation x5, other arithmetic  2.53 us
  transfers between devices with their start and end apart: 4, of which 3 were waited for; matrix products, arithmetic and copies ran while one was open for 11% of the time, Pallas kernels for 0%

profile of v9, /device:TPU:14, one launch (start us, length us, event | category | flops | bytes accessed | tf_op | source)
XLA Modules:
  0.0 95.6 jit_solution(17556860716623297283)
XLA Ops:
  0.0 14.4 %collective-permute-start.1 = (bf16[2,1,4,2,128,128]{5,4,3,2,1,0:T(8,128)(2,1)}, bf16[2,1,4,2,128,128]{5,4,3,2,1,0:T(8,128)(2,1)S(1)}, u32[]{:S(2)}, u32[]{:S(2)}) collective-permute-start(bf16[2,1,4,2,128,128]{5,4,3,2,1,0:T(8,128)(2,1)} %param.8), channel_id=1, source_target_pairs={{32,64},{96,128},{160,192},{224,256},{288,320},{352,384},{416,448}... | collective-permute-start | bytes 1572872 | tf_op jit(solution)/shard_map/ppermute | solution.py:92
  14.4 1.9 %collective-permute-start = (bf16[2,1,4,2,128,128]{5,4,3,2,0,1:T(8,128)(2,1)}, bf16[2,1,4,2,128,128]{5,4,3,2,0,1:T(8,128)(2,1)}, u32[]{:S(2)}, u32[]{:S(2)}) collective-permute-start(bf16[2,1,4,2,128,128]{5,4,3,2,0,1:T(8,128)(2,1)} %bitcast.202), channel_id=1, source_target_pairs={{0,32},{32,0},{64,96},{96,64},{128,160},{160,128},{192,224},{224,1... | collective-permute-start | bytes 1572872 | tf_op jit(solution)/shard_map/ppermute | solution.py:93
  16.3 1.5 %convolution_bitcast_fusion.6 = f32[2,1,4,2,128,2,128]{6,4,5,3,2,0,1:T(8,128)S(1)} fusion(bf16[2,1,4,2,128,128]{5,4,3,2,1,0:T(8,128)(2,1)} %param.8, bf16[4,2,128,128]{3,2,1,0:T(8,128)(2,1)S(1)} %bitcast.199), kind=kOutput, calls=%fused_computation.6 | convolution fusion | flops 134217728 | bytes 2883584 | tf_op jit(solution)/shard_map/fneiqr,fnegsr->fneiqgs/dot_general | solution.py:50
  17.8 0.1 fusion.41
  17.9 0.1 fusion.42
  17.9 0.5 convolution_bitcast_fusion.5
  18.4 0.1 fusion.17
  18.5 0.1 fusion.19
  18.6 1.1 %select_bitcast_fusion = (bf16[4,2,128,128]{3,2,1,0:T(8,128)(2,1)S(1)}, bf16[4,2,128,128]{3,2,1,0:T(8,128)(2,1)S(1)}) fusion(bf16[1,4,2,128,128]{4,3,2,1,0:T(8,128)(2,1)} %param.5, bf16[1,4,2,128,128]{4,3,2,1,0:T(8,128)(2,1)} %param.7, pred[]{:T(512)S(6)} %eq.12), kind=kLoop, calls=%fused_computation.96 | loop fusion | flops 262144 | bytes 1048577 | tf_op jit(solution)/shard_map/broadcast_in_dim | solution.py:49
  19.7 1.5 %convolution_bitcast_fusion.4 = f32[2,1,4,2,128,2,128]{4,6,3,5,2,0,1:T(8,128)S(1)} fusion(bf16[2,1,4,2,128,128]{5,4,3,2,0,1:T(8,128)(2,1)} %collective-permute-done, bf16[4,2,128,128]{3,2,1,0:T(8,128)(2,1)S(1)} %get-tuple-element.16), kind=kOutput, calls=%fused_computation.4 | convolution fusion | flops 134217728 | bytes 2883584 | tf_op jit(solution)/shard_map/fneiqr,fnegsr->fneiqgs/dot_general | solution.py:50
  21.1 0.1 fusion.43
  21.2 0.1 fusion.44
  21.3 0.5 convolution_bitcast_fusion.3
  21.7 0.1 fusion.13
  21.8 0.1 maximum_add_fusion
  22.0 16.5 %collective-permute-done.1 = bf16[2,1,4,2,128,128]{5,4,3,2,1,0:T(8,128)(2,1)S(1)} collective-permute-done((bf16[2,1,4,2,128,128]{5,4,3,2,1,0:T(8,128)(2,1)}, bf16[2,1,4,2,128,128]{5,4,3,2,1,0:T(8,128)(2,1)S(1)}, u32[]{:S(2)}, u32[]{:S(2)}) %collective-permute-start.1) | collective-permute-done | bytes 524320 | tf_op jit(solution)/shard_map/ppermute | solution.py:92
  38.5 0.4 convolution_bitcast_fusion.2
  38.9 0.1 fusion.45
  39.0 0.5 convolution_bitcast_fusion.1
  39.5 0.1 fusion.8
  39.7 0.2 fusion.4
  39.8 0.3 copy.67
  40.1 0.2 reshape.648
  40.3 1.3 %copy.68 = bf16[32,2,4,2,512]{4,3,2,1,0:T(2,128)(2,1)} copy(bf16[32,2,4,2,512]{4,0,3,2,1:T(8,128)(2,1)S(1)} %reshape.648) | data formatting | bytes 1048576 | tf_op jit(solution)/shard_map/reshape | solution.py:105
  41.7 10.2 %all-to-all-start = ((bf16[32,2,4,2,512]{4,3,2,1,0:T(2,128)(2,1)}), bf16[32,2,4,2,512]{4,3,2,1,0:T(2,128)(2,1)S(1)}, u32[]{:S(2)}, u32[]{:S(2)}) async-start(bf16[32,2,4,2,512]{4,3,2,1,0:T(2,128)(2,1)} %copy.68), calls=%async_computation | async-start | bytes 1048576 | tf_op jit(solution)/shard_map/all_to_all | solution.py:120
  51.9 0.6 fusion.85
  52.5 0.2 copy.52
  52.8 0.1 concatenate.71
  52.9 0.1 copy.49
  53.0 0.5 fusion.81
  53.5 0.5 negate_convert_fusion.2
  54.1 0.2 copy.50
  54.3 0.2 copy.51
  54.5 0.3 fusion.47
  54.8 1.2 %pad_maximum_fusion = bf16[128,4,512]{2,1,0:T(4,128)(2,1)S(1)} fusion(bf16[128,1,512]{2,1,0:T(2,128)(2,1)S(1)} %fusion.47, bf16[128,1,512]{2,1,0:T(2,128)(2,1)S(1)} %copy.52, bf16[128,1,512]{2,1,0:T(2,128)(2,1)S(1)} %copy.51, bf16[128,1,512]{2,1,0:T(2,128)(2,1)S(1)} %copy.50), kind=kLoop, calls=%fused_computation.51 | loop fusion | flops 2097152 | bytes 1048576 | tf_op jit(solution)/shard_map/stack | solution.py:143
  56.0 0.1 convert_element_type.111
  56.2 0.6 fusion.79
  56.8 12.2 %all-to-all-done = bf16[32,2,4,2,512]{4,3,2,1,0:T(2,128)(2,1)S(1)} async-done(((bf16[32,2,4,2,512]{4,3,2,1,0:T(2,128)(2,1)}), bf16[32,2,4,2,512]{4,3,2,1,0:T(2,128)(2,1)S(1)}, u32[]{:S(2)}, u32[]{:S(2)}) %all-to-all-start) | async-done | bytes 524320 | tf_op jit(solution)/shard_map/all_to_all | solution.py:120
  69.0 0.6 convolution_bitcast_fusion
  69.6 0.3 fusion.39
  69.9 0.4 fusion.1
  70.3 1.0 %reshape.649 = bf16[32,4,2,2,512]{4,3,2,1,0:T(2,128)(2,1)} reshape(bf16[512,512]{1,0:T(8,128)(2,1)S(1)} %fusion.1) | data formatting | bytes 1048576 | tf_op jit(solution)/shard_map/reshape | solution.py:151
  71.3 4.9 %all-to-all-start.1 = ((bf16[32,4,2,2,512]{4,3,2,1,0:T(2,128)(2,1)}), bf16[32,4,2,2,512]{4,3,2,1,0:T(2,128)(2,1)S(1)}, u32[]{:S(2)}, u32[]{:S(2)}) async-start(bf16[32,4,2,2,512]{4,3,2,1,0:T(2,128)(2,1)} %reshape.649), calls=%async_computation.1 | async-start | bytes 1048576 | tf_op jit(solution)/shard_map/all_to_all | solution.py:152
  76.2 0.1 copy.71
  76.3 17.3 %all-to-all-done.1 = bf16[32,4,2,2,512]{4,3,2,1,0:T(2,128)(2,1)S(1)} async-done(((bf16[32,4,2,2,512]{4,3,2,1,0:T(2,128)(2,1)}), bf16[32,4,2,2,512]{4,3,2,1,0:T(2,128)(2,1)S(1)}, u32[]{:S(2)}, u32[]{:S(2)}) %all-to-all-start.1) | async-done | bytes 524320 | tf_op jit(solution)/shard_map/all_to_all | solution.py:152
  93.6 0.3 reshape.668
  93.9 0.5 fusion.3
  94.5 1.1 %fusion.2 = bf16[2,1,4,2,128,128]{5,4,3,2,1,0:T(8,128)(2,1)} fusion(bf16[2,4,2,128,128]{3,4,2,0,1:T(8,128)(2,1)S(1)} %fusion.3, bf16[1,128,128]{2,1,0:T(8,128)(2,1)S(1)} %copy-done.1), kind=kOutput, calls=%fused_computation.12 | convolution fusion | flops 67371008 | bytes 1081344 | tf_op jit(solution)/shard_map/fetnpr,nsr->fnetps/dot_general | solution.py:158
  (10 shorter events, 0.1 us)
Async XLA Ops:
  0.0 16.3 %copy-start = (bf16[1,4,2,128,128]{4,3,2,1,0:T(8,128)(2,1)S(1)}, bf16[1,4,2,128,128]{4,3,2,1,0:T(8,128)(2,1)}, u32[]{:S(2)}) copy-start(bf16[1,4,2,128,128]{4,3,2,1,0:T(8,128)(2,1)} %param.6) | copy-start | bytes 786436
  0.0 38.5 %collective-permute-start.1 = (bf16[2,1,4,2,128,128]{5,4,3,2,1,0:T(8,128)(2,1)}, bf16[2,1,4,2,128,128]{5,4,3,2,1,0:T(8,128)(2,1)S(1)}, u32[]{:S(2)}, u32[]{:S(2)}) collective-permute-start(bf16[2,1,4,2,128,128]{5,4,3,2,1,0:T(8,128)(2,1)} %param.8), channel_id=1, source_target_pairs={{32,64},{96,128},{160,192},{224,256},{288,320},{352,384},{416,448}... | collective-permute-start | bytes 1572872 | tf_op jit(solution)/shard_map/ppermute | solution.py:92
  14.4 5.3 %collective-permute-start = (bf16[2,1,4,2,128,128]{5,4,3,2,0,1:T(8,128)(2,1)}, bf16[2,1,4,2,128,128]{5,4,3,2,0,1:T(8,128)(2,1)}, u32[]{:S(2)}, u32[]{:S(2)}) collective-permute-start(bf16[2,1,4,2,128,128]{5,4,3,2,0,1:T(8,128)(2,1)} %bitcast.202), channel_id=1, source_target_pairs={{0,32},{32,0},{64,96},{96,64},{128,160},{160,128},{192,224},{224,1... | collective-permute-start | bytes 1572872 | tf_op jit(solution)/shard_map/ppermute | solution.py:93
  41.7 27.3 %all-to-all-start = ((bf16[32,2,4,2,512]{4,3,2,1,0:T(2,128)(2,1)}), bf16[32,2,4,2,512]{4,3,2,1,0:T(2,128)(2,1)S(1)}, u32[]{:S(2)}, u32[]{:S(2)}) async-start(bf16[32,2,4,2,512]{4,3,2,1,0:T(2,128)(2,1)} %copy.68), calls=%async_computation | async-start | bytes 1048576 | tf_op jit(solution)/shard_map/all_to_all | solution.py:120
  69.9 6.3 %copy-start.1 = (bf16[1,128,128]{2,1,0:T(8,128)(2,1)S(1)}, bf16[1,128,128]{2,1,0:T(8,128)(2,1)}, u32[]{:S(2)}) copy-start(bf16[1,128,128]{2,1,0:T(8,128)(2,1)} %param.9) | copy-start | bytes 98308
  71.3 22.3 %all-to-all-start.1 = ((bf16[32,4,2,2,512]{4,3,2,1,0:T(2,128)(2,1)}), bf16[32,4,2,2,512]{4,3,2,1,0:T(2,128)(2,1)S(1)}, u32[]{:S(2)}, u32[]{:S(2)}) async-start(bf16[32,4,2,2,512]{4,3,2,1,0:T(2,128)(2,1)} %reshape.649), calls=%async_computation.1 | async-start | bytes 1048576 | tf_op jit(solution)/shard_map/all_to_all | solution.py:152

commit v10 on v9

--- a/solution.py
+++ b/solution.py
@@ -96,7 +96,10 @@
     green_on = jnp.where(even, green_upper, green_lower)
     green_across = jnp.where(even, green_lower, green_upper)
     near_sum = diag_term + congruence(green_on, partner)
-    near_sum, neighbour = lax.optimization_barrier((near_sum, neighbour))
+    coulomb_split = jnp.transpose(
+        coulomb.reshape(block_count, block_order, lax.axis_size("energy"), -1), (0, 2, 3, 1)
+    )
+    near_sum, neighbour, coulomb_split = lax.optimization_barrier((near_sum, neighbour, coulomb_split))
     across_term = congruence(green_across, neighbour)
     total = near_sum + across_term
     groups = lax.axis_size("energy")
@@ -151,9 +154,8 @@
     polar = (combined * factor).astype(jnp.bfloat16).reshape(groups, energy_local, 2, 2, -1)
     returned = lax.all_to_all(polar, "energy", 0, 0, tiled=True)
     returned = returned.reshape(groups, energy_local, 2, 2, block_count, -1, block_order)
-    coulomb_split = coulomb.reshape(block_count, block_order, groups, -1)
     left_product = jnp.einsum(
-        "npxi,xeftnir->fetnpr", coulomb_split, returned, preferred_element_type=jnp.float32
+        "nxip,xeftnir->fetnpr", coulomb_split, returned, preferred_element_type=jnp.float32
     ).astype(jnp.bfloat16)
     screened = jnp.einsum(
         "fetnpr,nsr->fnetps", left_product, coulomb, preferred_element_type=jnp.float32

time: 96 us -> 95 us (0.990)
  blocking collectives: 0 us -> 22.1 us
  waiting for transfers between devices: 46 us -> 28.4 us
  starting transfers between devices: 31.4 us -> 26.5 us
    all_to_all x0 -> x1, blocking collectives: none -> 22.1 us  [body(): returned = lax.all_to_all(polar, 'energy', 0, 0, tiled=True)]
    all_to_all x1 -> x0, waiting for transfers between devices: 17.3 us -> none  [body(): returned = lax.all_to_all(polar, 'energy', 0, 0, tiled=True)]
    all_to_all x1 -> x0, starting transfers between devices: 4.86 us -> none  [body(): returned = lax.all_to_all(polar, 'energy', 0, 0, tiled=True)]
  transfers between devices with their start and end apart: 4 -> 3, of which waited for: 3 -> 2; matrix products, arithmetic and copies ran while one was open for 11% -> 11% of each run, Pallas kernels for 0% -> 0%
where the time goes in v10:
time: 95 us; the launch traced here: 94.6 us
  waiting for transfers between devices  28.4 us (30%)
  starting transfers between devices  26.5 us (28%)
  blocking collectives  22.1 us (23%)
  matrix products  7.52 us (8%)
  other arithmetic  6.1 us (6%)
  local copies, waits for them, and re-layouts  3.6 us (4%)
    all_to_all x1, blocking collectives, body(): returned = lax.all_to_all(polar, 'energy', 0, 0, tiled=True)  22.1 us
    ppermute x1, waiting for transfers between devices, body(): neighbour = lax.ppermute(self_energy, 'space', across)  16.2 us
    ppermute x1, starting transfers between devices, body(): neighbour = lax.ppermute(self_energy, 'space', across)  14.4 us
    all_to_all x1, waiting for transfers between devices, body(): entries = lax.all_to_all(outgoing, 'energy', 0, 0, tiled=True)  12.2 us
    all_to_all x1, starting transfers between devices, body(): entries = lax.all_to_all(outgoing, 'energy', 0, 0, tiled=True)  10.2 us
    dot_general x3, matrix products, congruence(): jnp.einsum('fneiqr,fnegsr->fneiqgs', sigma, green, preferred_element_type...  3.38 us
    another operation x5, other arithmetic  2.53 us
    ppermute x1, starting transfers between devices, body(): partner = lax.ppermute(self_energy, 'space', on_chip)  1.92 us
  transfers between devices with their start and end apart: 3, of which 2 were waited for; matrix products, arithmetic and copies ran while one was open for 11% of the time, Pallas kernels for 0%

profile of v10, /device:TPU:14, one launch (start us, length us, event | category | flops | bytes accessed | tf_op | source)
XLA Modules:
  0.0 94.6 jit_solution(14154586512216816956)
XLA Ops:
  0.0 14.4 %collective-permute-start.1 = (bf16[2,1,4,2,128,128]{5,4,3,2,1,0:T(8,128)(2,1)}, bf16[2,1,4,2,128,128]{5,4,3,2,1,0:T(8,128)(2,1)S(1)}, u32[]{:S(2)}, u32[]{:S(2)}) collective-permute-start(bf16[2,1,4,2,128,128]{5,4,3,2,1,0:T(8,128)(2,1)} %param.8), channel_id=1, source_target_pairs={{32,64},{96,128},{160,192},{224,256},{288,320},{352,384},{416,448}... | collective-permute-start | bytes 1572872 | tf_op jit(solution)/shard_map/ppermute | solution.py:92
  14.4 1.9 %collective-permute-start = (bf16[2,1,4,2,128,128]{5,4,3,2,0,1:T(8,128)(2,1)}, bf16[2,1,4,2,128,128]{5,4,3,2,0,1:T(8,128)(2,1)}, u32[]{:S(2)}, u32[]{:S(2)}) collective-permute-start(bf16[2,1,4,2,128,128]{5,4,3,2,0,1:T(8,128)(2,1)} %bitcast.205), channel_id=1, source_target_pairs={{0,32},{32,0},{64,96},{96,64},{128,160},{160,128},{192,224},{224,1... | collective-permute-start | bytes 1572872 | tf_op jit(solution)/shard_map/ppermute | solution.py:93
  16.3 1.5 %convolution_bitcast_fusion.6 = f32[2,1,4,2,128,2,128]{6,4,5,3,2,0,1:T(8,128)S(1)} fusion(bf16[2,1,4,2,128,128]{5,4,3,2,1,0:T(8,128)(2,1)} %param.8, bf16[4,2,128,128]{3,2,1,0:T(8,128)(2,1)S(1)} %bitcast.202), kind=kOutput, calls=%fused_computation.6 | convolution fusion | flops 134217728 | bytes 2883584 | tf_op jit(solution)/shard_map/fneiqr,fnegsr->fneiqgs/dot_general | solution.py:50
  17.8 0.1 fusion.41
  17.9 0.1 fusion.42
  17.9 0.5 convolution_bitcast_fusion.5
  18.4 0.1 fusion.17
  18.5 0.2 copy-done.1
  18.7 0.1 copy.63
  18.8 0.1 fusion.19
  18.9 1.1 %select_bitcast_fusion = (bf16[4,2,128,128]{3,2,1,0:T(8,128)(2,1)S(1)}, bf16[4,2,128,128]{3,2,1,0:T(8,128)(2,1)S(1)}) fusion(bf16[1,4,2,128,128]{4,3,2,1,0:T(8,128)(2,1)} %param.5, bf16[1,4,2,128,128]{4,3,2,1,0:T(8,128)(2,1)} %param.7, pred[]{:T(512)S(6)} %eq.12), kind=kLoop, calls=%fused_computation.96 | loop fusion | flops 262144 | bytes 1048577 | tf_op jit(solution)/shard_map/broadcast_in_dim | solution.py:49
  20.0 1.5 %convolution_bitcast_fusion.4 = f32[2,1,4,2,128,2,128]{4,6,3,5,2,0,1:T(8,128)S(1)} fusion(bf16[2,1,4,2,128,128]{5,4,3,2,0,1:T(8,128)(2,1)} %collective-permute-done, bf16[4,2,128,128]{3,2,1,0:T(8,128)(2,1)S(1)} %get-tuple-element.18), kind=kOutput, calls=%fused_computation.4 | convolution fusion | flops 134217728 | bytes 2883584 | tf_op jit(solution)/shard_map/fneiqr,fnegsr->fneiqgs/dot_general | solution.py:50
  21.4 0.1 fusion.43
  21.5 0.1 fusion.44
  21.6 0.5 convolution_bitcast_fusion.3
  22.0 0.1 fusion.13
  22.1 0.1 maximum_add_fusion
  22.3 16.2 %collective-permute-done.1 = bf16[2,1,4,2,128,128]{5,4,3,2,1,0:T(8,128)(2,1)S(1)} collective-permute-done((bf16[2,1,4,2,128,128]{5,4,3,2,1,0:T(8,128)(2,1)}, bf16[2,1,4,2,128,128]{5,4,3,2,1,0:T(8,128)(2,1)S(1)}, u32[]{:S(2)}, u32[]{:S(2)}) %collective-permute-start.1) | collective-permute-done | bytes 524320 | tf_op jit(solution)/shard_map/ppermute | solution.py:92
  38.5 0.4 convolution_bitcast_fusion.2
  38.9 0.1 fusion.45
  39.0 0.5 convolution_bitcast_fusion.1
  39.5 0.1 fusion.8
  39.7 0.2 fusion.4
  39.8 0.3 copy.68
  40.1 0.2 reshape.650
  40.3 1.3 %copy.69 = bf16[32,2,4,2,512]{4,3,2,1,0:T(2,128)(2,1)} copy(bf16[32,2,4,2,512]{4,0,3,2,1:T(8,128)(2,1)S(1)} %reshape.650) | data formatting | bytes 1048576 | tf_op jit(solution)/shard_map/reshape | solution.py:108
  41.7 10.2 %all-to-all-start = ((bf16[32,2,4,2,512]{4,3,2,1,0:T(2,128)(2,1)}), bf16[32,2,4,2,512]{4,3,2,1,0:T(2,128)(2,1)S(1)}, u32[]{:S(2)}, u32[]{:S(2)}) async-start(bf16[32,2,4,2,512]{4,3,2,1,0:T(2,128)(2,1)} %copy.69), calls=%async_computation | async-start | bytes 1048576 | tf_op jit(solution)/shard_map/all_to_all | solution.py:123
  51.9 0.6 fusion.85
  52.5 0.2 copy.52
  52.8 0.1 concatenate.71
  52.9 0.1 copy.49
  53.0 0.5 fusion.81
  53.5 0.5 negate_convert_fusion.2
  54.1 0.2 copy.50
  54.3 0.2 copy.51
  54.5 0.3 fusion.47
  54.8 1.2 %pad_maximum_fusion = bf16[128,4,512]{2,1,0:T(4,128)(2,1)S(1)} fusion(bf16[128,1,512]{2,1,0:T(2,128)(2,1)S(1)} %fusion.47, bf16[128,1,512]{2,1,0:T(2,128)(2,1)S(1)} %copy.52, bf16[128,1,512]{2,1,0:T(2,128)(2,1)S(1)} %copy.51, bf16[128,1,512]{2,1,0:T(2,128)(2,1)S(1)} %copy.50), kind=kLoop, calls=%fused_computation.51 | loop fusion | flops 2097152 | bytes 1048576 | tf_op jit(solution)/shard_map/stack | solution.py:146
  56.0 0.1 convert_element_type.111
  56.2 0.6 fusion.79
  56.8 12.2 %all-to-all-done = bf16[32,2,4,2,512]{4,3,2,1,0:T(2,128)(2,1)S(1)} async-done(((bf16[32,2,4,2,512]{4,3,2,1,0:T(2,128)(2,1)}), bf16[32,2,4,2,512]{4,3,2,1,0:T(2,128)(2,1)S(1)}, u32[]{:S(2)}, u32[]{:S(2)}) %all-to-all-start) | async-done | bytes 524320 | tf_op jit(solution)/shard_map/all_to_all | solution.py:123
  69.0 0.6 convolution_bitcast_fusion
  69.6 0.3 fusion.39
  69.9 0.4 fusion.1
  70.3 0.2 reshape.651
  70.5 22.1 %all_to_all.10 = bf16[32,4,2,2,512]{4,3,2,1,0:T(2,128)(2,1)S(1)} all-to-all(bf16[32,4,2,2,512]{4,3,2,1,0:T(2,128)(2,1)S(1)} %reshape.651), channel_id=1, replica_groups=mesh['space'=24,'energy'=32] {'energy'}, dimensions={0} | all-to-all | bytes 1048576 | tf_op jit(solution)/shard_map/all_to_all | solution.py:155
  92.6 0.3 reshape.670
  92.9 0.5 fusion.3
  93.5 1.1 %fusion.2 = bf16[2,1,4,2,128,128]{5,4,3,2,1,0:T(8,128)(2,1)} fusion(bf16[2,4,2,128,128]{3,4,2,0,1:T(8,128)(2,1)S(1)} %fusion.3, bf16[1,128,128]{2,1,0:T(8,128)(2,1)S(1)} %copy-done.1), kind=kOutput, calls=%fused_computation.12 | convolution fusion | flops 67371008 | bytes 1081344 | tf_op jit(solution)/shard_map/fetnpr,nsr->fnetps/dot_general | solution.py:160
  (9 shorter events, 0.1 us)
Async XLA Ops:
  0.0 16.3 %copy-start = (bf16[1,4,2,128,128]{4,3,2,1,0:T(8,128)(2,1)S(1)}, bf16[1,4,2,128,128]{4,3,2,1,0:T(8,128)(2,1)}, u32[]{:S(2)}) copy-start(bf16[1,4,2,128,128]{4,3,2,1,0:T(8,128)(2,1)} %param.6) | copy-start | bytes 786436
  0.0 38.5 %collective-permute-start.1 = (bf16[2,1,4,2,128,128]{5,4,3,2,1,0:T(8,128)(2,1)}, bf16[2,1,4,2,128,128]{5,4,3,2,1,0:T(8,128)(2,1)S(1)}, u32[]{:S(2)}, u32[]{:S(2)}) collective-permute-start(bf16[2,1,4,2,128,128]{5,4,3,2,1,0:T(8,128)(2,1)} %param.8), channel_id=1, source_target_pairs={{32,64},{96,128},{160,192},{224,256},{288,320},{352,384},{416,448}... | collective-permute-start | bytes 1572872 | tf_op jit(solution)/shard_map/ppermute | solution.py:92
  14.4 5.6 %collective-permute-start = (bf16[2,1,4,2,128,128]{5,4,3,2,0,1:T(8,128)(2,1)}, bf16[2,1,4,2,128,128]{5,4,3,2,0,1:T(8,128)(2,1)}, u32[]{:S(2)}, u32[]{:S(2)}) collective-permute-start(bf16[2,1,4,2,128,128]{5,4,3,2,0,1:T(8,128)(2,1)} %bitcast.205), channel_id=1, source_target_pairs={{0,32},{32,0},{64,96},{96,64},{128,160},{160,128},{192,224},{224,1... | collective-permute-start | bytes 1572872 | tf_op jit(solution)/shard_map/ppermute | solution.py:93
  17.9 0.8 copy-start.1
  41.7 27.3 %all-to-all-start = ((bf16[32,2,4,2,512]{4,3,2,1,0:T(2,128)(2,1)}), bf16[32,2,4,2,512]{4,3,2,1,0:T(2,128)(2,1)S(1)}, u32[]{:S(2)}, u32[]{:S(2)}) async-start(bf16[32,2,4,2,512]{4,3,2,1,0:T(2,128)(2,1)} %copy.69), calls=%async_computation | async-start | bytes 1048576 | tf_op jit(solution)/shard_map/all_to_all | solution.py:123

commit v11 on v7

--- a/solution.py
+++ b/solution.py
@@ -149,6 +149,7 @@
         preferred_element_type=jnp.float32,
     )
     polar = (combined * factor).astype(jnp.bfloat16).reshape(groups, energy_local, 2, 2, -1)
+    polar = polar.reshape(groups, 4 * energy_local, -1)
     returned = lax.all_to_all(polar, "energy", 0, 0, tiled=True)
     returned = returned.reshape(groups, energy_local, 2, 2, block_count, -1, block_order)
     returned = jnp.transpose(returned, (2, 1, 3, 4, 0, 5, 6))

time: 95 us -> 94.6 us (level)
  no operation moved by 1% of the time
where the time goes in v11:
time: 94.6 us; the launch traced here: 94.2 us
  waiting for transfers between devices  28.7 us (30%)
  starting transfers between devices  26.5 us (28%)
  blocking collectives  22.1 us (23%)
  matrix products  7.28 us (8%)
  other arithmetic  6.1 us (6%)
  local copies, waits for them, and re-layouts  3.15 us (3%)
    all_to_all x1, blocking collectives, body(): returned = lax.all_to_all(polar, 'energy', 0, 0, tiled=True)  22.1 us
    ppermute x1, waiting for transfers between devices, body(): neighbour = lax.ppermute(self_energy, 'space', across)  16.5 us
    ppermute x1, starting transfers between devices, body(): neighbour = lax.ppermute(self_energy, 'space', across)  14.4 us
    all_to_all x1, waiting for transfers between devices, body(): entries = lax.all_to_all(outgoing, 'energy', 0, 0, tiled=True)  12.2 us
    all_to_all x1, starting transfers between devices, body(): entries = lax.all_to_all(outgoing, 'energy', 0, 0, tiled=True)  10.2 us
    dot_general x3, matrix products, congruence(): jnp.einsum('fneiqr,fnegsr->fneiqgs', sigma, green, preferred_element_type...  3.38 us
    another operation x5, other arithmetic  2.53 us
    ppermute x1, starting transfers between devices, body(): partner = lax.ppermute(self_energy, 'space', on_chip)  1.92 us
  transfers between devices with their start and end apart: 3, of which 2 were waited for; matrix products, arithmetic and copies ran while one was open for 11% of the time, Pallas kernels for 0%

profile of v11, /device:TPU:14, one launch (start us, length us, event | category | flops | bytes accessed | tf_op | source)
XLA Modules:
  0.0 94.2 jit_solution(13616651333314835578)
XLA Ops:
  0.0 14.4 %collective-permute-start.1 = (bf16[2,1,4,2,128,128]{5,4,3,2,1,0:T(8,128)(2,1)}, bf16[2,1,4,2,128,128]{5,4,3,2,1,0:T(8,128)(2,1)S(1)}, u32[]{:S(2)}, u32[]{:S(2)}) collective-permute-start(bf16[2,1,4,2,128,128]{5,4,3,2,1,0:T(8,128)(2,1)} %param.8), channel_id=1, source_target_pairs={{32,64},{96,128},{160,192},{224,256},{288,320},{352,384},{416,448}... | collective-permute-start | bytes 1572872 | tf_op jit(solution)/shard_map/ppermute | solution.py:92
  14.4 1.9 %collective-permute-start = (bf16[2,1,4,2,128,128]{5,4,3,2,0,1:T(8,128)(2,1)}, bf16[2,1,4,2,128,128]{5,4,3,2,0,1:T(8,128)(2,1)}, u32[]{:S(2)}, u32[]{:S(2)}) collective-permute-start(bf16[2,1,4,2,128,128]{5,4,3,2,0,1:T(8,128)(2,1)} %bitcast.204), channel_id=1, source_target_pairs={{0,32},{32,0},{64,96},{96,64},{128,160},{160,128},{192,224},{224,1... | collective-permute-start | bytes 1572872 | tf_op jit(solution)/shard_map/ppermute | solution.py:93
  16.3 1.5 %convolution_bitcast_fusion.6 = f32[2,1,4,2,128,2,128]{6,4,5,3,2,0,1:T(8,128)S(1)} fusion(bf16[2,1,4,2,128,128]{5,4,3,2,1,0:T(8,128)(2,1)} %param.8, bf16[4,2,128,128]{3,2,1,0:T(8,128)(2,1)S(1)} %bitcast.198), kind=kOutput, calls=%fused_computation.6 | convolution fusion | flops 134217728 | bytes 2883584 | tf_op jit(solution)/shard_map/fneiqr,fnegsr->fneiqgs/dot_general | solution.py:50
  17.8 0.1 fusion.38
  17.9 0.1 fusion.39
  17.9 0.5 convolution_bitcast_fusion.5
  18.4 0.1 fusion.16
  18.5 0.1 fusion.18
  18.6 1.1 %select_bitcast_fusion = (bf16[4,2,128,128]{3,2,1,0:T(8,128)(2,1)S(1)}, bf16[4,2,128,128]{3,2,1,0:T(8,128)(2,1)S(1)}) fusion(bf16[1,4,2,128,128]{4,3,2,1,0:T(8,128)(2,1)} %param.5, bf16[1,4,2,128,128]{4,3,2,1,0:T(8,128)(2,1)} %param.7, pred[]{:T(512)S(6)} %eq.12), kind=kLoop, calls=%fused_computation.93 | loop fusion | flops 262144 | bytes 1048577 | tf_op jit(solution)/shard_map/broadcast_in_dim | solution.py:49
  19.6 0.0 collective-permute-done
  19.7 1.5 %convolution_bitcast_fusion.4 = f32[2,1,4,2,128,2,128]{4,6,3,5,2,0,1:T(8,128)S(1)} fusion(bf16[2,1,4,2,128,128]{5,4,3,2,0,1:T(8,128)(2,1)} %collective-permute-done, bf16[4,2,128,128]{3,2,1,0:T(8,128)(2,1)S(1)} %get-tuple-element.16), kind=kOutput, calls=%fused_computation.4 | convolution fusion | flops 134217728 | bytes 2883584 | tf_op jit(solution)/shard_map/fneiqr,fnegsr->fneiqgs/dot_general | solution.py:50
  21.1 0.1 fusion.40
  21.2 0.1 fusion.41
  21.3 0.5 convolution_bitcast_fusion.3
  21.7 0.1 fusion.12
  21.8 0.1 maximum_add_fusion
  22.0 16.5 %collective-permute-done.1 = bf16[2,1,4,2,128,128]{5,4,3,2,1,0:T(8,128)(2,1)S(1)} collective-permute-done((bf16[2,1,4,2,128,128]{5,4,3,2,1,0:T(8,128)(2,1)}, bf16[2,1,4,2,128,128]{5,4,3,2,1,0:T(8,128)(2,1)S(1)}, u32[]{:S(2)}, u32[]{:S(2)}) %collective-permute-start.1) | collective-permute-done | bytes 524320 | tf_op jit(solution)/shard_map/ppermute | solution.py:92
  38.5 0.4 convolution_bitcast_fusion.2
  38.9 0.1 fusion.42
  39.0 0.1 fusion.43
  39.0 0.5 convolution_bitcast_fusion.1
  39.5 0.1 fusion.7
  39.7 0.2 fusion.3
  39.8 0.3 copy.88
  40.1 0.2 reshape.644
  40.3 1.3 %copy.89 = bf16[32,2,4,2,512]{4,3,1,2,0:T(2,128)(2,1)} copy(bf16[32,2,4,2,512]{4,0,3,2,1:T(8,128)(2,1)S(1)} %reshape.644) | data formatting | bytes 1048576 | tf_op jit(solution)/shard_map/reshape | solution.py:105
  41.7 10.2 %all-to-all-start = ((bf16[32,2,4,2,512]{4,3,1,2,0:T(2,128)(2,1)}), bf16[32,2,4,2,512]{4,3,1,2,0:T(2,128)(2,1)S(1)}, u32[]{:S(2)}, u32[]{:S(2)}) async-start(bf16[32,2,4,2,512]{4,3,1,2,0:T(2,128)(2,1)} %copy.89), calls=%async_computation | async-start | bytes 1048576 | tf_op jit(solution)/shard_map/all_to_all | solution.py:120
  51.9 0.6 fusion.82
  52.5 0.2 copy.73
  52.8 0.1 concatenate.71
  52.9 0.1 copy.70
  53.0 0.5 fusion.78
  53.5 0.5 negate_convert_fusion.2
  54.1 0.2 copy.71
  54.3 0.2 copy.72
  54.5 0.3 fusion.44
  54.8 1.2 %pad_maximum_fusion = bf16[128,4,512]{2,1,0:T(4,128)(2,1)S(1)} fusion(bf16[128,1,512]{2,1,0:T(2,128)(2,1)S(1)} %fusion.44, bf16[128,1,512]{2,1,0:T(2,128)(2,1)S(1)} %copy.73, bf16[128,1,512]{2,1,0:T(2,128)(2,1)S(1)} %copy.72, bf16[128,1,512]{2,1,0:T(2,128)(2,1)S(1)} %copy.71), kind=kLoop, calls=%fused_computation.50 | loop fusion | flops 2097152 | bytes 1048576 | tf_op jit(solution)/shard_map/stack | solution.py:143
  56.0 0.1 convert_element_type.111
  56.2 0.6 fusion.76
  56.8 12.2 %all-to-all-done = bf16[32,2,4,2,512]{4,3,1,2,0:T(2,128)(2,1)S(1)} async-done(((bf16[32,2,4,2,512]{4,3,1,2,0:T(2,128)(2,1)}), bf16[32,2,4,2,512]{4,3,1,2,0:T(2,128)(2,1)S(1)}, u32[]{:S(2)}, u32[]{:S(2)}) %all-to-all-start) | async-done | bytes 524320 | tf_op jit(solution)/shard_map/all_to_all | solution.py:120
  69.0 0.6 convolution_bitcast_fusion
  69.6 0.3 fusion.36
  69.9 0.4 fusion
  70.3 0.0 copy-start.1
  70.3 22.1 %all_to_all.10 = bf16[32,16,512]{2,1,0:T(8,128)(2,1)S(1)} all-to-all(bf16[32,16,512]{2,1,0:T(8,128)(2,1)S(1)} %bitcast.203), channel_id=1, replica_groups=mesh['space'=24,'energy'=32] {'energy'}, dimensions={0} | all-to-all | bytes 1048576 | tf_op jit(solution)/shard_map/all_to_all | solution.py:153
  92.4 0.1 reshape.645
  92.5 0.2 copy.91
  92.8 1.4 %fusion.2 = bf16[2,1,4,2,128,128]{5,4,3,2,1,0:T(8,128)(2,1)} fusion(bf16[2,4,2,128,128]{4,3,2,1,0:T(8,128)(2,1)S(1)} %bitcast.202, bf16[1,128,128]{2,1,0:T(8,128)(2,1)S(1)} %copy-done.1), kind=kOutput, calls=%fused_computation.12 | convolution fusion | flops 134742016 | bytes 1081344 | tf_op jit(solution)/shard_map/fetnpr,nsr->fnetps/dot_general | solution.py:160
  (7 shorter events, 0.1 us)
Async XLA Ops:
  0.0 16.3 %copy-start = (bf16[1,4,2,128,128]{4,3,2,1,0:T(8,128)(2,1)S(1)}, bf16[1,4,2,128,128]{4,3,2,1,0:T(8,128)(2,1)}, u32[]{:S(2)}) copy-start(bf16[1,4,2,128,128]{4,3,2,1,0:T(8,128)(2,1)} %param.6) | copy-start | bytes 786436
  0.0 38.5 %collective-permute-start.1 = (bf16[2,1,4,2,128,128]{5,4,3,2,1,0:T(8,128)(2,1)}, bf16[2,1,4,2,128,128]{5,4,3,2,1,0:T(8,128)(2,1)S(1)}, u32[]{:S(2)}, u32[]{:S(2)}) collective-permute-start(bf16[2,1,4,2,128,128]{5,4,3,2,1,0:T(8,128)(2,1)} %param.8), channel_id=1, source_target_pairs={{32,64},{96,128},{160,192},{224,256},{288,320},{352,384},{416,448}... | collective-permute-start | bytes 1572872 | tf_op jit(solution)/shard_map/ppermute | solution.py:92
  14.4 5.3 %collective-permute-start = (bf16[2,1,4,2,128,128]{5,4,3,2,0,1:T(8,128)(2,1)}, bf16[2,1,4,2,128,128]{5,4,3,2,0,1:T(8,128)(2,1)}, u32[]{:S(2)}, u32[]{:S(2)}) collective-permute-start(bf16[2,1,4,2,128,128]{5,4,3,2,0,1:T(8,128)(2,1)} %bitcast.204), channel_id=1, source_target_pairs={{0,32},{32,0},{64,96},{96,64},{128,160},{160,128},{192,224},{224,1... | collective-permute-start | bytes 1572872 | tf_op jit(solution)/shard_map/ppermute | solution.py:93
  41.7 27.3 %all-to-all-start = ((bf16[32,2,4,2,512]{4,3,1,2,0:T(2,128)(2,1)}), bf16[32,2,4,2,512]{4,3,1,2,0:T(2,128)(2,1)S(1)}, u32[]{:S(2)}, u32[]{:S(2)}) async-start(bf16[32,2,4,2,512]{4,3,1,2,0:T(2,128)(2,1)} %copy.89), calls=%async_computation | async-start | bytes 1048576 | tf_op jit(solution)/shard_map/all_to_all | solution.py:120
  70.3 22.4 %copy-start.1 = (bf16[1,128,128]{2,1,0:T(8,128)(2,1)S(1)}, bf16[1,128,128]{2,1,0:T(8,128)(2,1)}, u32[]{:S(2)}) copy-start(bf16[1,128,128]{2,1,0:T(8,128)(2,1)} %param.9) | copy-start | bytes 98308

commit v12 on v10

--- a/solution.py
+++ b/solution.py
@@ -152,6 +152,7 @@
         preferred_element_type=jnp.float32,
     )
     polar = (combined * factor).astype(jnp.bfloat16).reshape(groups, energy_local, 2, 2, -1)
+    polar = polar.reshape(groups, 4 * energy_local, -1)
     returned = lax.all_to_all(polar, "energy", 0, 0, tiled=True)
     returned = returned.reshape(groups, energy_local, 2, 2, block_count, -1, block_order)
     left_product = jnp.einsum(

time: 95 us -> 94.6 us (level)
  no operation moved by 1% of the time
where the time goes in v12:
time: 94.6 us; the launch traced here: 94.2 us
  waiting for transfers between devices  28.4 us (30%)
  starting transfers between devices  26.5 us (28%)
  blocking collectives  22.1 us (23%)
  matrix products  7.52 us (8%)
  other arithmetic  6.1 us (6%)
  local copies, waits for them, and re-layouts  3.2 us (3%)
    all_to_all x1, blocking collectives, body(): returned = lax.all_to_all(polar, 'energy', 0, 0, tiled=True)  22.1 us
    ppermute x1, waiting for transfers between devices, body(): neighbour = lax.ppermute(self_energy, 'space', across)  16.2 us
    ppermute x1, starting transfers between devices, body(): neighbour = lax.ppermute(self_energy, 'space', across)  14.4 us
    all_to_all x1, waiting for transfers between devices, body(): entries = lax.all_to_all(outgoing, 'energy', 0, 0, tiled=True)  12.2 us
    all_to_all x1, starting transfers between devices, body(): entries = lax.all_to_all(outgoing, 'energy', 0, 0, tiled=True)  10.2 us
    dot_general x3, matrix products, congruence(): jnp.einsum('fneiqr,fnegsr->fneiqgs', sigma, green, preferred_element_type...  3.38 us
    another operation x5, other arithmetic  2.53 us
    ppermute x1, starting transfers between devices, body(): partner = lax.ppermute(self_energy, 'space', on_chip)  1.92 us
  transfers between devices with their start and end apart: 3, of which 2 were waited for; matrix products, arithmetic and copies ran while one was open for 11% of the time, Pallas kernels for 0%

profile of v12, /device:TPU:14, one launch (start us, length us, event | category | flops | bytes accessed | tf_op | source)
XLA Modules:
  0.0 94.2 jit_solution(7572017122836189816)
XLA Ops:
  0.0 14.4 %collective-permute-start.1 = (bf16[2,1,4,2,128,128]{5,4,3,2,1,0:T(8,128)(2,1)}, bf16[2,1,4,2,128,128]{5,4,3,2,1,0:T(8,128)(2,1)S(1)}, u32[]{:S(2)}, u32[]{:S(2)}) collective-permute-start(bf16[2,1,4,2,128,128]{5,4,3,2,1,0:T(8,128)(2,1)} %param.8), channel_id=1, source_target_pairs={{32,64},{96,128},{160,192},{224,256},{288,320},{352,384},{416,448}... | collective-permute-start | bytes 1572872 | tf_op jit(solution)/shard_map/ppermute | solution.py:92
  14.4 1.9 %collective-permute-start = (bf16[2,1,4,2,128,128]{5,4,3,2,0,1:T(8,128)(2,1)}, bf16[2,1,4,2,128,128]{5,4,3,2,0,1:T(8,128)(2,1)}, u32[]{:S(2)}, u32[]{:S(2)}) collective-permute-start(bf16[2,1,4,2,128,128]{5,4,3,2,0,1:T(8,128)(2,1)} %bitcast.207), channel_id=1, source_target_pairs={{0,32},{32,0},{64,96},{96,64},{128,160},{160,128},{192,224},{224,1... | collective-permute-start | bytes 1572872 | tf_op jit(solution)/shard_map/ppermute | solution.py:93
  16.3 1.5 %convolution_bitcast_fusion.6 = f32[2,1,4,2,128,2,128]{6,4,5,3,2,0,1:T(8,128)S(1)} fusion(bf16[2,1,4,2,128,128]{5,4,3,2,1,0:T(8,128)(2,1)} %param.8, bf16[4,2,128,128]{3,2,1,0:T(8,128)(2,1)S(1)} %bitcast.203), kind=kOutput, calls=%fused_computation.6 | convolution fusion | flops 134217728 | bytes 2883584 | tf_op jit(solution)/shard_map/fneiqr,fnegsr->fneiqgs/dot_general | solution.py:50
  17.8 0.1 fusion.41
  17.9 0.1 fusion.42
  17.9 0.5 convolution_bitcast_fusion.5
  18.4 0.1 fusion.17
  18.5 0.2 copy-done.1
  18.7 0.1 copy.62
  18.8 0.1 fusion.19
  18.9 1.1 %select_bitcast_fusion = (bf16[4,2,128,128]{3,2,1,0:T(8,128)(2,1)S(1)}, bf16[4,2,128,128]{3,2,1,0:T(8,128)(2,1)S(1)}) fusion(bf16[1,4,2,128,128]{4,3,2,1,0:T(8,128)(2,1)} %param.5, bf16[1,4,2,128,128]{4,3,2,1,0:T(8,128)(2,1)} %param.7, pred[]{:T(512)S(6)} %eq.12), kind=kLoop, calls=%fused_computation.96 | loop fusion | flops 262144 | bytes 1048577 | tf_op jit(solution)/shard_map/broadcast_in_dim | solution.py:49
  20.0 1.5 %convolution_bitcast_fusion.4 = f32[2,1,4,2,128,2,128]{4,6,3,5,2,0,1:T(8,128)S(1)} fusion(bf16[2,1,4,2,128,128]{5,4,3,2,0,1:T(8,128)(2,1)} %collective-permute-done, bf16[4,2,128,128]{3,2,1,0:T(8,128)(2,1)S(1)} %get-tuple-element.18), kind=kOutput, calls=%fused_computation.4 | convolution fusion | flops 134217728 | bytes 2883584 | tf_op jit(solution)/shard_map/fneiqr,fnegsr->fneiqgs/dot_general | solution.py:50
  21.4 0.1 fusion.43
  21.5 0.1 fusion.44
  21.6 0.5 convolution_bitcast_fusion.3
  22.0 0.1 fusion.13
  22.1 0.1 maximum_add_fusion
  22.3 16.2 %collective-permute-done.1 = bf16[2,1,4,2,128,128]{5,4,3,2,1,0:T(8,128)(2,1)S(1)} collective-permute-done((bf16[2,1,4,2,128,128]{5,4,3,2,1,0:T(8,128)(2,1)}, bf16[2,1,4,2,128,128]{5,4,3,2,1,0:T(8,128)(2,1)S(1)}, u32[]{:S(2)}, u32[]{:S(2)}) %collective-permute-start.1) | collective-permute-done | bytes 524320 | tf_op jit(solution)/shard_map/ppermute | solution.py:92
  38.5 0.4 convolution_bitcast_fusion.2
  38.9 0.1 fusion.45
  39.0 0.1 fusion.46
  39.0 0.5 convolution_bitcast_fusion.1
  39.5 0.1 fusion.8
  39.7 0.2 fusion.4
  39.8 0.3 copy.67
  40.1 0.2 reshape.647
  40.3 1.3 %copy.68 = bf16[32,2,4,2,512]{4,3,2,1,0:T(2,128)(2,1)} copy(bf16[32,2,4,2,512]{4,0,3,2,1:T(8,128)(2,1)S(1)} %reshape.647) | data formatting | bytes 1048576 | tf_op jit(solution)/shard_map/reshape | solution.py:108
  41.7 10.2 %all-to-all-start = ((bf16[32,2,4,2,512]{4,3,2,1,0:T(2,128)(2,1)}), bf16[32,2,4,2,512]{4,3,2,1,0:T(2,128)(2,1)S(1)}, u32[]{:S(2)}, u32[]{:S(2)}) async-start(bf16[32,2,4,2,512]{4,3,2,1,0:T(2,128)(2,1)} %copy.68), calls=%async_computation | async-start | bytes 1048576 | tf_op jit(solution)/shard_map/all_to_all | solution.py:123
  51.9 0.6 fusion.85
  52.5 0.2 copy.51
  52.8 0.1 concatenate.71
  52.9 0.1 copy.48
  53.0 0.5 fusion.81
  53.5 0.5 negate_convert_fusion.2
  54.1 0.2 copy.49
  54.3 0.2 copy.50
  54.5 0.3 fusion.47
  54.8 1.2 %pad_maximum_fusion = bf16[128,4,512]{2,1,0:T(4,128)(2,1)S(1)} fusion(bf16[128,1,512]{2,1,0:T(2,128)(2,1)S(1)} %fusion.47, bf16[128,1,512]{2,1,0:T(2,128)(2,1)S(1)} %copy.51, bf16[128,1,512]{2,1,0:T(2,128)(2,1)S(1)} %copy.50, bf16[128,1,512]{2,1,0:T(2,128)(2,1)S(1)} %copy.49), kind=kLoop, calls=%fused_computation.51 | loop fusion | flops 2097152 | bytes 1048576 | tf_op jit(solution)/shard_map/stack | solution.py:146
  56.0 0.1 convert_element_type.111
  56.2 0.6 fusion.79
  56.8 12.2 %all-to-all-done = bf16[32,2,4,2,512]{4,3,2,1,0:T(2,128)(2,1)S(1)} async-done(((bf16[32,2,4,2,512]{4,3,2,1,0:T(2,128)(2,1)}), bf16[32,2,4,2,512]{4,3,2,1,0:T(2,128)(2,1)S(1)}, u32[]{:S(2)}, u32[]{:S(2)}) %all-to-all-start) | async-done | bytes 524320 | tf_op jit(solution)/shard_map/all_to_all | solution.py:123
  69.0 0.6 convolution_bitcast_fusion
  69.6 0.3 fusion.39
  69.9 0.4 fusion.1
  70.3 22.1 %all_to_all.10 = bf16[32,16,512]{2,1,0:T(8,128)(2,1)S(1)} all-to-all(bf16[32,16,512]{2,1,0:T(8,128)(2,1)S(1)} %bitcast.206), channel_id=1, replica_groups=mesh['space'=24,'energy'=32] {'energy'}, dimensions={0} | all-to-all | bytes 1048576 | tf_op jit(solution)/shard_map/all_to_all | solution.py:156
  92.4 0.1 reshape.648
  92.5 0.5 fusion.3
  93.0 1.1 %fusion.2 = bf16[2,1,4,2,128,128]{5,4,3,2,1,0:T(8,128)(2,1)} fusion(bf16[2,4,2,128,128]{3,4,2,0,1:T(8,128)(2,1)S(1)} %fusion.3, bf16[1,128,128]{2,1,0:T(8,128)(2,1)S(1)} %copy-done.1), kind=kOutput, calls=%fused_computation.12 | convolution fusion | flops 67371008 | bytes 1081344 | tf_op jit(solution)/shard_map/fetnpr,nsr->fnetps/dot_general | solution.py:161
  (8 shorter events, 0.1 us)
Async XLA Ops:
  0.0 16.3 %copy-start = (bf16[1,4,2,128,128]{4,3,2,1,0:T(8,128)(2,1)S(1)}, bf16[1,4,2,128,128]{4,3,2,1,0:T(8,128)(2,1)}, u32[]{:S(2)}) copy-start(bf16[1,4,2,128,128]{4,3,2,1,0:T(8,128)(2,1)} %param.6) | copy-start | bytes 786436
  0.0 38.5 %collective-permute-start.1 = (bf16[2,1,4,2,128,128]{5,4,3,2,1,0:T(8,128)(2,1)}, bf16[2,1,4,2,128,128]{5,4,3,2,1,0:T(8,128)(2,1)S(1)}, u32[]{:S(2)}, u32[]{:S(2)}) collective-permute-start(bf16[2,1,4,2,128,128]{5,4,3,2,1,0:T(8,128)(2,1)} %param.8), channel_id=1, source_target_pairs={{32,64},{96,128},{160,192},{224,256},{288,320},{352,384},{416,448}... | collective-permute-start | bytes 1572872 | tf_op jit(solution)/shard_map/ppermute | solution.py:92
  14.4 5.6 %collective-permute-start = (bf16[2,1,4,2,128,128]{5,4,3,2,0,1:T(8,128)(2,1)}, bf16[2,1,4,2,128,128]{5,4,3,2,0,1:T(8,128)(2,1)}, u32[]{:S(2)}, u32[]{:S(2)}) collective-permute-start(bf16[2,1,4,2,128,128]{5,4,3,2,0,1:T(8,128)(2,1)} %bitcast.207), channel_id=1, source_target_pairs={{0,32},{32,0},{64,96},{96,64},{128,160},{160,128},{192,224},{224,1... | collective-permute-start | bytes 1572872 | tf_op jit(solution)/shard_map/ppermute | solution.py:93
  17.9 0.8 copy-start.1
  41.7 27.3 %all-to-all-start = ((bf16[32,2,4,2,512]{4,3,2,1,0:T(2,128)(2,1)}), bf16[32,2,4,2,512]{4,3,2,1,0:T(2,128)(2,1)S(1)}, u32[]{:S(2)}, u32[]{:S(2)}) async-start(bf16[32,2,4,2,512]{4,3,2,1,0:T(2,128)(2,1)} %copy.68), calls=%async_computation | async-start | bytes 1048576 | tf_op jit(solution)/shard_map/all_to_all | solution.py:123
